TPU v7x, 256 devices: a whole 4x4x8 slice. The times are simulated.
256 devices in a mesh: ctx: 4 (over y), exp: 64 (over z, x, core).
Axes of the slice: x: 4, y: 4, z: 8, core: 2. Of those that a mesh axis runs over, the one named last changes fastest.
Arguments:
- residual_in: bfloat16 [64, 256, 1536], P('exp', 'ctx'), may hold values from -6 to 6
- queries: bfloat16 [64, 256, 1536], P('exp', 'ctx'), may hold values from -6 to 6
- new_kv: bfloat16 [64, 256, 1024], P('exp', 'ctx'), may hold values from -6 to 6
- cache_kv: bfloat16 [64, 4096, 1024], P('exp', 'ctx'), may hold values from -6 to 6
- cache_len: int32 [64], P('exp'), may hold values from 1 to 4096, 133120 in all
- out_proj: bfloat16 [1536, 1536], replicated, may hold values from -0.625 to 0.625
- norm_gain: float32 [1536], replicated, may hold values from 0.1 to 1.9
- routes: int32 [64, 256, 6], P('exp', 'ctx'), may hold values from 0 to 63, all different within a row; in each aligned block of 64 rows (0 to 63, 64 to 127, ..., all dimensions but the last counted through in order) at most 9 rows name the same one
- route_w: bfloat16 [64, 256, 6], P('exp', 'ctx'), may hold values from 0.049804688 to 0.5
- w_gate_up: bfloat16 [64, 1536, 1024], P('exp'), may hold values from -0.15625 to 0.15625
- w_down: bfloat16 [64, 512, 1536], P('exp'), may hold values from -0.25 to 0.25
Outputs:
- layer_out: bfloat16 [64, 256, 1536], P('exp', 'ctx')
Inputs may be any that keep to these rules, and one draw needn't show every extreme that they name: `cache_len`: the largest length is exactly 4096. `routes`: each token names 6 different experts; among the new tokens of one device (aligned blocks of 64 tokens) no expert is named by more than 9 tokens, a bound that some block reaches.
All inputs are finite; a program needn't handle non-finite values. No bound on the sum of `cache_len` on one device may be relied on, other than what follows from the above.
Results may differ from a plain program's by a relative error of at most 0.02.
Values may be sent and summed in bfloat16 or wider, within the bound.
No kernel may reach another device: no remote copies, remote signals or barrier semaphores. Data moves between devices by JAX's collectives and lax.ppermute only.
A program may use at most 128 MiB of HBM per device.

v0:
```python
import jax
import jax.numpy as jnp
from jax import lax
from jax.sharding import PartitionSpec as P

D = 1536
KVH = 4
HD = 128
GROUP = 3


NEG_BIG = -1e30


def score_block(query_grid, piece, score_scale):
    row_count = piece.shape[0]
    key_width = piece.shape[1] // 2
    key_part = piece[:, :key_width].reshape(row_count, KVH, HD)
    value_part = piece[:, key_width:].reshape(row_count, KVH, HD)
    scores = (
        jnp.einsum("qkgd,rkd->kgqr", query_grid, key_part, preferred_element_type=jnp.float32)
        * score_scale
    )
    return (scores, value_part)


def local(
    residual_in,
    queries,
    new_kv,
    cache_kv,
    cache_len,
    out_proj,
    norm_gain,
    routes,
    route_w,
    w_gate_up,
    w_down,
):
    tok_count = residual_in.shape[1]
    cache_rows = cache_kv.shape[1]
    ctx_pos = lax.axis_index("ctx")
    length = cache_len[0]
    score_scale = HD ** (-0.5)
    local_keys = jnp.concatenate([cache_kv[0], new_kv[0]], 0)
    query_grid = queries[0].reshape(tok_count, KVH, GROUP, HD)
    query_pos = ctx_pos * tok_count + jnp.arange(tok_count)
    block_rows = cache_rows + tok_count
    piece = lax.all_gather(local_keys, "ctx", axis=0, tiled=True)
    run_max = jnp.full((KVH, GROUP, tok_count), NEG_BIG, jnp.float32)
    scores, value_part = score_block(query_grid, piece, score_scale)
    row_index = jnp.arange(piece.shape[0])
    shard_index = row_index // block_rows
    offset = row_index % block_rows
    cached = offset < cache_rows
    cache_pos = shard_index * cache_rows + offset
    new_pos = shard_index * tok_count + offset - cache_rows
    usable = jnp.where(
        cached[None, :], (cache_pos < length)[None, :], new_pos[None, :] <= query_pos[:, None]
    )
    masked = jnp.where(usable, scores, NEG_BIG)
    new_max = jnp.maximum(run_max, jnp.max(masked, -1))
    softmax_terms = jnp.where(usable, jnp.exp(scores - new_max[..., None]), 0.0)
    run_sum = jnp.sum(softmax_terms, -1)
    run_acc = jnp.einsum(
        "kgqr,rkd->kgqd",
        softmax_terms.astype(jnp.bfloat16),
        value_part,
        preferred_element_type=jnp.float32,
    )
    attended = (
        (run_acc / run_sum[..., None]).transpose(2, 0, 1, 3).reshape(tok_count, KVH * GROUP * HD)
    )
    attended = attended.astype(jnp.bfloat16)
    mixed = (
        residual_in[0].astype(jnp.float32)
        + jnp.dot(attended, out_proj, preferred_element_type=jnp.float32)
    ).astype(jnp.bfloat16)
    widened = mixed.astype(jnp.float32)
    normed = (
        widened * lax.rsqrt(jnp.mean(widened * widened, -1, keepdims=True) + 1e-06) * norm_gain
    ).astype(jnp.bfloat16)
    top_count = routes.shape[2]
    local_experts = w_gate_up.shape[0]
    expert_total = local_experts * lax.axis_size("exp")
    capacity = min(tok_count, 3 * tok_count * top_count // (2 * expert_total))
    expert_ids = routes[0].reshape(-1)
    token_ids = jnp.arange(tok_count * top_count) // top_count
    one_hot = (expert_ids[:, None] == jnp.arange(expert_total)[None, :]).astype(jnp.int32)
    before = jnp.cumsum(one_hot, 0) - one_hot
    slot_index = jnp.sum(before * one_hot, 1)
    outgoing = (
        jnp.zeros((expert_total, capacity, D), jnp.bfloat16)
        .at[expert_ids, slot_index]
        .set(normed[token_ids])
    )
    hidden_half = w_gate_up.shape[2] // 2
    incoming = lax.all_to_all(outgoing, "exp", split_axis=0, concat_axis=0, tiled=True)
    item_count = incoming.shape[1]
    grouped = incoming.reshape(-1, local_experts, item_count, incoming.shape[2])
    gate_up = jnp.einsum("sekd,edf->sekf", grouped, w_gate_up, preferred_element_type=jnp.float32)
    activated = (jax.nn.silu(gate_up[..., :hidden_half]) * gate_up[..., hidden_half:]).astype(
        jnp.bfloat16
    )
    result = jnp.einsum(
        "sekf,efd->sekd", activated, w_down, preferred_element_type=jnp.float32
    ).astype(jnp.bfloat16)
    returned = lax.all_to_all(
        result.reshape(incoming.shape), "exp", split_axis=0, concat_axis=0, tiled=True
    )
    picked = returned[expert_ids, slot_index].reshape(tok_count, top_count, -1)
    blended = jnp.einsum("qk,qkd->qd", route_w[0], picked, preferred_element_type=jnp.float32)
    return (widened + blended).astype(jnp.bfloat16)[None]


def solution(mesh):
    return jax.shard_map(
        local,
        mesh=mesh,
        in_specs=(
            P("exp", "ctx", None),
            P("exp", "ctx", None),
            P("exp", "ctx", None),
            P("exp", "ctx", None),
            P("exp"),
            P(),
            P(),
            P("exp", "ctx", None),
            P("exp", "ctx", None),
            P("exp", None, None),
            P("exp", None, None),
        ),
        out_specs=P("exp", "ctx", None),
        check_vma=False,
    )
```

profile of v0, /device:TPU:1, one launch (start us, length us, event | category | flops | bytes accessed | tf_op | source)
XLA Modules:
  0.0 423.9 jit_solution(8894068005494485637)
XLA Ops:
  6.5 3.4 pad_maximum_fusion
  12.1 0.9 reduce-window.6
  13.8 90.1 %all-gather.2.cloned.1.call-done = bf16[4352,1024]{1,0:T(8,128)(2,1)} async-done(((bf16[1088,1024]{1,0:T(8,128)(2,1)}), bf16[4352,1024]{1,0:T(8,128)(2,1)}) %all-gather.2.cloned.1.call-update) | async-done | bytes 8912912 | tf_op jit(solution)/shard_map/all_gather | solution.py:49
  103.8 7.6 %fusion.52 = (bf16[4352,512]{1,0:T(8,128)(2,1)}, bf16[4352,512]{1,0:T(8,128)(2,1)}) fusion(bf16[4352,1024]{1,0:T(8,128)(2,1)} %all-gather.2.cloned.1.call-done), kind=kLoop, calls=%fused_computation.79 | loop fusion | bytes 17825792 | tf_op jit(solution)/shard_map/slice | solution.py:18
  111.4 6.5 %copy.46 = bf16[4352,512]{0,1:T(8,128)(2,1)} copy(bf16[4352,512]{1,0:T(8,128)(2,1)} %get-tuple-element.8) | data formatting | bytes 8912896
  117.9 6.5 %copy.45 = bf16[4352,512]{0,1:T(8,128)(2,1)} copy(bf16[4352,512]{1,0:T(8,128)(2,1)} %get-tuple-element.7) | data formatting | bytes 8912896
  124.4 9.6 %fusion = (f32[4,3,64]{2,1,0:T(4,128)S(1)}, f32[4,4352,64,3]{1,2,3,0:T(8,128)}) fusion(pred[64,4352]{1,0:T(8,128)(4,1)S(1)} %compare_select_fusion, bf16[4352,4,128,1]{0,2,3,1:T(8,128)(2,1)} %bitcast.99, bf16[64,4,3,128]{3,2,1,0:T(4,128)(2,1)} %reshape_squeeze.6), kind=kOutput, calls=%fused_computation.5 | convolution fusion | flops 865664256 | bytes 18304000 | tf_op jit(solution)/shard_map/qkgd,rkd->kgqr/dot_general | solution.py:21
  134.0 8.1 %fusion.3 = f32[4,3,64]{2,1,0:T(4,128)S(1)} fusion(f32[4,4352,64,3]{1,2,3,0:T(8,128)} %get-tuple-element.10, f32[4,3,64]{2,1,0:T(4,128)S(1)} %broadcast_maximum_fusion, pred[64,4352]{1,0:T(8,128)(4,1)S(1)} %compare_select_fusion), kind=kLoop, calls=%fused_computation.8 | loop fusion | flops 13368576 | bytes 13654016 | tf_op jit(solution)/shard_map/reduce_sum | solution.py:64
  142.1 8.4 %fusion.26 = bf16[64,4,3,128]{3,0,2,1:T(8,128)(2,1)S(1)} fusion(bf16[4352,4,128,1]{0,2,3,1:T(8,128)(2,1)} %bitcast.100, f32[4,4352,64,3]{1,2,3,0:T(8,128)} %get-tuple-element.10, f32[4,3,64]{2,1,0:T(4,128)S(1)} %broadcast_maximum_fusion, pred[64,4352]{1,0:T(8,128)(4,1)S(1)} %compare_select_fusion, f32[64,4,3]{0,2,1:T(4,128)S(1)} %bitcast.104), kind=kOutput, calls=%fused_computation.27 | convolution fusion | flops 869203968 | bytes 18307072 | tf_op jit(solution)/shard_map/kgqr,rkd->kgqd/dot_general | solution.py:65
  151.6 3.4 multiply_reduce_fusion
  155.9 2.8 gather_fusion
  158.7 1.4 broadcast_in_dim.57
  160.1 62.6 %scatter_fusion = bf16[64,9,1536]{2,0,1:T(8,128)(2,1)} fusion(bf16[64,9,1536]{2,0,1:T(8,128)(2,1)} %broadcast_in_dim.57, s32[384]{0:T(512)S(1)} %get-tuple-element.6, bf16[384,1536]{1,0:T(8,128)(2,1)} %gather_fusion), kind=kCustom, calls=%fused_computation.2 | custom fusion | bytes 3542016 | tf_op jit(solution)/shard_map/scatter | solution.py:95
  222.7 2.6 copy.33
  225.3 83.7 %all_to_all.10 = bf16[64,9,1536]{2,1,0:T(8,128)(2,1)S(1)} all-to-all(bf16[64,9,1536]{2,1,0:T(8,128)(2,1)S(1)} %copy.33), channel_id=1, replica_groups=mesh['ctx'=4,'exp'=64] {'exp'}, dimensions={0} | all-to-all | bytes 3538944 | tf_op jit(solution)/shard_map/all_to_all | solution.py:98
  309.0 2.5 fusion.13
  311.5 1.1 convolution_convert_fusion
  312.6 2.8 copy.35
  315.5 6.5 %all-to-all-start.1 = ((bf16[64,9,1536]{2,1,0:T(8,128)(2,1)}), bf16[64,9,1536]{2,1,0:T(8,128)(2,1)}, u32[]{:S(2)}, u32[]{:S(2)}) async-start(bf16[64,9,1536]{2,1,0:T(8,128)(2,1)} %copy.35), calls=%async_computation.1 | async-start | bytes 6291456 | tf_op jit(solution)/shard_map/all_to_all | solution.py:108
  322.7 71.6 %all-to-all-done.1 = bf16[64,9,1536]{2,1,0:T(8,128)(2,1)} async-done(((bf16[64,9,1536]{2,1,0:T(8,128)(2,1)}), bf16[64,9,1536]{2,1,0:T(8,128)(2,1)}, u32[]{:S(2)}, u32[]{:S(2)}) %all-to-all-start.1) | async-done | bytes 1769504 | tf_op jit(solution)/shard_map/all_to_all | solution.py:108
  394.3 4.2 copy.36
  398.5 12.7 %gather_fusion.1 = bf16[384,1536]{1,0:T(8,128)(2,1)} fusion(bf16[64,9,1536]{2,0,1:T(8,128)(2,1)} %copy.36, s32[384]{0:T(512)S(1)} %get-tuple-element.5), kind=kCustom, calls=%fused_computation.1 | custom fusion | bytes 2362368 | tf_op jit(solution)/shard_map/gather | solution.py:111
  411.2 3.1 reshape.183
  414.3 2.0 fusion.53
  (41 shorter events, 5.5 us)
Async XLA Ops:
  6.5 302.4 %copy-start = (bf16[1,1536,1024]{2,1,0:T(8,128)(2,1)S(1)}, bf16[1,1536,1024]{2,1,0:T(8,128)(2,1)}, u32[]{:S(2)}) copy-start(bf16[1,1536,1024]{2,1,0:T(8,128)(2,1)} %param.20) | copy-start | bytes 9437188
  6.5 97.3 %all-gather.2.cloned.1.call-start = ((), (), s32[]{:S(2)}) async-start(), calls=%async_computation.2 | async-start | bytes 11141120 | tf_op jit(solution)/shard_map/all_gather | solution.py:49
  6.5 3.5 copy-start.5
  6.5 4.6 %copy-start.3 = (bf16[1,64,1536]{2,1,0:T(8,128)(2,1)S(1)}, bf16[1,64,1536]{2,1,0:T(8,128)(2,1)}, u32[]{:S(2)}) copy-start(bf16[1,64,1536]{2,1,0:T(8,128)(2,1)} %param.12) | copy-start | bytes 589828
  150.5 5.3 %copy-start.4 = (f32[1536]{0:T(1024)S(1)}, f32[1536]{0:T(1024)}, u32[]{:S(2)}) copy-start(f32[1536]{0:T(1024)} %param.17) | copy-start | bytes 18436
  155.0 0.8 copy-start.1
  309.0 2.5 copy-start.7
  315.5 6.5 %copy-start.6 = (bf16[1,64,6]{1,2,0:T(8,128)(2,1)S(1)}, bf16[1,64,6]{1,2,0:T(8,128)(2,1)}, u32[]{:S(2)}) copy-start(bf16[1,64,6]{1,2,0:T(8,128)(2,1)} %param.19) | copy-start | bytes 2308
  315.5 78.9 %all-to-all-start.1 = ((bf16[64,9,1536]{2,1,0:T(8,128)(2,1)}), bf16[64,9,1536]{2,1,0:T(8,128)(2,1)}, u32[]{:S(2)}, u32[]{:S(2)}) async-start(bf16[64,9,1536]{2,1,0:T(8,128)(2,1)} %copy.35), calls=%async_computation.1 | async-start | bytes 6291456 | tf_op jit(solution)/shard_map/all_to_all | solution.py:108
  411.2 5.1 %copy-start.2 = (f32[64,1536]{1,0:T(8,128)S(1)}, f32[64,1536]{1,0:T(8,128)}, u32[]{:S(2)}) copy-start(f32[64,1536]{1,0:T(8,128)} %copy-done.1) | copy-start | bytes 1179652
Sparse Core Ops, SparseCore 0:
  10.1 93.6 all-gather.1
where the time goes:
time: 427 us; the launch traced here: 424 us
  waiting for transfers between devices  162 us (38%)
  local copies, waits for them, and re-layouts  117 us (27%)
  blocking collectives  83.7 us (20%)
  matrix products  27.1 us (6%)
  between operations  14.2 us (3%)
  other arithmetic  13.8 us (3%)
  starting transfers between devices  6.53 us (2%)
    all_gather x1, waiting for transfers between devices, local(): piece = lax.all_gather(local_keys, 'ctx', axis=0, tiled=True)  90.1 us
    all_to_all x1, blocking collectives, local(): lax.all_to_all(outgoing, 'exp', split_axis=0, concat_axis=0, tiled=True)  83.7 us
    all_to_all x1, waiting for transfers between devices, local(): lax.all_to_all(result.reshape(incoming.shape), 'exp', split_axis=0, conca...  71.6 us
    scatter x2, local copies, waits for them, and re-layouts, local(): outgoing = jnp.zeros((expert_total, capacity, D), jnp.bfloat16).at[expert...  65.2 us
    unnamed x19, local copies, waits for them, and re-layouts  13.8 us
    gather x1, local copies, waits for them, and re-layouts, local(): picked = returned[expert_ids, slot_index].reshape(tok_count, top_count, -1)  12.7 us
    dot_general x1, matrix products, score_block(): jnp.einsum('qkgd,rkd->kgqr', query_grid, key_part, preferred_element_type...  9.64 us
  transfers between devices with their start and end apart: 2, of which 2 were waited for; matrix products, arithmetic and copies ran while one was open for 1% of the time, Pallas kernels for 0%

commit v1 on v0

v1 whole, which is shorter than its diff:
```python
import jax
import jax.numpy as jnp
from jax import lax
from jax.sharding import PartitionSpec as P

D = 1536
KVH = 4
HD = 128
GROUP = 3


NEG_BIG = -1e30


def local(
    residual_in,
    queries,
    new_kv,
    cache_kv,
    cache_len,
    out_proj,
    norm_gain,
    routes,
    route_w,
    w_gate_up,
    w_down,
):
    tok_count = residual_in.shape[1]
    cache_rows = cache_kv.shape[1]
    n_ctx = lax.axis_size("ctx")
    ctx_pos = lax.axis_index("ctx")
    length = cache_len[0]
    score_scale = HD ** (-0.5)
    heads = KVH * GROUP

    all_queries = lax.all_gather(queries[0], "ctx", axis=0, tiled=True)
    query_total = all_queries.shape[0]
    query_grid = all_queries.reshape(query_total, KVH, GROUP, HD)
    local_keys = jnp.concatenate([cache_kv[0], new_kv[0]], 0)
    key_rows = local_keys.shape[0]
    key_width = local_keys.shape[1] // 2
    key_part = local_keys[:, :key_width].reshape(key_rows, KVH, HD)
    value_part = local_keys[:, key_width:].reshape(key_rows, KVH, HD)
    scores = (
        jnp.einsum("qkgd,rkd->kgqr", query_grid, key_part, preferred_element_type=jnp.float32)
        * score_scale
    )
    row_index = jnp.arange(key_rows)
    cached = row_index < cache_rows
    cache_pos = ctx_pos * cache_rows + row_index
    new_pos = ctx_pos * tok_count + row_index - cache_rows
    query_pos = jnp.arange(query_total)
    usable = jnp.where(
        cached[None, :], (cache_pos < length)[None, :], new_pos[None, :] <= query_pos[:, None]
    )
    part_max = jnp.max(jnp.where(usable, scores, NEG_BIG), -1)
    softmax_terms = jnp.where(usable, jnp.exp(scores - part_max[..., None]), 0.0)
    part_sum = jnp.sum(softmax_terms, -1)
    part_acc = jnp.einsum(
        "kgqr,rkd->qkgd",
        softmax_terms.astype(jnp.bfloat16),
        value_part,
        preferred_element_type=jnp.float32,
    )
    part_acc = part_acc.reshape(n_ctx, tok_count, heads, HD)
    stats = jnp.stack([part_max, part_sum], 0).reshape(2, heads, n_ctx, tok_count)
    stats = stats.transpose(2, 3, 1, 0).reshape(n_ctx, tok_count, heads * 2)
    got_acc = lax.all_to_all(part_acc, "ctx", split_axis=0, concat_axis=0, tiled=True)
    got_stats = lax.all_to_all(stats, "ctx", split_axis=0, concat_axis=0, tiled=True)
    got_stats = got_stats.reshape(n_ctx, tok_count, heads, 2)
    got_max = got_stats[..., 0]
    got_sum = got_stats[..., 1]
    top_max = jnp.max(got_max, 0)
    rescale = jnp.exp(got_max - top_max[None])
    total_sum = jnp.sum(rescale * got_sum, 0)
    total_acc = jnp.sum(rescale[..., None] * got_acc, 0)
    attended = (total_acc / total_sum[..., None]).reshape(tok_count, heads * HD)
    attended = attended.astype(jnp.bfloat16)
    mixed = (
        residual_in[0].astype(jnp.float32)
        + jnp.dot(attended, out_proj, preferred_element_type=jnp.float32)
    ).astype(jnp.bfloat16)
    widened = mixed.astype(jnp.float32)
    normed = (
        widened * lax.rsqrt(jnp.mean(widened * widened, -1, keepdims=True) + 1e-06) * norm_gain
    ).astype(jnp.bfloat16)
    top_count = routes.shape[2]
    local_experts = w_gate_up.shape[0]
    expert_total = local_experts * lax.axis_size("exp")
    capacity = min(tok_count, 3 * tok_count * top_count // (2 * expert_total))
    expert_ids = routes[0].reshape(-1)
    one_hot = (expert_ids[:, None] == jnp.arange(expert_total)[None, :]).astype(jnp.int32)
    before = jnp.cumsum(one_hot, 0) - one_hot
    slot_index = jnp.sum(before * one_hot, 1)
    dest = (expert_ids * capacity + slot_index).reshape(tok_count, top_count)
    slot_ids = jnp.arange(expert_total * capacity)
    hits = dest[None, :, :] == slot_ids[:, None, None]
    select = jnp.any(hits, -1).astype(jnp.bfloat16)
    outgoing = jnp.dot(select, normed, preferred_element_type=jnp.float32).astype(jnp.bfloat16)
    outgoing = outgoing.reshape(expert_total, capacity, D)
    hidden_half = w_gate_up.shape[2] // 2
    incoming = lax.all_to_all(outgoing, "exp", split_axis=0, concat_axis=0, tiled=True)
    item_count = incoming.shape[1]
    grouped = incoming.reshape(-1, local_experts, item_count, incoming.shape[2])
    gate_up = jnp.einsum("sekd,edf->sekf", grouped, w_gate_up, preferred_element_type=jnp.float32)
    activated = (jax.nn.silu(gate_up[..., :hidden_half]) * gate_up[..., hidden_half:]).astype(
        jnp.bfloat16
    )
    result = jnp.einsum(
        "sekf,efd->sekd", activated, w_down, preferred_element_type=jnp.float32
    ).astype(jnp.bfloat16)
    returned = lax.all_to_all(
        result.reshape(incoming.shape), "exp", split_axis=0, concat_axis=0, tiled=True
    )
    weights = route_w[0]
    combine = jnp.sum(
        jnp.where(hits.transpose(1, 0, 2), weights[:, None, :], jnp.zeros((), weights.dtype)), -1
    )
    blended = jnp.dot(
        combine, returned.reshape(-1, D), preferred_element_type=jnp.float32
    )
    return (widened + blended).astype(jnp.bfloat16)[None]


def solution(mesh):
    return jax.shard_map(
        local,
        mesh=mesh,
        in_specs=(
            P("exp", "ctx", None),
            P("exp", "ctx", None),
            P("exp", "ctx", None),
            P("exp", "ctx", None),
            P("exp"),
            P(),
            P(),
            P("exp", "ctx", None),
            P("exp", "ctx", None),
            P("exp", None, None),
            P("exp", None, None),
        ),
        out_specs=P("exp", "ctx", None),
        check_vma=False,
    )
```

time: 427 us -> 277 us (0.65)
  local copies, waits for them, and re-layouts: 117 us -> 26.4 us
  waiting for transfers between devices: 162 us -> 83.8 us
  blocking collectives: 83.7 us -> 104 us
  between operations: 14.2 us -> 1.02 us
  starting transfers between devices: 6.53 us -> 14.3 us
    all_gather x1 -> x0, waiting for transfers between devices: 90.1 us -> none  [local(): piece = lax.all_gather(local_keys, 'ctx', axis=0, tiled=True)]
    scatter x2 -> x0, local copies, waits for them, and re-layouts: 65.2 us -> none  [local(): outgoing = jnp.zeros((expert_total, capacity, D), jnp.bfloat16).at[expert...]
    gather x2 -> x0, local copies, waits for them, and re-layouts: 15.5 us -> none  [the longest x1 12.7 us: local(): picked = returned[expert_ids, slot_index].reshape(tok_count, top_count, -1)]
    all_gather x0 -> x1, blocking collectives: none -> 13.6 us  [local(): all_queries = lax.all_gather(queries[0], 'ctx', axis=0, tiled=True)]
    unnamed x19 -> x18, local copies, waits for them, and re-layouts: 13.8 us -> 0.92 us
    all_to_all x0 -> x2, waiting for transfers between devices: none -> 12.2 us  [the longest x1 12.2 us: local(): lax.all_to_all(part_acc, 'ctx', split_axis=0, concat_axis=0, tiled=True)]
    reshape x1 -> x3, local copies, waits for them, and re-layouts: 3.1 us -> 11.2 us  [the longest x1 4.24 us: local(): returned.reshape(-1, D)]
    all_to_all x0 -> x2, starting transfers between devices: none -> 7.79 us  [the longest x1 4.53 us: local(): lax.all_to_all(part_acc, 'ctx', split_axis=0, concat_axis=0, tiled=True)]
  transfers between devices with their start and end apart: 2 -> 3, of which waited for: 2 -> 2; matrix products, arithmetic and copies ran while one was open for 1% -> 8% of each run, Pallas kernels for 0% -> 0%
where the time goes in v1:
time: 277 us; the launch traced here: 276 us
  blocking collectives  104 us (38%)
  waiting for transfers between devices  83.8 us (30%)
  matrix products  29.3 us (11%)
  local copies, waits for them, and re-layouts  26.4 us (10%)
  other arithmetic  17 us (6%)
  starting transfers between devices  14.3 us (5%)
    all_to_all x1, blocking collectives, local(): lax.all_to_all(outgoing, 'exp', split_axis=0, concat_axis=0, tiled=True)  90.3 us
    all_to_all x1, waiting for transfers between devices, local(): lax.all_to_all(result.reshape(incoming.shape), 'exp', split_axis=0, conca...  71.6 us
    all_gather x1, blocking collectives, local(): all_queries = lax.all_gather(queries[0], 'ctx', axis=0, tiled=True)  13.6 us
    all_to_all x1, waiting for transfers between devices, local(): lax.all_to_all(part_acc, 'ctx', split_axis=0, concat_axis=0, tiled=True)  12.2 us
    dot_general x1, matrix products, local(): jnp.einsum('kgqr,rkd->qkgd', softmax_terms.astype(jnp.bfloat16), value_pa...  9.14 us
    dot_general x1, matrix products, local(): jnp.einsum('qkgd,rkd->kgqr', query_grid, key_part, preferred_element_type...  8.52 us
    reduce_sum x1, other arithmetic, local(): part_sum = jnp.sum(softmax_terms, -1)  7.48 us
    all_to_all x1, starting transfers between devices, local(): lax.all_to_all(result.reshape(incoming.shape), 'exp', split_axis=0, conca...  6.52 us
  transfers between devices with their start and end apart: 3, of which 2 were waited for; matrix products, arithmetic and copies ran while one was open for 8% of the time, Pallas kernels for 0%

profile of v1, /device:TPU:1, one launch (start us, length us, event | category | flops | bytes accessed | tf_op | source)
XLA Modules:
  0.0 275.6 jit_solution(6451135125738383920)
XLA Ops:
  0.8 3.2 %fusion.25 = (bf16[1088,512]{1,0:T(8,128)(2,1)}, bf16[1088,512]{1,0:T(8,128)(2,1)}) fusion(bf16[1024,1024]{1,0:T(8,128)(2,1)} %bitcast.119, bf16[64,1024]{1,0:T(8,128)(2,1)} %bitcast.123), kind=kLoop, calls=%fused_computation.28 | loop fusion | flops 4456448 | bytes 4456448 | tf_op jit(solution)/shard_map/concatenate | solution.py:39
  4.0 2.4 copy.119
  6.4 13.6 %all-gather = bf16[1,256,1536]{2,1,0:T(8,128)(2,1)} all-gather(bf16[1,64,1536]{2,1,0:T(8,128)(2,1)S(1)} %copy-done.1), channel_id=2, replica_groups=mesh['ctx'=4,'exp'=64] {'ctx'}, dimensions={1}, use_global_device_ids=true | all-gather | bytes 983040 | tf_op jit(solution)/shard_map/all_gather | solution.py:36
  20.0 2.3 copy.120
  23.2 8.5 %fusion = (f32[4,3,256]{2,1,0:T(4,128)S(1)}, f32[4,1088,256,3]{2,1,3,0:T(8,128)}) fusion(pred[256,1088]{0,1:T(8,128)(4,1)S(1)} %fusion.26, bf16[1088,4,128,1]{0,2,3,1:T(8,128)(2,1)} %bitcast.117, bf16[256,4,3,128]{0,3,2,1:T(8,128)(2,1)} %bitcast.118), kind=kOutput, calls=%fused_computation.2 | convolution fusion | flops 865661952 | bytes 15560704 | tf_op jit(solution)/shard_map/qkgd,rkd->kgqr/dot_general | solution.py:45
  31.8 7.5 %fusion.4 = f32[4,3,256]{2,1,0:T(4,128)S(1)} fusion(f32[4,1088,256,3]{2,1,3,0:T(8,128)} %get-tuple-element.11, f32[4,3,256]{2,1,0:T(4,128)S(1)} %get-tuple-element.10, pred[256,1088]{0,1:T(8,128)(4,1)S(1)} %fusion.26), kind=kLoop, calls=%fused_computation.6 | loop fusion | flops 13366272 | bytes 13672448 | tf_op jit(solution)/shard_map/reduce_sum | solution.py:58
  40.2 3.3 %all-to-all-start = ((f32[4,1,1536]{2,1,0:T(1,128)}), f32[4,1,1536]{2,1,0:T(1,128)S(1)}, u32[]{:S(2)}, u32[]{:S(2)}) async-start(f32[4,1,1536]{2,1,0:T(1,128)} %reshape.117), calls=%async_computation | async-start | bytes 49152 | tf_op jit(solution)/shard_map/all_to_all | solution.py:69
  43.4 2.4 copy.126
  45.8 9.1 %fusion.21 = f32[256,4,3,128]{0,3,2,1:T(8,128)} fusion(bf16[1088,4,128,1]{0,2,3,1:T(8,128)(2,1)} %bitcast.120, f32[4,1088,256,3]{2,1,3,0:T(8,128)} %get-tuple-element.11, f32[4,3,256]{2,1,0:T(4,128)S(1)} %get-tuple-element.10, pred[256,1088]{0,1:T(8,128)(4,1)S(1)} %fusion.26), kind=kOutput, calls=%fused_computation.25 | convolution fusion | flops 869007360 | bytes 16347136 | tf_op jit(solution)/shard_map/kgqr,rkd->qkgd/dot_general | solution.py:59
  54.9 3.0 %copy.128 = f32[256,4,3,128]{3,0,2,1:T(8,128)} copy(f32[256,4,3,128]{0,3,2,1:T(8,128)} %fusion.21) | data formatting | bytes 3145728 | tf_op jit(solution)/shard_map/kgqr,rkd->qkgd/transpose | solution.py:59
  58.0 2.8 copy.129
  61.0 4.5 %all-to-all-start.1 = ((f32[4,64,12,128]{3,1,2,0:T(8,128)}), f32[4,64,12,128]{3,1,2,0:T(8,128)}, u32[]{:S(2)}, u32[]{:S(2)}) async-start(f32[4,64,12,128]{3,1,2,0:T(8,128)} %copy.129), calls=%async_computation.1 | async-start | bytes 3145728 | tf_op jit(solution)/shard_map/all_to_all | solution.py:68
  69.4 12.2 %all-to-all-done.1 = f32[4,64,12,128]{3,1,2,0:T(8,128)} async-done(((f32[4,64,12,128]{3,1,2,0:T(8,128)}), f32[4,64,12,128]{3,1,2,0:T(8,128)}, u32[]{:S(2)}, u32[]{:S(2)}) %all-to-all-start.1) | async-done | bytes 1572896 | tf_op jit(solution)/shard_map/all_to_all | solution.py:68
  81.5 1.9 multiply_reduce_fusion
  83.5 3.5 %multiply_reduce_fusion.1 = (f32[64]{0:T(128)S(1)}, f32[64,1536]{1,0:T(8,128)S(1)}) fusion(bf16[1536,1536]{1,0:T(8,128)(2,1)} %param.16, bf16[1,64,1536]{2,1,0:T(8,128)(2,1)} %param.11, f32[64,12,128]{2,0,1:T(8,128)S(1)} %multiply_reduce_fusion, f32[64,12]{0,1:T(8,128)S(1)} %fusion.41), kind=kOutput, calls=%fused_computation.39 | convolution fusion | flops 302776256 | bytes 5704960 | tf_op jit(solution)/shard_map/dot_general | solution.py:81
  87.0 1.9 convolution_convert_fusion
  88.9 4.2 %reshape.104 = bf16[64,9,1536]{2,1,0:T(8,128)(2,1)} reshape(bf16[576,1536]{1,0:T(8,128)(2,1)} %convolution_convert_fusion) | data formatting | bytes 3538944 | tf_op jit(solution)/shard_map/reshape | solution.py:100
  93.1 90.3 %all_to_all.20 = bf16[64,9,1536]{2,1,0:T(8,128)(2,1)S(1)} all-to-all(bf16[64,9,1536]{2,1,0:T(8,128)(2,1)} %reshape.104), channel_id=1, replica_groups=mesh['ctx'=4,'exp'=64] {'exp'}, dimensions={0} | all-to-all | bytes 3538944 | tf_op jit(solution)/shard_map/all_to_all | solution.py:102
  183.4 2.5 fusion.15
  187.0 2.8 %copy.138 = bf16[64,9,1536]{2,1,0:T(8,128)(2,1)} copy(bf16[64,9,1536]{2,0,1:T(8,128)(2,1)S(1)} %convolution_convert_fusion.1) | data formatting | bytes 3538944 | tf_op jit(solution)/shard_map/convert_element_type | solution.py:111
  189.8 6.5 %all-to-all-start.3 = ((bf16[64,9,1536]{2,1,0:T(8,128)(2,1)}), bf16[64,9,1536]{2,1,0:T(8,128)(2,1)}, u32[]{:S(2)}, u32[]{:S(2)}) async-start(bf16[64,9,1536]{2,1,0:T(8,128)(2,1)} %copy.138), calls=%async_computation.3 | async-start | bytes 6291456 | tf_op jit(solution)/shard_map/all_to_all | solution.py:112
  197.2 71.6 %all-to-all-done.3 = bf16[64,9,1536]{2,1,0:T(8,128)(2,1)} async-done(((bf16[64,9,1536]{2,1,0:T(8,128)(2,1)}), bf16[64,9,1536]{2,1,0:T(8,128)(2,1)}, u32[]{:S(2)}, u32[]{:S(2)}) %all-to-all-start.3) | async-done | bytes 1769504 | tf_op jit(solution)/shard_map/all_to_all | solution.py:112
  268.7 4.2 %reshape.108 = bf16[576,1536]{1,0:T(8,128)(2,1)} reshape(bf16[64,9,1536]{2,1,0:T(8,128)(2,1)} %all-to-all-done.3) | data formatting | bytes 3538944 | tf_op jit(solution)/shard_map/reshape | solution.py:120
  273.0 2.7 fusion.13
  (46 shorter events, 7.8 us)
Async XLA Ops:
  0.0 183.4 %copy-start = (bf16[1,1536,1024]{2,1,0:T(8,128)(2,1)S(1)}, bf16[1,1536,1024]{2,1,0:T(8,128)(2,1)}, u32[]{:S(2)}) copy-start(bf16[1,1536,1024]{2,1,0:T(8,128)(2,1)} %param.20) | copy-start | bytes 9437188
  4.0 2.4 copy-start.1
  40.2 20.8 %all-to-all-start = ((f32[4,1,1536]{2,1,0:T(1,128)}), f32[4,1,1536]{2,1,0:T(1,128)S(1)}, u32[]{:S(2)}, u32[]{:S(2)}) async-start(f32[4,1,1536]{2,1,0:T(1,128)} %reshape.117), calls=%async_computation | async-start | bytes 49152 | tf_op jit(solution)/shard_map/all_to_all | solution.py:69
  58.0 2.8 copy-start.3
  61.0 20.6 %all-to-all-start.1 = ((f32[4,64,12,128]{3,1,2,0:T(8,128)}), f32[4,64,12,128]{3,1,2,0:T(8,128)}, u32[]{:S(2)}, u32[]{:S(2)}) async-start(f32[4,64,12,128]{3,1,2,0:T(8,128)} %copy.129), calls=%async_computation.1 | async-start | bytes 3145728 | tf_op jit(solution)/shard_map/all_to_all | solution.py:68
  83.5 3.5 %copy-start.2 = (pred[576,64]{0,1:T(8,128)(4,1)S(1)}, pred[576,64]{0,1:T(8,128)(4,1)}, u32[]{:S(2)}) copy-start(pred[576,64]{0,1:T(8,128)(4,1)} %fusion.28) | copy-start | bytes 110596
  83.5 3.5 %copy-start.4 = (f32[1536]{0:T(1024)S(1)}, f32[1536]{0:T(1024)}, u32[]{:S(2)}) copy-start(f32[1536]{0:T(1024)} %param.17) | copy-start | bytes 18436
  183.4 2.5 copy-start.6
  189.8 6.5 %copy-start.5 = (bf16[1,64,6]{1,2,0:T(8,128)(2,1)S(1)}, bf16[1,64,6]{1,2,0:T(8,128)(2,1)}, u32[]{:S(2)}) copy-start(bf16[1,64,6]{1,2,0:T(8,128)(2,1)} %param.19) | copy-start | bytes 2308
  189.8 78.9 %all-to-all-start.3 = ((bf16[64,9,1536]{2,1,0:T(8,128)(2,1)}), bf16[64,9,1536]{2,1,0:T(8,128)(2,1)}, u32[]{:S(2)}, u32[]{:S(2)}) async-start(bf16[64,9,1536]{2,1,0:T(8,128)(2,1)} %copy.138), calls=%async_computation.3 | async-start | bytes 6291456 | tf_op jit(solution)/shard_map/all_to_all | solution.py:112

commit v2 on v1

--- a/solution.py
+++ b/solution.py
@@ -1,7 +1,7 @@
 import jax
 import jax.numpy as jnp
 from jax import lax
-from jax.sharding import PartitionSpec as P
+from jax.sharding import Mesh, PartitionSpec as P
 
 D = 1536
 KVH = 4
@@ -10,6 +10,24 @@
 
 
 NEG_BIG = -1e30
+
+
+EXP_AXES = ("z", "x", "core")
+CHIP_AXES = ("z", "x")
+
+
+def dispatch(rows):
+    split = rows.reshape(-1, 2, *rows.shape[1:])
+    split = lax.all_to_all(split, "core", split_axis=1, concat_axis=1, tiled=True)
+    split = lax.all_to_all(split, CHIP_AXES, split_axis=0, concat_axis=0, tiled=True)
+    return split.reshape(rows.shape)
+
+
+def undispatch(rows):
+    split = rows.reshape(-1, 2, *rows.shape[1:])
+    split = lax.all_to_all(split, CHIP_AXES, split_axis=0, concat_axis=0, tiled=True)
+    split = lax.all_to_all(split, "core", split_axis=1, concat_axis=1, tiled=True)
+    return split.reshape(rows.shape)
 
 
 def local(
@@ -86,7 +104,7 @@
     ).astype(jnp.bfloat16)
     top_count = routes.shape[2]
     local_experts = w_gate_up.shape[0]
-    expert_total = local_experts * lax.axis_size("exp")
+    expert_total = local_experts * lax.axis_size(EXP_AXES)
     capacity = min(tok_count, 3 * tok_count * top_count // (2 * expert_total))
     expert_ids = routes[0].reshape(-1)
     one_hot = (expert_ids[:, None] == jnp.arange(expert_total)[None, :]).astype(jnp.int32)
@@ -99,7 +117,7 @@
     outgoing = jnp.dot(select, normed, preferred_element_type=jnp.float32).astype(jnp.bfloat16)
     outgoing = outgoing.reshape(expert_total, capacity, D)
     hidden_half = w_gate_up.shape[2] // 2
-    incoming = lax.all_to_all(outgoing, "exp", split_axis=0, concat_axis=0, tiled=True)
+    incoming = dispatch(outgoing)
     item_count = incoming.shape[1]
     grouped = incoming.reshape(-1, local_experts, item_count, incoming.shape[2])
     gate_up = jnp.einsum("sekd,edf->sekf", grouped, w_gate_up, preferred_element_type=jnp.float32)
@@ -109,9 +127,7 @@
     result = jnp.einsum(
         "sekf,efd->sekd", activated, w_down, preferred_element_type=jnp.float32
     ).astype(jnp.bfloat16)
-    returned = lax.all_to_all(
-        result.reshape(incoming.shape), "exp", split_axis=0, concat_axis=0, tiled=True
-    )
+    returned = undispatch(result.reshape(incoming.shape))
     weights = route_w[0]
     combine = jnp.sum(
         jnp.where(hits.transpose(1, 0, 2), weights[:, None, :], jnp.zeros((), weights.dtype)), -1
@@ -123,22 +139,29 @@
 
 
 def solution(mesh):
+    exp_size = mesh.shape["exp"]
+    x_size, core_size = 4, 2
+    devices = mesh.devices.reshape(
+        mesh.shape["ctx"], exp_size // (x_size * core_size), x_size, core_size
+    )
+    fine = Mesh(devices, ("ctx",) + EXP_AXES)
+    rows = P(EXP_AXES, "ctx", None)
     return jax.shard_map(
         local,
-        mesh=mesh,
+        mesh=fine,
         in_specs=(
-            P("exp", "ctx", None),
-            P("exp", "ctx", None),
-            P("exp", "ctx", None),
-            P("exp", "ctx", None),
-            P("exp"),
+            rows,
+            rows,
+            rows,
+            rows,
+            P(EXP_AXES),
             P(),
             P(),
-            P("exp", "ctx", None),
-            P("exp", "ctx", None),
-            P("exp", None, None),
-            P("exp", None, None),
+            rows,
+            rows,
+            P(EXP_AXES, None, None),
+            P(EXP_AXES, None, None),
         ),
-        out_specs=P("exp", "ctx", None),
+        out_specs=rows,
         check_vma=False,
     )

time: 277 us -> 251 us (0.906)
  waiting for transfers between devices: 83.8 us -> 51.3 us
  local copies, waits for them, and re-layouts: 26.4 us -> 48.9 us
  blocking collectives: 104 us -> 86.7 us
    all_to_all x1, waiting for transfers between devices: 71.6 us -> 39.1 us  [undispatch(): lax.all_to_all(split, CHIP_AXES, split_axis=0, concat_axis=0, tiled=True)]
    another operation x0 -> x6, local copies, waits for them, and re-layouts: none -> 24.8 us  [the longest x2 8.58 us: undispatch(): split = rows.reshape(-1, 2, *rows.shape[1:])]
    all_to_all x1 -> x3, blocking collectives: 90.3 us -> 73.1 us  [the longest x1 53.7 us: dispatch(): lax.all_to_all(split, CHIP_AXES, split_axis=0, concat_axis=0, tiled=True)]
    all_to_all x0 -> x4, local copies, waits for them, and re-layouts: none -> 8.9 us  [the longest x1 2.78 us: undispatch(): lax.all_to_all(split, 'core', split_axis=1, concat_axis=1, tiled=True)]
    reshape x2 -> x0, local copies, waits for them, and re-layouts: 8.43 us -> none  [the longest x1 4.24 us: local(): returned.reshape(-1, D)]
    convert_element_type x1 -> x0, local copies, waits for them, and re-layouts: 2.82 us -> none  [local(): result = jnp.einsum('sekf,efd->sekd', activated, w_down, preferred_elemen...]
  transfers between devices with their start and end apart: 3 -> 3, of which waited for: 2 -> 2; matrix products, arithmetic and copies ran while one was open for 8% -> 9% of each run, Pallas kernels for 0% -> 0%
where the time goes in v2:
time: 251 us; the launch traced here: 250 us
  blocking collectives  86.7 us (35%)
  waiting for transfers between devices  51.3 us (20%)
  local copies, waits for them, and re-layouts  48.9 us (19%)
  matrix products  31.6 us (13%)
  other arithmetic  17 us (7%)
  starting transfers between devices  13.3 us (5%)
    all_to_all x1, blocking collectives, dispatch(): lax.all_to_all(split, CHIP_AXES, split_axis=0, concat_axis=0, tiled=True)  53.7 us
    all_to_all x1, waiting for transfers between devices, undispatch(): lax.all_to_all(split, CHIP_AXES, split_axis=0, concat_axis=0, tiled=True)  39.1 us
    all_gather x1, blocking collectives, local(): all_queries = lax.all_gather(queries[0], 'ctx', axis=0, tiled=True)  13.6 us
    all_to_all x1, waiting for transfers between devices, local(): lax.all_to_all(part_acc, 'ctx', split_axis=0, concat_axis=0, tiled=True)  12.2 us
    all_to_all x1, blocking collectives, dispatch(): lax.all_to_all(split, 'core', split_axis=1, concat_axis=1, tiled=True)  10.4 us
    dot_general x1, matrix products, local(): jnp.einsum('kgqr,rkd->qkgd', softmax_terms.astype(jnp.bfloat16), value_pa...  9.14 us
    all_to_all x1, blocking collectives, undispatch(): lax.all_to_all(split, 'core', split_axis=1, concat_axis=1, tiled=True)  9.02 us
    another operation x2, local copies, waits for them, and re-layouts, undispatch(): split = rows.reshape(-1, 2, *rows.shape[1:])  8.58 us
  transfers between devices with their start and end apart: 3, of which 2 were waited for; matrix products, arithmetic and copies ran while one was open for 9% of the time, Pallas kernels for 0%

profile of v2, /device:TPU:1, one launch (start us, length us, event | category | flops | bytes accessed | tf_op | source)
XLA Modules:
  0.0 249.9 jit_solution(8289831702695127616)
XLA Ops:
  0.8 3.2 %fusion.23 = (bf16[1088,512]{1,0:T(8,128)(2,1)}, bf16[1088,512]{1,0:T(8,128)(2,1)}) fusion(bf16[1024,1024]{1,0:T(8,128)(2,1)} %bitcast.132, bf16[64,1024]{1,0:T(8,128)(2,1)} %bitcast.136), kind=kLoop, calls=%fused_computation.28 | loop fusion | flops 4456448 | bytes 4456448 | tf_op jit(solution)/shard_map/concatenate | solution.py:57
  6.4 13.6 %all-gather = bf16[1,256,1536]{2,1,0:T(8,128)(2,1)} all-gather(bf16[1,64,1536]{2,1,0:T(8,128)(2,1)S(1)} %copy-done.1), channel_id=2, replica_groups=mesh['ctx'=4,'z'=8,'x'=4,'core'=2] {'ctx'}, dimensions={1}, use_global_device_ids=true | all-gather | bytes 983040 | tf_op jit(solution)/shard_map/all_gather | solution.py:54
  23.2 8.5 %fusion = (f32[4,3,256]{2,1,0:T(4,128)S(1)}, f32[4,1088,256,3]{2,1,3,0:T(8,128)}) fusion(pred[256,1088]{0,1:T(8,128)(4,1)S(1)} %fusion.24, bf16[1088,4,128,1]{0,2,3,1:T(8,128)(2,1)} %bitcast.130, bf16[256,4,3,128]{0,3,2,1:T(8,128)(2,1)} %bitcast.131), kind=kOutput, calls=%fused_computation.2 | convolution fusion | flops 865661952 | bytes 15560704 | tf_op jit(solution)/shard_map/qkgd,rkd->kgqr/dot_general | solution.py:63
  31.8 7.5 %fusion.4 = f32[4,3,256]{2,1,0:T(4,128)S(1)} fusion(f32[4,1088,256,3]{2,1,3,0:T(8,128)} %get-tuple-element.11, f32[4,3,256]{2,1,0:T(4,128)S(1)} %get-tuple-element.10, pred[256,1088]{0,1:T(8,128)(4,1)S(1)} %fusion.24), kind=kLoop, calls=%fused_computation.6 | loop fusion | flops 13366272 | bytes 13672448 | tf_op jit(solution)/shard_map/reduce_sum | solution.py:76
  40.2 3.3 %all-to-all-start = ((f32[4,1,1536]{2,1,0:T(1,128)}), f32[4,1,1536]{2,1,0:T(1,128)S(1)}, u32[]{:S(2)}, u32[]{:S(2)}) async-start(f32[4,1,1536]{2,1,0:T(1,128)} %reshape.110), calls=%async_computation | async-start | bytes 49152 | tf_op jit(solution)/shard_map/all_to_all | solution.py:87
  45.8 9.1 %fusion.19 = f32[256,4,3,128]{0,3,2,1:T(8,128)} fusion(bf16[1088,4,128,1]{0,2,3,1:T(8,128)(2,1)} %bitcast.133, f32[4,1088,256,3]{2,1,3,0:T(8,128)} %get-tuple-element.11, f32[4,3,256]{2,1,0:T(4,128)S(1)} %get-tuple-element.10, pred[256,1088]{0,1:T(8,128)(4,1)S(1)} %fusion.24), kind=kOutput, calls=%fused_computation.25 | convolution fusion | flops 869007360 | bytes 16347136 | tf_op jit(solution)/shard_map/kgqr,rkd->qkgd/dot_general | solution.py:77
  54.9 3.0 %copy.136 = f32[256,4,3,128]{3,0,2,1:T(8,128)} copy(f32[256,4,3,128]{0,3,2,1:T(8,128)} %fusion.19) | data formatting | bytes 3145728 | tf_op jit(solution)/shard_map/kgqr,rkd->qkgd/transpose | solution.py:77
  58.0 2.8 %copy.137 = f32[4,64,12,128]{3,1,2,0:T(8,128)} copy(f32[4,64,12,128]{3,1,0,2:T(8,128)} %bitcast.129) | data formatting | bytes 3145728 | tf_op jit(solution)/shard_map/reshape | solution.py:83
  61.0 4.5 %all-to-all-start.1 = ((f32[4,64,12,128]{3,1,2,0:T(8,128)}), f32[4,64,12,128]{3,1,2,0:T(8,128)}, u32[]{:S(2)}, u32[]{:S(2)}) async-start(f32[4,64,12,128]{3,1,2,0:T(8,128)} %copy.137), calls=%async_computation.1 | async-start | bytes 3145728 | tf_op jit(solution)/shard_map/all_to_all | solution.py:86
  69.4 12.2 %all-to-all-done.1 = f32[4,64,12,128]{3,1,2,0:T(8,128)} async-done(((f32[4,64,12,128]{3,1,2,0:T(8,128)}), f32[4,64,12,128]{3,1,2,0:T(8,128)}, u32[]{:S(2)}, u32[]{:S(2)}) %all-to-all-start.1) | async-done | bytes 1572896 | tf_op jit(solution)/shard_map/all_to_all | solution.py:86
  83.5 3.5 %multiply_reduce_fusion.1 = (f32[64]{0:T(128)S(1)}, f32[64,1536]{1,0:T(8,128)S(1)}) fusion(bf16[1536,1536]{1,0:T(8,128)(2,1)} %param.16, bf16[1,64,1536]{2,1,0:T(8,128)(2,1)} %param.11, f32[64,12,128]{2,0,1:T(8,128)S(1)} %multiply_reduce_fusion, f32[64,12]{0,1:T(8,128)S(1)} %fusion.39), kind=kOutput, calls=%fused_computation.39 | convolution fusion | flops 302776256 | bytes 5704960 | tf_op jit(solution)/shard_map/dot_general | solution.py:99
  88.9 4.2 %reshape_reshape.10 = bf16[32,2,9,1536]{3,2,1,0:T(8,128)(2,1)} reshape(bf16[576,1536]{1,0:T(8,128)(2,1)} %convolution_convert_fusion) | data formatting | bytes 3538944 | tf_op jit(solution)/shard_map/reshape;reshape | solution.py:20
  93.1 3.0 %copy.145 = bf16[32,2,9,1536]{3,0,2,1:T(8,128)(2,1)S(1)} copy(bf16[32,2,9,1536]{3,2,1,0:T(8,128)(2,1)} %reshape_reshape.10) | data formatting | bytes 3538944 | tf_op jit(solution)/shard_map/reshape;reshape | solution.py:20
  96.0 10.4 %all_to_all.30 = bf16[32,2,9,1536]{3,0,2,1:T(8,128)(2,1)S(1)} all-to-all(bf16[32,2,9,1536]{3,0,2,1:T(8,128)(2,1)S(1)} %copy.145), channel_id=1, replica_groups=mesh['ctx'=4,'z'=8,'x'=4,'core'=2] {'core'}, dimensions={1} | all-to-all | bytes 3538944 | tf_op jit(solution)/shard_map/all_to_all | solution.py:21
  108.3 53.7 %all_to_all.31 = bf16[32,2,9,1536]{3,1,2,0:T(2,128)(2,1)S(1)} all-to-all(bf16[32,2,9,1536]{3,1,2,0:T(2,128)(2,1)S(1)} %copy.146), channel_id=1, replica_groups=mesh['ctx'=4,'z'=8,'x'=4,'core'=2] {'z','x'}, dimensions={0} | all-to-all | bytes 3538944 | tf_op jit(solution)/shard_map/all_to_all | solution.py:22
  164.5 4.8 %reshape.98 = bf16[64,9,1536]{2,0,1:T(8,128)(2,1)} reshape(bf16[32,2,9,1536]{3,1,0,2:T(2,128)(2,1)} %copy.147) | data formatting | bytes 3538944 | tf_op jit(solution)/shard_map/reshape.4
  169.4 3.6 %fusion.15 = f32[64,1,9,1024]{3,0,2,1:T(8,128)S(1)} fusion(bf16[64,9,1536]{2,0,1:T(8,128)(2,1)} %reshape.98, bf16[1,1536,1024]{2,1,0:T(8,128)(2,1)S(1)} %copy-done), kind=kOutput, calls=%fused_computation.22 | convolution fusion | flops 1811939328 | bytes 7274496 | tf_op jit(solution)/shard_map/sekd,edf->sekf/dot_general | solution.py:123
  175.3 4.7 %reshape_reshape.11 = bf16[32,2,9,1536]{3,1,0,2:T(2,128)(2,1)} reshape(bf16[64,1,9,1536]{3,0,2,1:T(8,128)(2,1)} %fusion.10) | data formatting | bytes 3538944 | tf_op jit(solution)/shard_map/reshape;reshape | solution.py:27
  180.0 3.9 %copy.148 = bf16[32,2,9,1536]{3,1,2,0:T(2,128)(2,1)} copy(bf16[32,2,9,1536]{3,1,0,2:T(2,128)(2,1)} %reshape_reshape.11) | data formatting | bytes 3538944 | tf_op jit(solution)/shard_map/reshape;reshape | solution.py:27
  183.9 5.6 %all-to-all-start.4 = ((bf16[32,2,9,1536]{3,1,2,0:T(2,128)(2,1)}), bf16[32,2,9,1536]{3,1,2,0:T(2,128)(2,1)}, u32[]{:S(2)}, u32[]{:S(2)}) async-start(bf16[32,2,9,1536]{3,1,2,0:T(2,128)(2,1)} %copy.148), calls=%async_computation.4 | async-start | bytes 3538944 | tf_op jit(solution)/shard_map/all_to_all | solution.py:28
  190.3 39.1 %all-to-all-done.4 = bf16[32,2,9,1536]{3,1,2,0:T(2,128)(2,1)} async-done(((bf16[32,2,9,1536]{3,1,2,0:T(2,128)(2,1)}), bf16[32,2,9,1536]{3,1,2,0:T(2,128)(2,1)}, u32[]{:S(2)}, u32[]{:S(2)}) %all-to-all-start.4) | async-done | bytes 1769504 | tf_op jit(solution)/shard_map/all_to_all | solution.py:28
  231.2 9.0 %all_to_all.32 = bf16[32,2,9,1536]{3,0,2,1:T(8,128)(2,1)S(1)} all-to-all(bf16[32,2,9,1536]{3,0,2,1:T(8,128)(2,1)S(1)} %copy.149), channel_id=1, replica_groups=mesh['ctx'=4,'z'=8,'x'=4,'core'=2] {'core'}, dimensions={1} | all-to-all | bytes 3538944 | tf_op jit(solution)/shard_map/all_to_all | solution.py:29
  240.2 2.8 %copy.150 = bf16[32,2,9,1536]{3,2,1,0:T(8,128)(2,1)} copy(bf16[32,2,9,1536]{3,0,2,1:T(8,128)(2,1)S(1)} %all_to_all.32) | data formatting | bytes 3538944 | tf_op jit(solution)/shard_map/all_to_all | solution.py:29
  243.0 4.2 %reshape_reshape.12 = bf16[576,1536]{1,0:T(8,128)(2,1)} reshape(bf16[32,2,9,1536]{3,2,1,0:T(8,128)(2,1)} %copy.150) | data formatting | bytes 3538944 | tf_op jit(solution)/shard_map/reshape;reshape | solution.py:136
  (55 shorter events, 28.7 us)
Async XLA Ops:
  0.0 169.4 %copy-start = (bf16[1,1536,1024]{2,1,0:T(8,128)(2,1)S(1)}, bf16[1,1536,1024]{2,1,0:T(8,128)(2,1)}, u32[]{:S(2)}) copy-start(bf16[1,1536,1024]{2,1,0:T(8,128)(2,1)} %param.20) | copy-start | bytes 9437188
  4.0 2.4 copy-start.1
  40.2 20.8 %all-to-all-start = ((f32[4,1,1536]{2,1,0:T(1,128)}), f32[4,1,1536]{2,1,0:T(1,128)S(1)}, u32[]{:S(2)}, u32[]{:S(2)}) async-start(f32[4,1,1536]{2,1,0:T(1,128)} %reshape.110), calls=%async_computation | async-start | bytes 49152 | tf_op jit(solution)/shard_map/all_to_all | solution.py:87
  58.0 2.8 %copy-start.3 = (s32[1,64,6]{1,0,2:T(1,128)S(1)}, s32[1,64,6]{1,0,2:T(1,128)}, u32[]{:S(2)}) copy-start(s32[1,64,6]{1,0,2:T(1,128)} %param.18) | copy-start | bytes 4612
  61.0 20.6 %all-to-all-start.1 = ((f32[4,64,12,128]{3,1,2,0:T(8,128)}), f32[4,64,12,128]{3,1,2,0:T(8,128)}, u32[]{:S(2)}, u32[]{:S(2)}) async-start(f32[4,64,12,128]{3,1,2,0:T(8,128)} %copy.137), calls=%async_computation.1 | async-start | bytes 3145728 | tf_op jit(solution)/shard_map/all_to_all | solution.py:86
  83.5 3.5 %copy-start.2 = (pred[576,64]{0,1:T(8,128)(4,1)S(1)}, pred[576,64]{0,1:T(8,128)(4,1)}, u32[]{:S(2)}) copy-start(pred[576,64]{0,1:T(8,128)(4,1)} %fusion.26) | copy-start | bytes 110596
  83.5 3.5 %copy-start.4 = (f32[1536]{0:T(1024)S(1)}, f32[1536]{0:T(1024)}, u32[]{:S(2)}) copy-start(f32[1536]{0:T(1024)} %param.17) | copy-start | bytes 18436
  169.4 3.6 %copy-start.6 = (bf16[1,512,1536]{2,1,0:T(8,128)(2,1)S(1)}, bf16[1,512,1536]{2,1,0:T(8,128)(2,1)}, u32[]{:S(2)}) copy-start(bf16[1,512,1536]{2,1,0:T(8,128)(2,1)} %param.21) | copy-start | bytes 4718596
  183.9 5.6 %copy-start.5 = (bf16[1,64,6]{1,2,0:T(8,128)(2,1)S(1)}, bf16[1,64,6]{1,2,0:T(8,128)(2,1)}, u32[]{:S(2)}) copy-start(bf16[1,64,6]{1,2,0:T(8,128)(2,1)} %param.19) | copy-start | bytes 2308
  183.9 45.5 %all-to-all-start.4 = ((bf16[32,2,9,1536]{3,1,2,0:T(2,128)(2,1)}), bf16[32,2,9,1536]{3,1,2,0:T(2,128)(2,1)}, u32[]{:S(2)}, u32[]{:S(2)}) async-start(bf16[32,2,9,1536]{3,1,2,0:T(2,128)(2,1)} %copy.148), calls=%async_computation.4 | async-start | bytes 3538944 | tf_op jit(solution)/shard_map/all_to_all | solution.py:28

commit v3 on v2

--- a/solution.py
+++ b/solution.py
@@ -1,6 +1,8 @@
 import jax
 import jax.numpy as jnp
 from jax import lax
+from jax.experimental import pallas as pl
+from jax.experimental.pallas import tpu as pltpu
 from jax.sharding import Mesh, PartitionSpec as P
 
 D = 1536
@@ -10,6 +12,65 @@
 
 
 NEG_BIG = -1e30
+
+
+def attend_kernel(scal_ref, q_ref, kc_ref, vc_ref, kn_ref, vn_ref, acc_ref, st_ref):
+    ctx_pos = scal_ref[0]
+    length = scal_ref[1]
+    scale = HD ** (-0.5)
+    q = q_ref[...]
+    dims = (((1,), (1,)), ((), ()))
+    s_c = lax.dot_general(q, kc_ref[...], dims, preferred_element_type=jnp.float32) * scale
+    s_n = lax.dot_general(q, kn_ref[...], dims, preferred_element_type=jnp.float32) * scale
+    n_q, n_cache = s_c.shape
+    n_new = s_n.shape[1]
+    use_c = ctx_pos * n_cache + lax.broadcasted_iota(jnp.int32, (n_q, n_cache), 1) < length
+    use_n = ctx_pos * n_new + lax.broadcasted_iota(jnp.int32, (n_q, n_new), 1) <= (
+        lax.broadcasted_iota(jnp.int32, (n_q, n_new), 0)
+    )
+    top = jnp.maximum(
+        jnp.max(jnp.where(use_c, s_c, NEG_BIG), 1, keepdims=True),
+        jnp.max(jnp.where(use_n, s_n, NEG_BIG), 1, keepdims=True),
+    )
+    p_c = jnp.where(use_c, jnp.exp(s_c - top), 0.0)
+    p_n = jnp.where(use_n, jnp.exp(s_n - top), 0.0)
+    total = jnp.sum(p_c, 1, keepdims=True) + jnp.sum(p_n, 1, keepdims=True)
+    acc_ref[...] = jnp.dot(
+        p_c.astype(jnp.bfloat16), vc_ref[...], preferred_element_type=jnp.float32
+    ) + jnp.dot(p_n.astype(jnp.bfloat16), vn_ref[...], preferred_element_type=jnp.float32)
+    lane = lax.broadcasted_iota(jnp.int32, acc_ref.shape, 1)
+    st_ref[...] = jnp.where(lane < 64, top, total)
+
+
+def partial_attention(scal, all_queries, cache_rows, new_rows):
+    n_q = all_queries.shape[0]
+    n_cache = cache_rows.shape[0]
+    n_new = new_rows.shape[0]
+    heads = KVH * GROUP
+    q_spec = pl.BlockSpec((n_q, HD), lambda k, g, s: (0, k * GROUP + g))
+    out_shape = jax.ShapeDtypeStruct((n_q, heads * HD), jnp.float32)
+    cost = pl.CostEstimate(
+        flops=4 * n_q * (n_cache + n_new) * HD * heads,
+        transcendentals=n_q * (n_cache + n_new) * heads,
+        bytes_accessed=2 * (all_queries.size + cache_rows.size + new_rows.size) + 8 * n_q * heads * HD,
+    )
+    return pl.pallas_call(
+        attend_kernel,
+        out_shape=(out_shape, out_shape),
+        grid_spec=pltpu.PrefetchScalarGridSpec(
+            num_scalar_prefetch=1,
+            grid=(KVH, GROUP),
+            in_specs=[
+                q_spec,
+                pl.BlockSpec((n_cache, HD), lambda k, g, s: (0, k)),
+                pl.BlockSpec((n_cache, HD), lambda k, g, s: (0, KVH + k)),
+                pl.BlockSpec((n_new, HD), lambda k, g, s: (0, k)),
+                pl.BlockSpec((n_new, HD), lambda k, g, s: (0, KVH + k)),
+            ],
+            out_specs=[q_spec, q_spec],
+        ),
+        cost_estimate=cost,
+    )(scal, all_queries, cache_rows, cache_rows, new_rows, new_rows)
 
 
 EXP_AXES = ("z", "x", "core")
@@ -52,46 +113,22 @@
     heads = KVH * GROUP
 
     all_queries = lax.all_gather(queries[0], "ctx", axis=0, tiled=True)
-    query_total = all_queries.shape[0]
-    query_grid = all_queries.reshape(query_total, KVH, GROUP, HD)
-    local_keys = jnp.concatenate([cache_kv[0], new_kv[0]], 0)
-    key_rows = local_keys.shape[0]
-    key_width = local_keys.shape[1] // 2
-    key_part = local_keys[:, :key_width].reshape(key_rows, KVH, HD)
-    value_part = local_keys[:, key_width:].reshape(key_rows, KVH, HD)
-    scores = (
-        jnp.einsum("qkgd,rkd->kgqr", query_grid, key_part, preferred_element_type=jnp.float32)
-        * score_scale
-    )
-    row_index = jnp.arange(key_rows)
-    cached = row_index < cache_rows
-    cache_pos = ctx_pos * cache_rows + row_index
-    new_pos = ctx_pos * tok_count + row_index - cache_rows
-    query_pos = jnp.arange(query_total)
-    usable = jnp.where(
-        cached[None, :], (cache_pos < length)[None, :], new_pos[None, :] <= query_pos[:, None]
-    )
-    part_max = jnp.max(jnp.where(usable, scores, NEG_BIG), -1)
-    softmax_terms = jnp.where(usable, jnp.exp(scores - part_max[..., None]), 0.0)
-    part_sum = jnp.sum(softmax_terms, -1)
-    part_acc = jnp.einsum(
-        "kgqr,rkd->qkgd",
-        softmax_terms.astype(jnp.bfloat16),
-        value_part,
-        preferred_element_type=jnp.float32,
-    )
-    part_acc = part_acc.reshape(n_ctx, tok_count, heads, HD)
-    stats = jnp.stack([part_max, part_sum], 0).reshape(2, heads, n_ctx, tok_count)
-    stats = stats.transpose(2, 3, 1, 0).reshape(n_ctx, tok_count, heads * 2)
-    got_acc = lax.all_to_all(part_acc, "ctx", split_axis=0, concat_axis=0, tiled=True)
-    got_stats = lax.all_to_all(stats, "ctx", split_axis=0, concat_axis=0, tiled=True)
-    got_stats = got_stats.reshape(n_ctx, tok_count, heads, 2)
-    got_max = got_stats[..., 0]
-    got_sum = got_stats[..., 1]
+    scal = jnp.stack([ctx_pos, length]).astype(jnp.int32)
+    part_acc, part_stats = partial_attention(scal, all_queries, cache_kv[0], new_kv[0])
+    part_stats = part_stats.reshape(n_ctx * tok_count, heads, HD)
+    stats = jnp.concatenate([part_stats[:, :, 0], part_stats[:, :, 64]], -1)
+    got_acc = lax.all_to_all(
+        part_acc.reshape(n_ctx, tok_count, heads * HD), "ctx", split_axis=0, concat_axis=0, tiled=True
+    )
+    got_stats = lax.all_to_all(
+        stats.reshape(n_ctx, tok_count, 2 * heads), "ctx", split_axis=0, concat_axis=0, tiled=True
+    )
+    got_max = got_stats[..., :heads]
+    got_sum = got_stats[..., heads:]
     top_max = jnp.max(got_max, 0)
     rescale = jnp.exp(got_max - top_max[None])
     total_sum = jnp.sum(rescale * got_sum, 0)
-    total_acc = jnp.sum(rescale[..., None] * got_acc, 0)
+    total_acc = jnp.sum(rescale[..., None] * got_acc.reshape(n_ctx, tok_count, heads, HD), 0)
     attended = (total_acc / total_sum[..., None]).reshape(tok_count, heads * HD)
     attended = attended.astype(jnp.bfloat16)
     mixed = (

time: 251 us -> 231 us (0.920)
  matrix products: 31.6 us -> 13.9 us
  Pallas kernels: 0 us -> 14.2 us
  other arithmetic: 17 us -> 6.37 us
  blocking collectives: 86.7 us -> 94.9 us
  waiting for transfers between devices: 51.3 us -> 45.6 us
  local copies, waits for them, and re-layouts: 48.9 us -> 44.6 us
  starting transfers between devices: 13.3 us -> 9.89 us
    dot_general x2 -> x0, matrix products: 17.7 us -> none  [the longest x1 9.14 us: local(): jnp.einsum('kgqr,rkd->qkgd', softmax_terms.astype(jnp.bfloat16), value_pa...]
    pallas_call x0 -> x1, Pallas kernels: none -> 14.2 us  [partial_attention(): pl.pallas_call(attend_kernel, out_shape=(out_shape, out_shape), grid_spec...]
    reduce_sum x2 -> x1, other arithmetic: 9.39 us -> 2.21 us  [local(): jnp.sum(rescale[..., None] * got_acc.reshape(n_ctx, tok_count, heads, HD)...]
    all_to_all x0 -> x1, blocking collectives: none -> 6.61 us  [local(): lax.all_to_all(stats.reshape(n_ctx, tok_count, 2 * heads), 'ctx', split_a...]
    all_to_all x2 -> x1, waiting for transfers between devices: 12.2 us -> 6.49 us  [local(): lax.all_to_all(part_acc.reshape(n_ctx, tok_count, heads * HD), 'ctx', spl...]
    mul x1 -> x2, local copies, waits for them, and re-layouts: 0.01 us -> 4.61 us  [local(): rescale[..., None] * got_acc.reshape(n_ctx, tok_count, heads, HD)]
    slice x3 -> x2, local copies, waits for them, and re-layouts: 5.03 us -> 1.22 us  [the longest x1 1 us: local(): stats = jnp.concatenate([part_stats[:, :, 0], part_stats[:, :, 64]], -1)]
    all_to_all x2 -> x1, starting transfers between devices: 7.79 us -> 4.34 us  [local(): lax.all_to_all(part_acc.reshape(n_ctx, tok_count, heads * HD), 'ctx', spl...]
  transfers between devices with their start and end apart: 3 -> 2, of which waited for: 2 -> 2; matrix products, arithmetic and copies ran while one was open for 9% -> 4% of each run, Pallas kernels for 0% -> 0%
where the time goes in v3:
time: 231 us; the launch traced here: 230 us
  blocking collectives  94.9 us (41%)
  waiting for transfers between devices  45.6 us (20%)
  local copies, waits for them, and re-layouts  44.6 us (19%)
  Pallas kernels  14.2 us (6%)
  matrix products  13.9 us (6%)
  starting transfers between devices  9.89 us (4%)
  other arithmetic  6.37 us (3%)
    all_to_all x1, blocking collectives, dispatch(): lax.all_to_all(split, CHIP_AXES, split_axis=0, concat_axis=0, tiled=True)  53.8 us
    all_to_all x1, waiting for transfers between devices, undispatch(): lax.all_to_all(split, CHIP_AXES, split_axis=0, concat_axis=0, tiled=True)  39.1 us
    all_gather x1, blocking collectives, local(): all_queries = lax.all_gather(queries[0], 'ctx', axis=0, tiled=True)  14.5 us
    pallas_call x1, Pallas kernels, partial_attention(): pl.pallas_call(attend_kernel, out_shape=(out_shape, out_shape), grid_spec...  14.2 us
    all_to_all x1, blocking collectives, dispatch(): lax.all_to_all(split, 'core', split_axis=1, concat_axis=1, tiled=True)  10.9 us
    all_to_all x1, blocking collectives, undispatch(): lax.all_to_all(split, 'core', split_axis=1, concat_axis=1, tiled=True)  9.02 us
    another operation x2, local copies, waits for them, and re-layouts, undispatch(): split = rows.reshape(-1, 2, *rows.shape[1:])  8.58 us
    another operation x2, local copies, waits for them, and re-layouts, dispatch(): split = rows.reshape(-1, 2, *rows.shape[1:])  7.15 us
  transfers between devices with their start and end apart: 2, of which 2 were waited for; matrix products, arithmetic and copies ran while one was open for 4% of the time, Pallas kernels for 0%

profile of v3, /device:TPU:1, one launch (start us, length us, event | category | flops | bytes accessed | tf_op | source)
XLA Modules:
  0.0 230.3 jit_solution(9156858286527818788)
XLA Ops:
  0.0 14.5 %all-gather = bf16[1,256,1536]{2,1,0:T(8,128)(2,1)} all-gather(bf16[1,64,1536]{2,1,0:T(8,128)(2,1)} %param.12), channel_id=2, replica_groups=mesh['ctx'=4,'z'=8,'x'=4,'core'=2] {'ctx'}, dimensions={1}, use_global_device_ids=true | all-gather | bytes 983040 | tf_op jit(solution)/shard_map/all_gather | solution.py:115
  15.8 14.2 %shard_map.109 = (f32[256,1536]{1,0:T(8,128)}, f32[256,1536]{1,0:T(8,128)}) custom-call(s32[2]{0:T(128)} %pad_add_fusion.scal_ref, bf16[256,1536]{1,0:T(8,128)(2,1)} %bitcast.90, bf16[1024,1024]{1,0:T(8,128)(2,1)} %bitcast.98, bf16[1024,1024]{1,0:T(8,128)(2,1)} %bitcast.99, bf16[64,1024]{1,0:T(8,128)(2,1)} %bitcast.100, bf16[64,1024]{1,0:T(8,128)(2,1)} %bitcast.101), custom_call_target="tpu_custom_call" | custom-call | flops 1711276032 | bytes 6160384 | tf_op jit(solution)/shard_map/pallas_call | solution.py:57
  30.0 3.1 %copy.61 = f32[256,1536]{0,1:T(8,128)} copy(f32[256,1536]{1,0:T(8,128)} %get-tuple-element.7) | data formatting | bytes 3145728 | tf_op jit(solution)/shard_map/pallas_call | solution.py:57
  34.3 6.6 %all_to_all.30 = f32[4,1,1536]{2,1,0:T(1,128)S(1)} all-to-all(f32[4,1,1536]{2,1,0:T(1,128)S(1)} %reshape.81), channel_id=1, replica_groups=mesh['ctx'=4,'z'=8,'x'=4,'core'=2] {'ctx'}, dimensions={0} | all-to-all | bytes 49152 | tf_op jit(solution)/shard_map/all_to_all | solution.py:123
  40.9 4.3 %all-to-all-start.1 = ((f32[4,64,1536]{2,1,0:T(8,128)}), f32[4,64,1536]{2,1,0:T(8,128)}, u32[]{:S(2)}, u32[]{:S(2)}) async-start(f32[4,64,1536]{2,1,0:T(8,128)} %bitcast.89), calls=%async_computation.1 | async-start | bytes 3145728 | tf_op jit(solution)/shard_map/all_to_all | solution.py:120
  51.6 2.6 %mul.51 = f32[4,64,1536]{2,1,0:T(8,128)} reshape(f32[4,64,12,128]{3,2,1,0:T(8,128)} %mul.50) | data formatting | bytes 3145728 | tf_op jit(solution)/shard_map/mul | solution.py:131
  54.3 6.5 %all-to-all-done.1 = f32[4,64,1536]{2,1,0:T(8,128)} async-done(((f32[4,64,1536]{2,1,0:T(8,128)}), f32[4,64,1536]{2,1,0:T(8,128)}, u32[]{:S(2)}, u32[]{:S(2)}) %all-to-all-start.1) | async-done | bytes 1572896 | tf_op jit(solution)/shard_map/all_to_all | solution.py:120
  63.3 3.4 %multiply_reduce_fusion.1 = (f32[64]{0:T(128)S(1)}, f32[64,1536]{1,0:T(8,128)S(1)}) fusion(bf16[1536,1536]{1,0:T(8,128)(2,1)} %param.16, f32[64,1536]{1,0:T(8,128)S(1)} %multiply_reduce_fusion, f32[8,8,12,128]{3,2,1,0:T(8,128)S(1)} %bitcast.88, bf16[1,64,1536]{2,1,0:T(8,128)(2,1)S(1)} %copy-done.1), kind=kOutput, calls=%fused_computation.25 | convolution fusion | flops 302776256 | bytes 6095104 | tf_op jit(solution)/shard_map/dot_general | solution.py:136
  68.7 4.2 %reshape_reshape.10 = bf16[32,2,9,1536]{3,2,1,0:T(8,128)(2,1)} reshape(bf16[576,1536]{1,0:T(8,128)(2,1)} %convolution_convert_fusion) | data formatting | bytes 3538944 | tf_op jit(solution)/shard_map/reshape;reshape | solution.py:81
  72.8 3.0 %copy.70 = bf16[32,2,9,1536]{3,0,2,1:T(8,128)(2,1)S(1)} copy(bf16[32,2,9,1536]{3,2,1,0:T(8,128)(2,1)} %reshape_reshape.10) | data formatting | bytes 3538944 | tf_op jit(solution)/shard_map/reshape;reshape | solution.py:81
  75.8 10.9 %all_to_all.31 = bf16[32,2,9,1536]{3,0,2,1:T(8,128)(2,1)S(1)} all-to-all(bf16[32,2,9,1536]{3,0,2,1:T(8,128)(2,1)S(1)} %copy.70), channel_id=1, replica_groups=mesh['ctx'=4,'z'=8,'x'=4,'core'=2] {'core'}, dimensions={1} | all-to-all | bytes 3538944 | tf_op jit(solution)/shard_map/all_to_all | solution.py:82
  88.6 53.8 %all_to_all.32 = bf16[32,2,9,1536]{3,1,2,0:T(2,128)(2,1)S(1)} all-to-all(bf16[32,2,9,1536]{3,1,2,0:T(2,128)(2,1)S(1)} %copy.71), channel_id=1, replica_groups=mesh['ctx'=4,'z'=8,'x'=4,'core'=2] {'z','x'}, dimensions={0} | all-to-all | bytes 3538944 | tf_op jit(solution)/shard_map/all_to_all | solution.py:83
  142.4 2.6 %copy.72 = bf16[32,2,9,1536]{3,1,0,2:T(2,128)(2,1)} copy(bf16[32,2,9,1536]{3,1,2,0:T(2,128)(2,1)S(1)} %all_to_all.32) | data formatting | bytes 3538944 | tf_op jit(solution)/shard_map/all_to_all | solution.py:83
  145.0 4.8 %reshape.70 = bf16[64,9,1536]{2,0,1:T(8,128)(2,1)} reshape(bf16[32,2,9,1536]{3,1,0,2:T(2,128)(2,1)} %copy.72) | data formatting | bytes 3538944 | tf_op jit(solution)/shard_map/reshape.4
  149.8 3.6 %fusion.7 = f32[64,1,9,1024]{3,0,2,1:T(8,128)S(1)} fusion(bf16[64,9,1536]{2,0,1:T(8,128)(2,1)} %reshape.70, bf16[1,1536,1024]{2,1,0:T(8,128)(2,1)S(1)} %copy-done), kind=kOutput, calls=%fused_computation.11 | convolution fusion | flops 1811939328 | bytes 7274496 | tf_op jit(solution)/shard_map/sekd,edf->sekf/dot_general | solution.py:160
  153.4 2.3 %fusion.2 = bf16[64,1,9,1536]{3,0,2,1:T(8,128)(2,1)} fusion(bf16[1,512,1536]{2,1,0:T(8,128)(2,1)S(1)} %copy-done.6, f32[64,1,9,1024]{3,0,2,1:T(8,128)S(1)} %fusion.7), kind=kOutput, calls=%fused_computation.4 | convolution fusion | flops 908623872 | bytes 5701632 | tf_op jit(solution)/shard_map/sekf,efd->sekd/dot_general | solution.py:164
  155.7 4.7 %reshape_reshape.11 = bf16[32,2,9,1536]{3,1,0,2:T(2,128)(2,1)} reshape(bf16[64,1,9,1536]{3,0,2,1:T(8,128)(2,1)} %fusion.2) | data formatting | bytes 3538944 | tf_op jit(solution)/shard_map/reshape;reshape | solution.py:88
  160.4 3.9 %copy.73 = bf16[32,2,9,1536]{3,1,2,0:T(2,128)(2,1)} copy(bf16[32,2,9,1536]{3,1,0,2:T(2,128)(2,1)} %reshape_reshape.11) | data formatting | bytes 3538944 | tf_op jit(solution)/shard_map/reshape;reshape | solution.py:88
  164.3 5.6 %all-to-all-start.4 = ((bf16[32,2,9,1536]{3,1,2,0:T(2,128)(2,1)}), bf16[32,2,9,1536]{3,1,2,0:T(2,128)(2,1)}, u32[]{:S(2)}, u32[]{:S(2)}) async-start(bf16[32,2,9,1536]{3,1,2,0:T(2,128)(2,1)} %copy.73), calls=%async_computation.4 | async-start | bytes 3538944 | tf_op jit(solution)/shard_map/all_to_all | solution.py:89
  170.7 39.1 %all-to-all-done.4 = bf16[32,2,9,1536]{3,1,2,0:T(2,128)(2,1)} async-done(((bf16[32,2,9,1536]{3,1,2,0:T(2,128)(2,1)}), bf16[32,2,9,1536]{3,1,2,0:T(2,128)(2,1)}, u32[]{:S(2)}, u32[]{:S(2)}) %all-to-all-start.4) | async-done | bytes 1769504 | tf_op jit(solution)/shard_map/all_to_all | solution.py:89
  211.6 9.0 %all_to_all.33 = bf16[32,2,9,1536]{3,0,2,1:T(8,128)(2,1)S(1)} all-to-all(bf16[32,2,9,1536]{3,0,2,1:T(8,128)(2,1)S(1)} %copy.74), channel_id=1, replica_groups=mesh['ctx'=4,'z'=8,'x'=4,'core'=2] {'core'}, dimensions={1} | all-to-all | bytes 3538944 | tf_op jit(solution)/shard_map/all_to_all | solution.py:90
  220.6 2.8 %copy.75 = bf16[32,2,9,1536]{3,2,1,0:T(8,128)(2,1)} copy(bf16[32,2,9,1536]{3,0,2,1:T(8,128)(2,1)S(1)} %all_to_all.33) | data formatting | bytes 3538944 | tf_op jit(solution)/shard_map/all_to_all | solution.py:90
  223.4 4.2 %reshape_reshape.12 = bf16[576,1536]{1,0:T(8,128)(2,1)} reshape(bf16[32,2,9,1536]{3,2,1,0:T(8,128)(2,1)} %copy.75) | data formatting | bytes 3538944 | tf_op jit(solution)/shard_map/reshape;reshape | solution.py:173
  227.6 2.7 %fusion.6 = bf16[1,64,1536]{2,1,0:T(8,128)(2,1)} fusion(f32[64,1536]{1,0:T(8,128)S(1)} %get-tuple-element.14, bf16[64,576]{1,0:T(8,128)(2,1)} %fusion.16, bf16[576,1536]{1,0:T(8,128)(2,1)} %reshape_reshape.12), kind=kOutput, calls=%fused_computation.10 | convolution fusion | flops 113442816 | bytes 2433024 | tf_op jit(solution)/shard_map/dot_general | solution.py:172
  (49 shorter events, 16.9 us)
Async XLA Ops:
  0.0 149.8 %copy-start = (bf16[1,1536,1024]{2,1,0:T(8,128)(2,1)S(1)}, bf16[1,1536,1024]{2,1,0:T(8,128)(2,1)}, u32[]{:S(2)}) copy-start(bf16[1,1536,1024]{2,1,0:T(8,128)(2,1)} %param.20) | copy-start | bytes 9437188
  34.0 11.3 %copy-start.3 = (s32[1,64,6]{1,0,2:T(1,128)S(1)}, s32[1,64,6]{1,0,2:T(1,128)}, u32[]{:S(2)}) copy-start(s32[1,64,6]{1,0,2:T(1,128)} %param.18) | copy-start | bytes 4612
  40.9 19.9 %all-to-all-start.1 = ((f32[4,64,1536]{2,1,0:T(8,128)}), f32[4,64,1536]{2,1,0:T(8,128)}, u32[]{:S(2)}, u32[]{:S(2)}) async-start(f32[4,64,1536]{2,1,0:T(8,128)} %bitcast.89), calls=%async_computation.1 | async-start | bytes 3145728 | tf_op jit(solution)/shard_map/all_to_all | solution.py:120
  60.8 2.4 %copy-start.1 = (bf16[1,64,1536]{2,1,0:T(8,128)(2,1)S(1)}, bf16[1,64,1536]{2,1,0:T(8,128)(2,1)}, u32[]{:S(2)}) copy-start(bf16[1,64,1536]{2,1,0:T(8,128)(2,1)} %param.11) | copy-start | bytes 589828
  63.3 3.5 %copy-start.2 = (pred[576,64]{0,1:T(8,128)(4,1)S(1)}, pred[576,64]{0,1:T(8,128)(4,1)}, u32[]{:S(2)}) copy-start(pred[576,64]{0,1:T(8,128)(4,1)} %fusion.13) | copy-start | bytes 110596
  63.3 3.5 %copy-start.4 = (f32[1536]{0:T(1024)S(1)}, f32[1536]{0:T(1024)}, u32[]{:S(2)}) copy-start(f32[1536]{0:T(1024)} %param.17) | copy-start | bytes 18436
  149.8 3.6 %copy-start.6 = (bf16[1,512,1536]{2,1,0:T(8,128)(2,1)S(1)}, bf16[1,512,1536]{2,1,0:T(8,128)(2,1)}, u32[]{:S(2)}) copy-start(bf16[1,512,1536]{2,1,0:T(8,128)(2,1)} %param.21) | copy-start | bytes 4718596
  164.3 5.6 %copy-start.5 = (bf16[1,64,6]{1,2,0:T(8,128)(2,1)S(1)}, bf16[1,64,6]{1,2,0:T(8,128)(2,1)}, u32[]{:S(2)}) copy-start(bf16[1,64,6]{1,2,0:T(8,128)(2,1)} %param.19) | copy-start | bytes 2308
  164.3 45.5 %all-to-all-start.4 = ((bf16[32,2,9,1536]{3,1,2,0:T(2,128)(2,1)}), bf16[32,2,9,1536]{3,1,2,0:T(2,128)(2,1)}, u32[]{:S(2)}, u32[]{:S(2)}) async-start(bf16[32,2,9,1536]{3,1,2,0:T(2,128)(2,1)} %copy.73), calls=%async_computation.4 | async-start | bytes 3538944 | tf_op jit(solution)/shard_map/all_to_all | solution.py:89

commit v4 on v3

v4 whole, which is shorter than its diff:
```python
import jax
import jax.numpy as jnp
from jax import lax
from jax.experimental import pallas as pl
from jax.experimental.pallas import tpu as pltpu
from jax.sharding import Mesh, PartitionSpec as P

D = 1536
KVH = 4
HD = 128
GROUP = 3


NEG_BIG = -1e30


def attend_kernel(scal_ref, q_ref, kc_ref, vc_ref, kn_ref, vn_ref, out_ref):
    head = pl.program_id(0) * GROUP + pl.program_id(1)
    heads = KVH * GROUP
    ctx_pos = scal_ref[0]
    length = scal_ref[1]
    scale = HD ** (-0.5)
    q = q_ref[...]
    dims = (((1,), (1,)), ((), ()))
    s_c = lax.dot_general(q, kc_ref[...], dims, preferred_element_type=jnp.float32) * scale
    s_n = lax.dot_general(q, kn_ref[...], dims, preferred_element_type=jnp.float32) * scale
    n_q, n_cache = s_c.shape
    n_new = s_n.shape[1]
    use_c = ctx_pos * n_cache + lax.broadcasted_iota(jnp.int32, (n_q, n_cache), 1) < length
    use_n = ctx_pos * n_new + lax.broadcasted_iota(jnp.int32, (n_q, n_new), 1) <= (
        lax.broadcasted_iota(jnp.int32, (n_q, n_new), 0)
    )
    top = jnp.maximum(
        jnp.max(jnp.where(use_c, s_c, NEG_BIG), 1, keepdims=True),
        jnp.max(jnp.where(use_n, s_n, NEG_BIG), 1, keepdims=True),
    )
    p_c = jnp.where(use_c, jnp.exp(s_c - top), 0.0)
    p_n = jnp.where(use_n, jnp.exp(s_n - top), 0.0)
    total = jnp.sum(p_c, 1, keepdims=True) + jnp.sum(p_n, 1, keepdims=True)
    acc = jnp.dot(
        p_c.astype(jnp.bfloat16), vc_ref[...], preferred_element_type=jnp.float32
    ) + jnp.dot(p_n.astype(jnp.bfloat16), vn_ref[...], preferred_element_type=jnp.float32)
    out_ref[:, pl.ds(pl.multiple_of(head * HD, HD), HD)] = acc
    stat_cols = slice(heads * HD, (heads + 1) * HD)

    @pl.when(head == 0)
    def _():
        out_ref[:, stat_cols] = jnp.zeros((n_q, HD), jnp.float32)

    lane = lax.broadcasted_iota(jnp.int32, (n_q, HD), 1)
    held = out_ref[:, stat_cols]
    out_ref[:, stat_cols] = jnp.where(lane == head, top, jnp.where(lane == heads + head, total, held))


def partial_attention(scal, all_queries, cache_rows, new_rows):
    n_q = all_queries.shape[0]
    n_cache = cache_rows.shape[0]
    n_new = new_rows.shape[0]
    heads = KVH * GROUP
    width = (heads + 1) * HD
    cost = pl.CostEstimate(
        flops=4 * n_q * (n_cache + n_new) * HD * heads,
        transcendentals=n_q * (n_cache + n_new) * heads,
        bytes_accessed=2 * (all_queries.size + cache_rows.size + new_rows.size) + 4 * n_q * width,
    )
    return pl.pallas_call(
        attend_kernel,
        out_shape=jax.ShapeDtypeStruct((n_q, width), jnp.float32),
        grid_spec=pltpu.PrefetchScalarGridSpec(
            num_scalar_prefetch=1,
            grid=(KVH, GROUP),
            in_specs=[
                pl.BlockSpec((n_q, HD), lambda k, g, s: (0, k * GROUP + g)),
                pl.BlockSpec((n_cache, HD), lambda k, g, s: (0, k)),
                pl.BlockSpec((n_cache, HD), lambda k, g, s: (0, KVH + k)),
                pl.BlockSpec((n_new, HD), lambda k, g, s: (0, k)),
                pl.BlockSpec((n_new, HD), lambda k, g, s: (0, KVH + k)),
            ],
            out_specs=pl.BlockSpec((n_q, width), lambda k, g, s: (0, 0)),
        ),
        cost_estimate=cost,
    )(scal, all_queries, cache_rows, cache_rows, new_rows, new_rows)


EXP_AXES = ("z", "x", "core")
CHIP_AXES = ("z", "x")


def local(
    residual_in,
    queries,
    new_kv,
    cache_kv,
    cache_len,
    out_proj,
    norm_gain,
    routes,
    route_w,
    w_gate_up,
    w_down,
):
    tok_count = residual_in.shape[1]
    cache_rows = cache_kv.shape[1]
    n_ctx = lax.axis_size("ctx")
    ctx_pos = lax.axis_index("ctx")
    length = cache_len[0]
    score_scale = HD ** (-0.5)
    heads = KVH * GROUP

    all_queries = lax.all_gather(queries[0], "ctx", axis=0, tiled=True)
    scal = jnp.stack([ctx_pos, length]).astype(jnp.int32)
    part = partial_attention(scal, all_queries, cache_kv[0], new_kv[0])
    got = lax.all_to_all(
        part.reshape(n_ctx, tok_count, part.shape[1]), "ctx", split_axis=0, concat_axis=0, tiled=True
    )
    got_acc = got[..., : heads * HD].reshape(n_ctx, tok_count, heads, HD)
    got_max = got[..., heads * HD : heads * HD + heads]
    got_sum = got[..., heads * HD + heads : heads * HD + 2 * heads]
    top_max = jnp.max(got_max, 0)
    rescale = jnp.exp(got_max - top_max[None])
    total_sum = jnp.sum(rescale * got_sum, 0)
    total_acc = jnp.sum(rescale[..., None] * got_acc, 0)
    attended = (total_acc / total_sum[..., None]).reshape(tok_count, heads * HD)
    attended = attended.astype(jnp.bfloat16)
    mixed = (
        residual_in[0].astype(jnp.float32)
        + jnp.dot(attended, out_proj, preferred_element_type=jnp.float32)
    ).astype(jnp.bfloat16)
    widened = mixed.astype(jnp.float32)
    normed = (
        widened * lax.rsqrt(jnp.mean(widened * widened, -1, keepdims=True) + 1e-06) * norm_gain
    ).astype(jnp.bfloat16)

    top_count = routes.shape[2]
    core_size = lax.axis_size("core")
    core_pos = lax.axis_index("core")
    expert_total = w_gate_up.shape[0] * lax.axis_size(EXP_AXES)
    capacity = min(tok_count, 3 * tok_count * top_count // (2 * expert_total))
    packed = jnp.concatenate(
        [
            normed,
            routes[0].astype(jnp.bfloat16),
            route_w[0],
            jnp.zeros((tok_count, HD - 2 * top_count), jnp.bfloat16),
        ],
        -1,
    )
    both = lax.all_gather(packed, "core", axis=0, tiled=True)
    normed_both = both[:, :D]
    routes_both = both[:, D : D + top_count].astype(jnp.int32)
    weights_both = both[:, D + top_count : D + 2 * top_count]
    expert_ids = routes_both.reshape(core_size, tok_count * top_count)
    one_hot = (expert_ids[..., None] == jnp.arange(expert_total)).astype(jnp.int32)
    before = jnp.cumsum(one_hot, 1) - one_hot
    slot_index = jnp.sum(before * one_hot, -1)
    block_rows = core_size * capacity
    source_core = jnp.arange(core_size)[:, None]
    dest = jnp.where(
        expert_ids % core_size == core_pos,
        (expert_ids // core_size) * block_rows + source_core * capacity + slot_index,
        -1,
    ).reshape(core_size * tok_count, top_count)
    chip_count = expert_total // core_size
    slot_ids = jnp.arange(chip_count * block_rows)
    hits = dest[None, :, :] == slot_ids[:, None, None]
    select = jnp.any(hits, -1).astype(jnp.bfloat16)
    outgoing = jnp.dot(select, normed_both, preferred_element_type=jnp.float32).astype(jnp.bfloat16)
    incoming = lax.all_to_all(
        outgoing.reshape(chip_count, block_rows, D), CHIP_AXES, split_axis=0, concat_axis=0, tiled=True
    ).reshape(-1, D)
    hidden_half = w_gate_up.shape[2] // 2
    gate_up = jnp.dot(incoming, w_gate_up[0], preferred_element_type=jnp.float32)
    activated = (jax.nn.silu(gate_up[:, :hidden_half]) * gate_up[:, hidden_half:]).astype(
        jnp.bfloat16
    )
    result = jnp.dot(activated, w_down[0], preferred_element_type=jnp.float32).astype(jnp.bfloat16)
    returned = lax.all_to_all(
        result.reshape(chip_count, block_rows, D), CHIP_AXES, split_axis=0, concat_axis=0, tiled=True
    ).reshape(-1, D)
    combine = jnp.sum(
        jnp.where(
            hits.transpose(1, 0, 2), weights_both[:, None, :], jnp.zeros((), weights_both.dtype)
        ),
        -1,
    )
    partial = jnp.dot(combine, returned, preferred_element_type=jnp.float32)
    blended = lax.psum_scatter(partial, "core", scatter_dimension=0, tiled=True)
    return (widened + blended).astype(jnp.bfloat16)[None]


def solution(mesh):
    exp_size = mesh.shape["exp"]
    x_size, core_size = 4, 2
    devices = mesh.devices.reshape(
        mesh.shape["ctx"], exp_size // (x_size * core_size), x_size, core_size
    )
    fine = Mesh(devices, ("ctx",) + EXP_AXES)
    rows = P(EXP_AXES, "ctx", None)
    return jax.shard_map(
        local,
        mesh=fine,
        in_specs=(
            rows,
            rows,
            rows,
            rows,
            P(EXP_AXES),
            P(),
            P(),
            rows,
            rows,
            P(EXP_AXES, None, None),
            P(EXP_AXES, None, None),
        ),
        out_specs=rows,
        check_vma=False,
    )
```

time: 231 us -> 274 us (1.19)
  waiting for transfers between devices: 45.6 us -> 81.1 us
  between operations: 0.86 us -> 14.3 us
  local copies, waits for them, and re-layouts: 44.6 us -> 31.4 us
  other arithmetic: 6.37 us -> 16.9 us
  blocking collectives: 94.9 us -> 89.1 us
    another operation x6 -> x2, local copies, waits for them, and re-layouts: 24.8 us -> 0.01 us  [the longest x2 8.58 us: undispatch(): split = rows.reshape(-1, 2, *rows.shape[1:])]
    all_to_all x2, waiting for transfers between devices: 45.6 us -> 68.1 us  [the longest x1 51.2 us: local(): lax.all_to_all(result.reshape(chip_count, block_rows, D), CHIP_AXES, spli...]
    reshape x0 -> x4, local copies, waits for them, and re-layouts: none -> 14.9 us  [the longest x1 3.84 us: local(): incoming = lax.all_to_all(outgoing.reshape(chip_count, block_rows, D), CH...]
    reduce_scatter x0 -> x1, waiting for transfers between devices: none -> 13 us  [local(): blended = lax.psum_scatter(partial, 'core', scatter_dimension=0, tiled=True)]
    all_to_all x4 -> x1, blocking collectives: 80.4 us -> 68 us  [local(): lax.all_to_all(outgoing.reshape(chip_count, block_rows, D), CHIP_AXES, sp...]
    all_to_all x5 -> x0, local copies, waits for them, and re-layouts: 9.49 us -> none  [the longest x1 2.78 us: undispatch(): lax.all_to_all(split, 'core', split_axis=1, concat_axis=1, tiled=True)]
    all_gather x0 -> x1, blocking collectives: none -> 6.79 us  [local(): both = lax.all_gather(packed, 'core', axis=0, tiled=True)]
    another operation x2, other arithmetic: 0.95 us -> 4.38 us
  transfers between devices with their start and end apart: 2 -> 3, of which waited for: 2 -> 3; matrix products, arithmetic and copies ran while one was open for 4% -> 1% of each run, Pallas kernels for 0% -> 0%
where the time goes in v4:
time: 274 us; the launch traced here: 272 us
  blocking collectives  89.1 us (33%)
  waiting for transfers between devices  81.1 us (30%)
  local copies, waits for them, and re-layouts  31.4 us (11%)
  other arithmetic  16.9 us (6%)
  matrix products  15.1 us (6%)
  Pallas kernels  14.8 us (5%)
  between operations  14.3 us (5%)
  starting transfers between devices  9.34 us (3%)
    all_to_all x1, blocking collectives, local(): lax.all_to_all(outgoing.reshape(chip_count, block_rows, D), CHIP_AXES, sp...  68 us
    all_to_all x1, waiting for transfers between devices, local(): lax.all_to_all(result.reshape(chip_count, block_rows, D), CHIP_AXES, spli...  51.2 us
    all_to_all x1, waiting for transfers between devices, local(): lax.all_to_all(part.reshape(n_ctx, tok_count, part.shape[1]), 'ctx', spli...  16.8 us
    pallas_call x1, Pallas kernels, partial_attention(): pl.pallas_call(attend_kernel, out_shape=jax.ShapeDtypeStruct((n_q, width)...  14.8 us
    all_gather x1, blocking collectives, local(): all_queries = lax.all_gather(queries[0], 'ctx', axis=0, tiled=True)  14.2 us
    reduce_scatter x1, waiting for transfers between devices, local(): blended = lax.psum_scatter(partial, 'core', scatter_dimension=0, tiled=True)  13 us
    all_gather x1, blocking collectives, local(): both = lax.all_gather(packed, 'core', axis=0, tiled=True)  6.79 us
  transfers between devices with their start and end apart: 3, of which 3 were waited for; matrix products, arithmetic and copies ran while one was open for 1% of the time, Pallas kernels for 0%

profile of v4, /device:TPU:1, one launch (start us, length us, event | category | flops | bytes accessed | tf_op | source)
XLA Modules:
  0.0 272.1 jit_solution(2775781482611920184)
XLA Ops:
  7.3 14.2 %all-gather = bf16[1,256,1536]{2,1,0:T(8,128)(2,1)} all-gather(bf16[1,64,1536]{2,1,0:T(8,128)(2,1)} %param.12), channel_id=2, replica_groups=mesh['ctx'=4,'z'=8,'x'=4,'core'=2] {'ctx'}, dimensions={1}, use_global_device_ids=true | all-gather | bytes 983040 | tf_op jit(solution)/shard_map/all_gather | solution.py:110
  22.2 14.8 %shard_map.109 = f32[256,1664]{1,0:T(8,128)} custom-call(s32[2]{0:T(128)} %pad_add_fusion.scal_ref, bf16[256,1536]{1,0:T(8,128)(2,1)} %bitcast.57, bf16[1024,1024]{1,0:T(8,128)(2,1)} %bitcast.54, bf16[1024,1024]{1,0:T(8,128)(2,1)} %bitcast.55, bf16[64,1024]{1,0:T(8,128)(2,1)} %bitcast.59, bf16[64,1024]{1,0:T(8,128)(2,1)} %bitcast.60), custom_call_target="tpu_custom_call" | custom-call | flops 1711276032 | bytes 4718592 | tf_op jit(solution)/shard_map/pallas_call | solution.py:66
  37.0 4.5 %all-to-all-start = ((f32[4,64,1664]{2,1,0:T(8,128)}), f32[4,64,1664]{2,1,0:T(8,128)}, u32[]{:S(2)}, u32[]{:S(2)}) async-start(f32[4,64,1664]{2,1,0:T(8,128)} %bitcast.56), calls=%async_computation | async-start | bytes 3407872 | tf_op jit(solution)/shard_map/all_to_all | solution.py:113
  43.1 16.8 %all-to-all-done = f32[4,64,1664]{2,1,0:T(8,128)} async-done(((f32[4,64,1664]{2,1,0:T(8,128)}), f32[4,64,1664]{2,1,0:T(8,128)}, u32[]{:S(2)}, u32[]{:S(2)}) %all-to-all-start) | async-done | bytes 1703968 | tf_op jit(solution)/shard_map/all_to_all | solution.py:113
  62.0 2.0 mul.59
  64.0 2.6 mul.60
  66.5 2.2 fusion.6
  69.0 3.4 %multiply_reduce_fusion = (f32[64]{0:T(128)S(1)}, f32[64,1536]{1,0:T(8,128)S(1)}) fusion(bf16[1536,1536]{1,0:T(8,128)(2,1)} %param.16, f32[64,1536]{1,0:T(8,128)S(1)} %fusion.6, f32[8,8,12,128]{3,2,1,0:T(8,128)S(1)} %bitcast.58, bf16[1,64,1536]{2,1,0:T(8,128)(2,1)S(1)} %copy-done.2), kind=kOutput, calls=%fused_computation.23 | convolution fusion | flops 302776256 | bytes 6095104 | tf_op jit(solution)/shard_map/dot_general | solution.py:127
  75.5 6.8 %all_gather.7 = bf16[128,1664]{1,0:T(8,128)(2,1)S(1)} all-gather(bf16[64,1664]{1,0:T(8,128)(2,1)} %concatenate.3), channel_id=1, replica_groups=mesh['ctx'=4,'z'=8,'x'=4,'core'=2] {'core'}, dimensions={0}, use_global_device_ids=true | all-gather | bytes 638976 | tf_op jit(solution)/shard_map/all_gather | solution.py:148
  86.4 4.4 %reduce-window.6 = s32[2,64,3,128]{3,1,2,0:T(8,128)} reduce-window(s32[2,64,3,128]{3,1,2,0:T(8,128)} %fusion.19, s32[]{:T(128)} %constant.55.clone.1), window={size=1x1x1x128 pad=0_0x0_0x0_0x127_0}, to_apply=%region_4.0 | reduce-window | flops 6242304 | bytes 393220 | tf_op jit(solution)/shard_map/reduce-window
  90.8 1.7 slice.44
  98.1 2.8 %convolution_convert_fusion = bf16[576,1536]{1,0:T(8,128)(2,1)} fusion(pred[576,128]{1,0:T(8,128)(4,1)S(1)} %fusion.5, bf16[128,1664]{1,0:T(8,128)(2,1)} %copy-done.1), kind=kOutput, calls=%fused_computation.2 | convolution fusion | flops 227377152 | bytes 2236416 | tf_op jit(solution)/shard_map/dot_general | solution.py:167
  100.9 3.6 %reshape.101 = bf16[32,18,1536]{2,1,0:T(8,128)(2,1)} reshape(bf16[576,1536]{1,0:T(8,128)(2,1)} %convolution_convert_fusion) | data formatting | bytes 3538944 | tf_op jit(solution)/shard_map/reshape | solution.py:169
  104.5 68.0 %all_to_all.15 = bf16[32,18,1536]{2,1,0:T(8,128)(2,1)} all-to-all(bf16[32,18,1536]{2,1,0:T(8,128)(2,1)} %reshape.101), channel_id=1, replica_groups=mesh['ctx'=4,'z'=8,'x'=4,'core'=2] {'z','x'}, dimensions={0} | all-to-all | bytes 3538944 | tf_op jit(solution)/shard_map/all_to_all | solution.py:168
  172.6 3.8 %reshape.102 = bf16[576,1536]{1,0:T(8,128)(2,1)} reshape(bf16[32,18,1536]{2,1,0:T(8,128)(2,1)} %all_to_all.15) | data formatting | bytes 3538944 | tf_op jit(solution)/shard_map/reshape | solution.py:170
  176.4 3.6 %fusion = f32[576,1024]{1,0:T(8,128)S(1)} fusion(bf16[576,1536]{1,0:T(8,128)(2,1)} %reshape.102, bf16[1,1536,1024]{2,1,0:T(8,128)(2,1)S(1)} %copy-done), kind=kOutput, calls=%fused_computation | convolution fusion | flops 1811939328 | bytes 7274496 | tf_op jit(solution)/shard_map/dot_general | solution.py:172
  180.0 2.3 convolution_convert_fusion.1
  182.4 3.6 %reshape.103 = bf16[32,18,1536]{2,1,0:T(8,128)(2,1)} reshape(bf16[576,1536]{1,0:T(8,128)(2,1)} %convolution_convert_fusion.1) | data formatting | bytes 3538944 | tf_op jit(solution)/shard_map/reshape | solution.py:178
  186.0 4.8 %all-to-all-start.2 = ((bf16[32,18,1536]{2,1,0:T(8,128)(2,1)}), bf16[32,18,1536]{2,1,0:T(8,128)(2,1)}, u32[]{:S(2)}, u32[]{:S(2)}) async-start(bf16[32,18,1536]{2,1,0:T(8,128)(2,1)} %reshape.103), calls=%async_computation.2 | async-start | bytes 4718592 | tf_op jit(solution)/shard_map/all_to_all | solution.py:177
  192.5 51.2 %all-to-all-done.2 = bf16[32,18,1536]{2,1,0:T(8,128)(2,1)} async-done(((bf16[32,18,1536]{2,1,0:T(8,128)(2,1)}), bf16[32,18,1536]{2,1,0:T(8,128)(2,1)}, u32[]{:S(2)}, u32[]{:S(2)}) %all-to-all-start.2) | async-done | bytes 1769504 | tf_op jit(solution)/shard_map/all_to_all | solution.py:177
  243.8 3.8 %reshape.104 = bf16[576,1536]{1,0:T(8,128)(2,1)} reshape(bf16[32,18,1536]{2,1,0:T(8,128)(2,1)} %all-to-all-done.2) | data formatting | bytes 3538944 | tf_op jit(solution)/shard_map/reshape | solution.py:179
  247.6 2.9 %fusion.32 = f32[128,1536]{1,0:T(8,128)} fusion(bf16[128,576]{0,1:T(8,128)(2,1)} %fusion.9, bf16[576,1536]{1,0:T(8,128)(2,1)} %reshape.104), kind=kOutput, calls=%fused_computation.59 | convolution fusion | flops 226492416 | bytes 2703360 | tf_op jit(solution)/shard_map/dot_general | solution.py:186
  250.6 13.0 %reduce-scatter.2.cloned.1.call-done = f32[64,1536]{1,0:T(8,128)} async-done(((f32[128,1536]{1,0:T(8,128)}), f32[64,1536]{1,0:T(8,128)}) %reduce-scatter.2.cloned.1.call-update) | async-done | bytes 393232 | tf_op jit(solution)/shard_map/reduce_scatter | solution.py:187
  263.5 1.7 fusion.14
  (47 shorter events, 19.0 us)
Async XLA Ops:
  6.5 169.9 %copy-start = (bf16[1,1536,1024]{2,1,0:T(8,128)(2,1)S(1)}, bf16[1,1536,1024]{2,1,0:T(8,128)(2,1)}, u32[]{:S(2)}) copy-start(bf16[1,1536,1024]{2,1,0:T(8,128)(2,1)} %param.20) | copy-start | bytes 9437188
  37.0 4.5 %copy-start.4 = (s32[1,64,6]{1,0,2:T(1,128)S(1)}, s32[1,64,6]{1,0,2:T(1,128)}, u32[]{:S(2)}) copy-start(s32[1,64,6]{1,0,2:T(1,128)} %param.18) | copy-start | bytes 4612
  37.0 4.6 %copy-start.5 = (bf16[1,64,6]{1,2,0:T(8,128)(2,1)S(1)}, bf16[1,64,6]{1,2,0:T(8,128)(2,1)}, u32[]{:S(2)}) copy-start(bf16[1,64,6]{1,2,0:T(8,128)(2,1)} %param.19) | copy-start | bytes 2308
  37.0 22.9 %all-to-all-start = ((f32[4,64,1664]{2,1,0:T(8,128)}), f32[4,64,1664]{2,1,0:T(8,128)}, u32[]{:S(2)}, u32[]{:S(2)}) async-start(f32[4,64,1664]{2,1,0:T(8,128)} %bitcast.56), calls=%async_computation | async-start | bytes 3407872 | tf_op jit(solution)/shard_map/all_to_all | solution.py:113
  66.5 2.4 copy-start.2
  69.0 3.5 %copy-start.3 = (f32[1536]{0:T(1024)S(1)}, f32[1536]{0:T(1024)}, u32[]{:S(2)}) copy-start(f32[1536]{0:T(1024)} %param.17) | copy-start | bytes 18436
  75.5 19.9 %copy-start.6 = (s32[128]{0:T(128)S(1)}, s32[128]{0:T(128)}, u32[]{:S(2)}) copy-start(s32[128]{0:T(128)} %add.58) | copy-start | bytes 1540
  82.3 0.8 copy-start.1
  176.4 3.6 %copy-start.7 = (bf16[1,512,1536]{2,1,0:T(8,128)(2,1)S(1)}, bf16[1,512,1536]{2,1,0:T(8,128)(2,1)}, u32[]{:S(2)}) copy-start(bf16[1,512,1536]{2,1,0:T(8,128)(2,1)} %param.21) | copy-start | bytes 4718596
  186.0 57.8 %all-to-all-start.2 = ((bf16[32,18,1536]{2,1,0:T(8,128)(2,1)}), bf16[32,18,1536]{2,1,0:T(8,128)(2,1)}, u32[]{:S(2)}, u32[]{:S(2)}) async-start(bf16[32,18,1536]{2,1,0:T(8,128)(2,1)} %reshape.103), calls=%async_computation.2 | async-start | bytes 4718592 | tf_op jit(solution)/shard_map/all_to_all | solution.py:177
  190.8 72.8 %reduce-scatter.2.cloned.1.call-start = ((), (), s32[]{:S(2)}) async-start(), calls=%async_computation.4 | async-start | bytes 1179648 | tf_op jit(solution)/shard_map/reduce_scatter | solution.py:187
Sparse Core Ops, SparseCore 0:
  250.7 12.7 reduce-scatter.1

commit v5 on v4

--- a/solution.py
+++ b/solution.py
@@ -40,16 +40,22 @@
     acc = jnp.dot(
         p_c.astype(jnp.bfloat16), vc_ref[...], preferred_element_type=jnp.float32
     ) + jnp.dot(p_n.astype(jnp.bfloat16), vn_ref[...], preferred_element_type=jnp.float32)
-    out_ref[:, pl.ds(pl.multiple_of(head * HD, HD), HD)] = acc
+    out_ref[:, pl.ds(pl.multiple_of(head * HD, HD), HD)] = acc.astype(out_ref.dtype)
     stat_cols = slice(heads * HD, (heads + 1) * HD)
 
     @pl.when(head == 0)
     def _():
-        out_ref[:, stat_cols] = jnp.zeros((n_q, HD), jnp.float32)
-
+        out_ref[:, stat_cols] = jnp.zeros((n_q, HD), out_ref.dtype)
+
+    top_hi = top.astype(jnp.bfloat16).astype(jnp.float32)
+    total_hi = total.astype(jnp.bfloat16).astype(jnp.float32)
     lane = lax.broadcasted_iota(jnp.int32, (n_q, HD), 1)
-    held = out_ref[:, stat_cols]
-    out_ref[:, stat_cols] = jnp.where(lane == head, top, jnp.where(lane == heads + head, total, held))
+    held = out_ref[:, stat_cols].astype(jnp.float32)
+    held = jnp.where(lane == head, top_hi, held)
+    held = jnp.where(lane == heads + head, top - top_hi, held)
+    held = jnp.where(lane == 2 * heads + head, total_hi, held)
+    held = jnp.where(lane == 3 * heads + head, total - total_hi, held)
+    out_ref[:, stat_cols] = held.astype(out_ref.dtype)
 
 
 def partial_attention(scal, all_queries, cache_rows, new_rows):
@@ -61,11 +67,11 @@
     cost = pl.CostEstimate(
         flops=4 * n_q * (n_cache + n_new) * HD * heads,
         transcendentals=n_q * (n_cache + n_new) * heads,
-        bytes_accessed=2 * (all_queries.size + cache_rows.size + new_rows.size) + 4 * n_q * width,
+        bytes_accessed=2 * (all_queries.size + cache_rows.size + new_rows.size) + 2 * n_q * width,
     )
     return pl.pallas_call(
         attend_kernel,
-        out_shape=jax.ShapeDtypeStruct((n_q, width), jnp.float32),
+        out_shape=jax.ShapeDtypeStruct((n_q, width), jnp.bfloat16),
         grid_spec=pltpu.PrefetchScalarGridSpec(
             num_scalar_prefetch=1,
             grid=(KVH, GROUP),
@@ -113,9 +119,11 @@
     got = lax.all_to_all(
         part.reshape(n_ctx, tok_count, part.shape[1]), "ctx", split_axis=0, concat_axis=0, tiled=True
     )
-    got_acc = got[..., : heads * HD].reshape(n_ctx, tok_count, heads, HD)
-    got_max = got[..., heads * HD : heads * HD + heads]
-    got_sum = got[..., heads * HD + heads : heads * HD + 2 * heads]
+    got_acc = got[..., : heads * HD].astype(jnp.float32).reshape(n_ctx, tok_count, heads, HD)
+    got_stats = got[..., heads * HD : heads * HD + 4 * heads].astype(jnp.float32)
+    got_stats = got_stats.reshape(n_ctx, tok_count, 4, heads)
+    got_max = got_stats[:, :, 0] + got_stats[:, :, 1]
+    got_sum = got_stats[:, :, 2] + got_stats[:, :, 3]
     top_max = jnp.max(got_max, 0)
     rescale = jnp.exp(got_max - top_max[None])
     total_sum = jnp.sum(rescale * got_sum, 0)
@@ -157,33 +165,34 @@
     source_core = jnp.arange(core_size)[:, None]
     dest = jnp.where(
         expert_ids % core_size == core_pos,
-        (expert_ids // core_size) * block_rows + source_core * capacity + slot_index,
+        ((expert_ids // core_size) * capacity + slot_index) * core_size + source_core,
         -1,
     ).reshape(core_size * tok_count, top_count)
     chip_count = expert_total // core_size
     slot_ids = jnp.arange(chip_count * block_rows)
     hits = dest[None, :, :] == slot_ids[:, None, None]
-    select = jnp.any(hits, -1).astype(jnp.bfloat16)
-    outgoing = jnp.dot(select, normed_both, preferred_element_type=jnp.float32).astype(jnp.bfloat16)
-    incoming = lax.all_to_all(
-        outgoing.reshape(chip_count, block_rows, D), CHIP_AXES, split_axis=0, concat_axis=0, tiled=True
-    ).reshape(-1, D)
+    slot_shape = (chip_count, capacity, core_size)
+    select = jnp.any(hits, -1).astype(jnp.bfloat16).reshape(*slot_shape, -1)
+    outgoing = jnp.einsum(
+        "jscr,rd->jscd", select, normed_both, preferred_element_type=jnp.float32
+    ).astype(jnp.bfloat16)
+    incoming = lax.all_to_all(outgoing, CHIP_AXES, split_axis=0, concat_axis=0, tiled=True)
     hidden_half = w_gate_up.shape[2] // 2
-    gate_up = jnp.dot(incoming, w_gate_up[0], preferred_element_type=jnp.float32)
-    activated = (jax.nn.silu(gate_up[:, :hidden_half]) * gate_up[:, hidden_half:]).astype(
+    gate_up = jnp.einsum("jscd,df->jscf", incoming, w_gate_up[0], preferred_element_type=jnp.float32)
+    activated = (jax.nn.silu(gate_up[..., :hidden_half]) * gate_up[..., hidden_half:]).astype(
         jnp.bfloat16
     )
-    result = jnp.dot(activated, w_down[0], preferred_element_type=jnp.float32).astype(jnp.bfloat16)
-    returned = lax.all_to_all(
-        result.reshape(chip_count, block_rows, D), CHIP_AXES, split_axis=0, concat_axis=0, tiled=True
-    ).reshape(-1, D)
+    result = jnp.einsum(
+        "jscf,fd->jscd", activated, w_down[0], preferred_element_type=jnp.float32
+    ).astype(jnp.bfloat16)
+    returned = lax.all_to_all(result, CHIP_AXES, split_axis=0, concat_axis=0, tiled=True)
     combine = jnp.sum(
         jnp.where(
             hits.transpose(1, 0, 2), weights_both[:, None, :], jnp.zeros((), weights_both.dtype)
         ),
         -1,
-    )
-    partial = jnp.dot(combine, returned, preferred_element_type=jnp.float32)
+    ).reshape(-1, *slot_shape)
+    partial = jnp.einsum("tjsc,jscd->td", combine, returned, preferred_element_type=jnp.float32)
     blended = lax.psum_scatter(partial, "core", scatter_dimension=0, tiled=True)
     return (widened + blended).astype(jnp.bfloat16)[None]
 

time: 274 us -> 228 us (0.83)
  waiting for transfers between devices: 81.1 us -> 59.1 us
  blocking collectives: 89.1 us -> 75.2 us
  local copies, waits for them, and re-layouts: 31.4 us -> 25 us
  matrix products: 15.1 us -> 11.1 us
    all_to_all x1, blocking collectives: 68 us -> 53.9 us  [local(): lax.all_to_all(outgoing, CHIP_AXES, split_axis=0, concat_axis=0, tiled=True)]
    reshape x4 -> x2, local copies, waits for them, and re-layouts: 14.9 us -> 1.65 us  [the longest x1 1.63 us: local(): select = jnp.any(hits, -1).astype(jnp.bfloat16).reshape(*slot_shape, -1)]
    all_to_all x1, waiting for transfers between devices: 51.2 us -> 38.2 us  [local(): lax.all_to_all(result, CHIP_AXES, split_axis=0, concat_axis=0, tiled=True)]
    all_to_all x1, waiting for transfers between devices: 16.8 us -> 7.5 us  [local(): lax.all_to_all(part.reshape(n_ctx, tok_count, part.shape[1]), 'ctx', spli...]
    convert_element_type x0 -> x2, local copies, waits for them, and re-layouts: none -> 4.84 us  [the longest x1 3.02 us: local(): result = jnp.einsum('jscf,fd->jscd', activated, w_down[0], preferred_elem...]
    dot_general x4, matrix products: 11.7 us -> 7.72 us  [the longest x1 2.94 us: local(): jnp.einsum('tjsc,jscd->td', combine, returned, preferred_element_type=jnp...]
where the time goes in v5:
time: 228 us; the launch traced here: 226 us
  blocking collectives  75.2 us (33%)
  waiting for transfers between devices  59.1 us (26%)
  local copies, waits for them, and re-layouts  25 us (11%)
  other arithmetic  16.9 us (7%)
  Pallas kernels  14.9 us (7%)
  between operations  14.3 us (6%)
  matrix products  11.1 us (5%)
  starting transfers between devices  9.68 us (4%)
    all_to_all x1, blocking collectives, local(): lax.all_to_all(outgoing, CHIP_AXES, split_axis=0, concat_axis=0, tiled=True)  53.9 us
    all_to_all x1, waiting for transfers between devices, local(): lax.all_to_all(result, CHIP_AXES, split_axis=0, concat_axis=0, tiled=True)  38.2 us
    pallas_call x1, Pallas kernels, partial_attention(): pl.pallas_call(attend_kernel, out_shape=jax.ShapeDtypeStruct((n_q, width)...  14.9 us
    all_gather x1, blocking collectives, local(): all_queries = lax.all_gather(queries[0], 'ctx', axis=0, tiled=True)  14.2 us
    reduce_scatter x1, waiting for transfers between devices, local(): blended = lax.psum_scatter(partial, 'core', scatter_dimension=0, tiled=True)  13.4 us
    all_to_all x1, waiting for transfers between devices, local(): lax.all_to_all(part.reshape(n_ctx, tok_count, part.shape[1]), 'ctx', spli...  7.5 us
    all_gather x1, blocking collectives, local(): both = lax.all_gather(packed, 'core', axis=0, tiled=True)  7.09 us
    all_to_all x1, starting transfers between devices, local(): lax.all_to_all(result, CHIP_AXES, split_axis=0, concat_axis=0, tiled=True)  5.42 us
  transfers between devices with their start and end apart: 3, of which 3 were waited for; matrix products, arithmetic and copies ran while one was open for 1% of the time, Pallas kernels for 0%

profile of v5, /device:TPU:1, one launch (start us, length us, event | category | flops | bytes accessed | tf_op | source)
XLA Modules:
  0.0 226.4 jit_solution(82046480383900454)
XLA Ops:
  7.3 14.2 %all-gather = bf16[1,256,1536]{2,1,0:T(8,128)(2,1)} all-gather(bf16[1,64,1536]{2,1,0:T(8,128)(2,1)} %param.12), channel_id=2, replica_groups=mesh['ctx'=4,'z'=8,'x'=4,'core'=2] {'ctx'}, dimensions={1}, use_global_device_ids=true | all-gather | bytes 983040 | tf_op jit(solution)/shard_map/all_gather | solution.py:116
  22.1 14.9 %shard_map.109 = bf16[256,1664]{1,0:T(8,128)(2,1)} custom-call(s32[2]{0:T(128)} %pad_add_fusion.scal_ref, bf16[256,1536]{1,0:T(8,128)(2,1)} %bitcast.76, bf16[1024,1024]{1,0:T(8,128)(2,1)} %bitcast.81, bf16[1024,1024]{1,0:T(8,128)(2,1)} %bitcast.82, bf16[64,1024]{1,0:T(8,128)(2,1)} %bitcast.83, bf16[64,1024]{1,0:T(8,128)(2,1)} %bitcast.84), custom_call_target="tpu_custom_call" | custom-call | flops 1711276032 | bytes 3866624 | tf_op jit(solution)/shard_map/pallas_call | solution.py:72
  37.1 4.2 %all-to-all-start = ((bf16[4,64,1664]{2,1,0:T(8,128)(2,1)}), bf16[4,64,1664]{2,1,0:T(8,128)(2,1)}, u32[]{:S(2)}, u32[]{:S(2)}) async-start(bf16[4,64,1664]{2,1,0:T(8,128)(2,1)} %bitcast.75), calls=%async_computation | async-start | bytes 1703936 | tf_op jit(solution)/shard_map/all_to_all | solution.py:119
  42.8 7.5 %all-to-all-done = bf16[4,64,1664]{2,1,0:T(8,128)(2,1)} async-done(((bf16[4,64,1664]{2,1,0:T(8,128)(2,1)}), bf16[4,64,1664]{2,1,0:T(8,128)(2,1)}, u32[]{:S(2)}, u32[]{:S(2)}) %all-to-all-start) | async-done | bytes 852000 | tf_op jit(solution)/shard_map/all_to_all | solution.py:119
  52.0 2.0 mul.57
  54.0 2.6 %mul.58 = f32[4,64,1536]{2,1,0:T(8,128)} reshape(f32[4,64,12,128]{3,2,1,0:T(8,128)} %mul.57) | data formatting | bytes 3145728 | tf_op jit(solution)/shard_map/mul | solution.py:130
  56.6 1.8 multiply_reduce_fusion
  60.8 3.4 %multiply_reduce_fusion.1 = (f32[64]{0:T(128)S(1)}, f32[64,1536]{1,0:T(8,128)S(1)}) fusion(bf16[64,1536]{0,1:T(8,128)(2,1)S(1)} %fusion.11, bf16[1536,1536]{1,0:T(8,128)(2,1)} %param.16, bf16[1,64,1536]{2,1,0:T(8,128)(2,1)} %param.11), kind=kOutput, calls=%fused_computation.25 | convolution fusion | flops 302579648 | bytes 5505280 | tf_op jit(solution)/shard_map/dot_general | solution.py:135
  65.6 1.7 concatenate.3
  67.3 7.1 %all_gather.7 = bf16[128,1664]{1,0:T(8,128)(2,1)S(1)} all-gather(bf16[64,1664]{1,0:T(8,128)(2,1)} %concatenate.3), channel_id=1, replica_groups=mesh['ctx'=4,'z'=8,'x'=4,'core'=2] {'core'}, dimensions={0}, use_global_device_ids=true | all-gather | bytes 638976 | tf_op jit(solution)/shard_map/all_gather | solution.py:156
  78.5 4.4 %reduce-window.6 = s32[2,64,3,128]{3,1,2,0:T(8,128)} reduce-window(s32[2,64,3,128]{3,1,2,0:T(8,128)} %fusion.18, s32[]{:T(128)} %constant.55.clone.1), window={size=1x1x1x128 pad=0_0x0_0x0_0x127_0}, to_apply=%region_4.0 | reduce-window | flops 6242304 | bytes 393220 | tf_op jit(solution)/shard_map/reduce-window
  82.9 1.7 slice.59
  87.5 1.6 fusion.25
  90.8 1.6 reshape.108
  92.5 1.7 convolution_convert_fusion
  94.2 1.8 copy.107
  96.0 53.9 %all_to_all.15 = bf16[32,9,2,1536]{3,2,1,0:T(2,128)(2,1)S(1)} all-to-all(bf16[32,9,2,1536]{3,2,1,0:T(2,128)(2,1)S(1)} %copy.107), channel_id=1, replica_groups=mesh['ctx'=4,'z'=8,'x'=4,'core'=2] {'z','x'}, dimensions={0} | all-to-all | bytes 3538944 | tf_op jit(solution)/shard_map/all_to_all | solution.py:179
  149.9 2.0 fusion
  153.0 3.0 %copy.110 = bf16[32,9,2,1536]{3,2,1,0:T(2,128)(2,1)} copy(bf16[32,9,2,1536]{3,0,1,2:T(8,128)(2,1)S(1)} %convolution_convert_fusion.1) | data formatting | bytes 3538944 | tf_op jit(solution)/shard_map/convert_element_type | solution.py:187
  156.1 5.4 %all-to-all-start.2 = ((bf16[32,9,2,1536]{3,2,1,0:T(2,128)(2,1)}), bf16[32,9,2,1536]{3,2,1,0:T(2,128)(2,1)}, u32[]{:S(2)}, u32[]{:S(2)}) async-start(bf16[32,9,2,1536]{3,2,1,0:T(2,128)(2,1)} %copy.110), calls=%async_computation.2 | async-start | bytes 3538944 | tf_op jit(solution)/shard_map/all_to_all | solution.py:188
  163.2 38.2 %all-to-all-done.2 = bf16[32,9,2,1536]{3,2,1,0:T(2,128)(2,1)} async-done(((bf16[32,9,2,1536]{3,2,1,0:T(2,128)(2,1)}), bf16[32,9,2,1536]{3,2,1,0:T(2,128)(2,1)}, u32[]{:S(2)}, u32[]{:S(2)}) %all-to-all-start.2) | async-done | bytes 1769504 | tf_op jit(solution)/shard_map/all_to_all | solution.py:188
  201.5 2.9 %convolution_bitcast_fusion = f32[128,1536]{1,0:T(8,128)} fusion(bf16[32,9,2,1536]{3,2,1,0:T(2,128)(2,1)} %all-to-all-done.2, bf16[128,32,9,2]{0,3,2,1:T(2,128)(2,1)} %bitcast.79), kind=kOutput, calls=%fused_computation.4 | convolution fusion | flops 226492416 | bytes 2703360 | tf_op jit(solution)/shard_map/tjsc,jscd->td/dot_general | solution.py:195
  204.4 13.4 %reduce-scatter.2.cloned.1.call-done = f32[64,1536]{1,0:T(8,128)} async-done(((f32[128,1536]{1,0:T(8,128)}), f32[64,1536]{1,0:T(8,128)}) %reduce-scatter.2.cloned.1.call-update) | async-done | bytes 393232 | tf_op jit(solution)/shard_map/reduce_scatter | solution.py:196
  217.8 1.7 fusion.14
  (48 shorter events, 19.1 us)
Async XLA Ops:
  6.5 143.4 %copy-start = (bf16[1,1536,1024]{2,1,0:T(8,128)(2,1)S(1)}, bf16[1,1536,1024]{2,1,0:T(8,128)(2,1)}, u32[]{:S(2)}) copy-start(bf16[1,1536,1024]{2,1,0:T(8,128)(2,1)} %param.20) | copy-start | bytes 9437188
  22.1 19.2 %copy-start.3 = (s32[1,64,6]{1,0,2:T(1,128)S(1)}, s32[1,64,6]{1,0,2:T(1,128)}, u32[]{:S(2)}) copy-start(s32[1,64,6]{1,0,2:T(1,128)} %param.18) | copy-start | bytes 4612
  22.1 19.3 %copy-start.4 = (bf16[1,64,6]{1,2,0:T(8,128)(2,1)S(1)}, bf16[1,64,6]{1,2,0:T(8,128)(2,1)}, u32[]{:S(2)}) copy-start(bf16[1,64,6]{1,2,0:T(8,128)(2,1)} %param.19) | copy-start | bytes 2308
  37.1 13.2 %all-to-all-start = ((bf16[4,64,1664]{2,1,0:T(8,128)(2,1)}), bf16[4,64,1664]{2,1,0:T(8,128)(2,1)}, u32[]{:S(2)}, u32[]{:S(2)}) async-start(bf16[4,64,1664]{2,1,0:T(8,128)(2,1)} %bitcast.75), calls=%async_computation | async-start | bytes 1703936 | tf_op jit(solution)/shard_map/all_to_all | solution.py:119
  60.8 3.5 %copy-start.2 = (f32[1536]{0:T(1024)S(1)}, f32[1536]{0:T(1024)}, u32[]{:S(2)}) copy-start(f32[1536]{0:T(1024)} %param.17) | copy-start | bytes 18436
  67.3 20.2 %copy-start.5 = (s32[128]{0:T(128)S(1)}, s32[128]{0:T(128)}, u32[]{:S(2)}) copy-start(s32[128]{0:T(128)} %add.79) | copy-start | bytes 1540
  74.4 0.8 copy-start.1
  149.9 2.0 copy-start.6
  156.1 45.4 %all-to-all-start.2 = ((bf16[32,9,2,1536]{3,2,1,0:T(2,128)(2,1)}), bf16[32,9,2,1536]{3,2,1,0:T(2,128)(2,1)}, u32[]{:S(2)}, u32[]{:S(2)}) async-start(bf16[32,9,2,1536]{3,2,1,0:T(2,128)(2,1)} %copy.110), calls=%async_computation.2 | async-start | bytes 3538944 | tf_op jit(solution)/shard_map/all_to_all | solution.py:188
  161.5 56.3 %reduce-scatter.2.cloned.1.call-start = ((), (), s32[]{:S(2)}) async-start(), calls=%async_computation.4 | async-start | bytes 1179648 | tf_op jit(solution)/shard_map/reduce_scatter | solution.py:196
Sparse Core Ops, SparseCore 0:
  204.5 13.2 reduce-scatter.1

commit v6 on v5

--- a/solution.py
+++ b/solution.py
@@ -113,6 +113,35 @@
     score_scale = HD ** (-0.5)
     heads = KVH * GROUP
 
+    top_count = routes.shape[2]
+    core_size = lax.axis_size("core")
+    core_pos = lax.axis_index("core")
+    expert_total = w_gate_up.shape[0] * lax.axis_size(EXP_AXES)
+    capacity = min(tok_count, 3 * tok_count * top_count // (2 * expert_total))
+    packed = jnp.concatenate(
+        [
+            routes[0].astype(jnp.bfloat16),
+            route_w[0],
+            jnp.zeros((tok_count, HD - 2 * top_count), jnp.bfloat16),
+        ],
+        -1,
+    )
+    both = lax.all_gather(packed, "core", axis=0, tiled=True)
+    routes_both = both[:, :top_count].astype(jnp.int32)
+    weights_both = both[:, top_count : 2 * top_count]
+    expert_ids = routes_both.reshape(core_size, tok_count * top_count)
+    pairs = expert_ids[:, :, None] == expert_ids[:, None, :]
+    earlier = jnp.arange(tok_count * top_count)
+    earlier = earlier[None, :] < earlier[:, None]
+    slot_index = jnp.sum((pairs & earlier[None]).astype(jnp.int32), -1)
+    block_rows = core_size * capacity
+    source_core = jnp.arange(core_size)[:, None]
+    dest = jnp.where(
+        expert_ids % core_size == core_pos,
+        ((expert_ids // core_size) * capacity + slot_index) * core_size + source_core,
+        -1,
+    ).reshape(core_size * tok_count, top_count)
+
     all_queries = lax.all_gather(queries[0], "ctx", axis=0, tiled=True)
     scal = jnp.stack([ctx_pos, length]).astype(jnp.int32)
     part = partial_attention(scal, all_queries, cache_kv[0], new_kv[0])
@@ -139,35 +168,7 @@
         widened * lax.rsqrt(jnp.mean(widened * widened, -1, keepdims=True) + 1e-06) * norm_gain
     ).astype(jnp.bfloat16)
 
-    top_count = routes.shape[2]
-    core_size = lax.axis_size("core")
-    core_pos = lax.axis_index("core")
-    expert_total = w_gate_up.shape[0] * lax.axis_size(EXP_AXES)
-    capacity = min(tok_count, 3 * tok_count * top_count // (2 * expert_total))
-    packed = jnp.concatenate(
-        [
-            normed,
-            routes[0].astype(jnp.bfloat16),
-            route_w[0],
-            jnp.zeros((tok_count, HD - 2 * top_count), jnp.bfloat16),
-        ],
-        -1,
-    )
-    both = lax.all_gather(packed, "core", axis=0, tiled=True)
-    normed_both = both[:, :D]
-    routes_both = both[:, D : D + top_count].astype(jnp.int32)
-    weights_both = both[:, D + top_count : D + 2 * top_count]
-    expert_ids = routes_both.reshape(core_size, tok_count * top_count)
-    one_hot = (expert_ids[..., None] == jnp.arange(expert_total)).astype(jnp.int32)
-    before = jnp.cumsum(one_hot, 1) - one_hot
-    slot_index = jnp.sum(before * one_hot, -1)
-    block_rows = core_size * capacity
-    source_core = jnp.arange(core_size)[:, None]
-    dest = jnp.where(
-        expert_ids % core_size == core_pos,
-        ((expert_ids // core_size) * capacity + slot_index) * core_size + source_core,
-        -1,
-    ).reshape(core_size * tok_count, top_count)
+    normed_both = lax.all_gather(normed, "core", axis=0, tiled=True)
     chip_count = expert_total // core_size
     slot_ids = jnp.arange(chip_count * block_rows)
     hits = dest[None, :, :] == slot_ids[:, None, None]
@@ -193,7 +194,9 @@
         -1,
     ).reshape(-1, *slot_shape)
     partial = jnp.einsum("tjsc,jscd->td", combine, returned, preferred_element_type=jnp.float32)
-    blended = lax.psum_scatter(partial, "core", scatter_dimension=0, tiled=True)
+    mine = lax.dynamic_slice_in_dim(partial, core_pos * tok_count, tok_count, 0)
+    theirs = lax.dynamic_slice_in_dim(partial, (1 - core_pos) * tok_count, tok_count, 0)
+    blended = mine + lax.ppermute(theirs, "core", [(0, 1), (1, 0)])
     return (widened + blended).astype(jnp.bfloat16)[None]
 
 

time: 228 us -> 184 us (0.81)
  waiting for transfers between devices: 59.1 us -> 40.5 us
  between operations: 14.3 us -> 1.01 us
  local copies, waits for them, and re-layouts: 25 us -> 15.6 us
  other arithmetic: 16.9 us -> 8.09 us
  blocking collectives: 75.2 us -> 80.2 us
  starting transfers between devices: 9.68 us -> 14 us
    reduce_scatter x1 -> x0, waiting for transfers between devices: 13.4 us -> none  [local(): blended = lax.psum_scatter(partial, 'core', scatter_dimension=0, tiled=True)]
    all_to_all x1, waiting for transfers between devices: 7.5 us -> 0.52 us  [local(): lax.all_to_all(part.reshape(n_ctx, tok_count, part.shape[1]), 'ctx', spli...]
    all_gather x0 -> x1, blocking collectives: none -> 6.73 us  [local(): normed_both = lax.all_gather(normed, 'core', axis=0, tiled=True)]
    another operation x2 -> x0, other arithmetic: 4.38 us -> none
    ppermute x0 -> x1, starting transfers between devices: none -> 4.21 us  [local(): blended = mine + lax.ppermute(theirs, 'core', [(0, 1), (1, 0)])]
    slice x3 -> x1, local copies, waits for them, and re-layouts: 3.58 us -> 0.82 us  [local(): weights_both = both[:, top_count:2 * top_count]]
  transfers between devices with their start and end apart: 3 -> 3, of which waited for: 3 -> 3; matrix products, arithmetic and copies ran while one was open for 1% -> 3% of each run, Pallas kernels for 0% -> 0%
where the time goes in v6:
time: 184 us
  blocking collectives  80.2 us (44%)
  waiting for transfers between devices  40.5 us (22%)
  local copies, waits for them, and re-layouts  15.6 us (8%)
  Pallas kernels  14.9 us (8%)
  starting transfers between devices  14 us (8%)
  matrix products  9.23 us (5%)
  other arithmetic  8.09 us (4%)
    all_to_all x1, blocking collectives, local(): lax.all_to_all(outgoing, CHIP_AXES, split_axis=0, concat_axis=0, tiled=True)  53.9 us
    all_to_all x1, waiting for transfers between devices, local(): lax.all_to_all(result, CHIP_AXES, split_axis=0, concat_axis=0, tiled=True)  38.3 us
    pallas_call x1, Pallas kernels, partial_attention(): pl.pallas_call(attend_kernel, out_shape=jax.ShapeDtypeStruct((n_q, width)...  14.9 us
    all_gather x1, blocking collectives, local(): all_queries = lax.all_gather(queries[0], 'ctx', axis=0, tiled=True)  14.2 us
    all_gather x1, blocking collectives, local(): normed_both = lax.all_gather(normed, 'core', axis=0, tiled=True)  6.73 us
    all_to_all x1, starting transfers between devices, local(): lax.all_to_all(result, CHIP_AXES, split_axis=0, concat_axis=0, tiled=True)  5.43 us
    all_gather x1, blocking collectives, local(): both = lax.all_gather(packed, 'core', axis=0, tiled=True)  5.34 us
    mul x2, local copies, waits for them, and re-layouts, local(): total_acc = jnp.sum(rescale[..., None] * got_acc, 0)  4.55 us
  transfers between devices with their start and end apart: 3, of which 3 were waited for; matrix products, arithmetic and copies ran while one was open for 3% of the time, Pallas kernels for 0%

profile of v6, /device:TPU:1, one launch (start us, length us, event | category | flops | bytes accessed | tf_op | source)
XLA Modules:
  0.0 183.6 jit_solution(12668547451770768347)
XLA Ops:
  0.8 14.2 %all-gather = bf16[1,256,1536]{2,1,0:T(8,128)(2,1)} all-gather(bf16[1,64,1536]{2,1,0:T(8,128)(2,1)} %param.12), channel_id=2, replica_groups=mesh['ctx'=4,'z'=8,'x'=4,'core'=2] {'ctx'}, dimensions={1}, use_global_device_ids=true | all-gather | bytes 983040 | tf_op jit(solution)/shard_map/all_gather | solution.py:145
  15.6 14.9 %shard_map.109 = bf16[256,1664]{1,0:T(8,128)(2,1)} custom-call(s32[2]{0:T(128)} %pad_add_fusion.scal_ref, bf16[256,1536]{1,0:T(8,128)(2,1)} %bitcast.54, bf16[1024,1024]{1,0:T(8,128)(2,1)} %bitcast.59, bf16[1024,1024]{1,0:T(8,128)(2,1)} %bitcast.60, bf16[64,1024]{1,0:T(8,128)(2,1)} %bitcast.61, bf16[64,1024]{1,0:T(8,128)(2,1)} %bitcast.62), custom_call_target="tpu_custom_call" | custom-call | flops 1711276032 | bytes 3866624 | tf_op jit(solution)/shard_map/pallas_call | solution.py:72
  30.5 4.3 %all-to-all-start = ((bf16[4,64,1664]{2,1,0:T(8,128)(2,1)}), bf16[4,64,1664]{2,1,0:T(8,128)(2,1)}, u32[]{:S(2)}, u32[]{:S(2)}) async-start(bf16[4,64,1664]{2,1,0:T(8,128)(2,1)} %bitcast.53), calls=%async_computation | async-start | bytes 1703936 | tf_op jit(solution)/shard_map/all_to_all | solution.py:148
  35.3 5.3 %all_gather.10 = bf16[128,128]{1,0:T(8,128)(2,1)S(1)} all-gather(bf16[64,128]{1,0:T(8,128)(2,1)S(1)} %maximum_maximum_fusion), channel_id=1, replica_groups=mesh['ctx'=4,'z'=8,'x'=4,'core'=2] {'core'}, dimensions={0}, use_global_device_ids=true | all-gather | bytes 49152 | tf_op jit(solution)/shard_map/all_gather | solution.py:129
  45.0 2.0 %mul.60 = f32[4,64,12,128]{3,2,1,0:T(8,128)} broadcast(f32[4,64,12]{2,1,0:T(8,128)S(1)} %copy.79), dimensions={0,1,2} | broadcast | bytes 1585152 | tf_op jit(solution)/shard_map/mul | solution.py:159
  47.0 2.6 %mul.61 = f32[4,64,1536]{2,1,0:T(8,128)} reshape(f32[4,64,12,128]{3,2,1,0:T(8,128)} %mul.60) | data formatting | bytes 3145728 | tf_op jit(solution)/shard_map/mul | solution.py:159
  49.6 1.8 %multiply_reduce_fusion = f32[64,1536]{1,0:T(8,128)S(1)} fusion(f32[4,64,1536]{2,1,0:T(8,128)} %mul.61, bf16[4,64,1664]{2,1,0:T(8,128)(2,1)} %all-to-all-done), kind=kLoop, calls=%fused_computation.15 | loop fusion | flops 1081344 | bytes 2752512 | tf_op jit(solution)/shard_map/reduce_sum | solution.py:159
  51.4 1.2 copy.99
  52.6 1.2 fusion.11
  53.8 3.5 %multiply_reduce_fusion.1 = (f32[64]{0:T(128)S(1)}, f32[64,1536]{1,0:T(8,128)S(1)}) fusion(bf16[64,1536]{0,1:T(8,128)(2,1)S(1)} %fusion.11, bf16[1536,1536]{1,0:T(8,128)(2,1)} %param.16, bf16[1,64,1536]{2,1,0:T(8,128)(2,1)} %param.11), kind=kOutput, calls=%fused_computation.27 | convolution fusion | flops 302579648 | bytes 5505280 | tf_op jit(solution)/shard_map/dot_general | solution.py:164
  57.4 6.7 %all_gather.11 = bf16[128,1536]{1,0:T(8,128)(2,1)S(1)} all-gather(bf16[64,1536]{1,0:T(8,128)(2,1)S(1)} %multiply_convert_fusion), channel_id=1, replica_groups=mesh['ctx'=4,'z'=8,'x'=4,'core'=2] {'core'}, dimensions={0}, use_global_device_ids=true | all-gather | bytes 589824 | tf_op jit(solution)/shard_map/all_gather | solution.py:171
  64.7 1.8 copy.89
  66.6 53.9 %all_to_all.15 = bf16[32,9,2,1536]{3,2,1,0:T(2,128)(2,1)S(1)} all-to-all(bf16[32,9,2,1536]{3,2,1,0:T(2,128)(2,1)S(1)} %copy.89), channel_id=1, replica_groups=mesh['ctx'=4,'z'=8,'x'=4,'core'=2] {'z','x'}, dimensions={0} | all-to-all | bytes 3538944 | tf_op jit(solution)/shard_map/all_to_all | solution.py:180
  120.5 2.0 %fusion = f32[32,9,2,1024]{3,0,2,1:T(8,128)S(1)} fusion(bf16[1,1536,1024]{2,1,0:T(8,128)(2,1)S(1)} %copy-done, bf16[32,9,2,1536]{3,2,1,0:T(2,128)(2,1)S(1)} %all_to_all.15), kind=kOutput, calls=%fused_computation | convolution fusion | flops 1811939328 | bytes 7274496 | tf_op jit(solution)/shard_map/jscd,df->jscf/dot_general | solution.py:182
  122.5 1.1 convolution_convert_fusion.1
  123.6 3.0 %copy.92 = bf16[32,9,2,1536]{3,2,1,0:T(2,128)(2,1)} copy(bf16[32,9,2,1536]{3,0,1,2:T(8,128)(2,1)S(1)} %convolution_convert_fusion.1) | data formatting | bytes 3538944 | tf_op jit(solution)/shard_map/convert_element_type | solution.py:188
  126.6 5.4 %all-to-all-start.2 = ((bf16[32,9,2,1536]{3,2,1,0:T(2,128)(2,1)}), bf16[32,9,2,1536]{3,2,1,0:T(2,128)(2,1)}, u32[]{:S(2)}, u32[]{:S(2)}) async-start(bf16[32,9,2,1536]{3,2,1,0:T(2,128)(2,1)} %copy.92), calls=%async_computation.2 | async-start | bytes 3538944 | tf_op jit(solution)/shard_map/all_to_all | solution.py:189
  132.9 0.9 fusion.10
  133.8 38.3 %all-to-all-done.2 = bf16[32,9,2,1536]{3,2,1,0:T(2,128)(2,1)} async-done(((bf16[32,9,2,1536]{3,2,1,0:T(2,128)(2,1)}), bf16[32,9,2,1536]{3,2,1,0:T(2,128)(2,1)}, u32[]{:S(2)}, u32[]{:S(2)}) %all-to-all-start.2) | async-done | bytes 1769504 | tf_op jit(solution)/shard_map/all_to_all | solution.py:189
  172.1 2.1 %convolution_bitcast_fusion = f32[128,1536]{1,0:T(8,128)S(1)} fusion(bf16[32,9,2,1536]{3,2,1,0:T(2,128)(2,1)} %all-to-all-done.2, bf16[128,32,9,2]{0,3,2,1:T(2,128)(2,1)} %bitcast.57), kind=kOutput, calls=%fused_computation.4 | convolution fusion | flops 226492416 | bytes 2703360 | tf_op jit(solution)/shard_map/tjsc,jscd->td/dot_general | solution.py:196
  174.2 0.9 copy-done.1
  175.8 4.2 %collective-permute-start = (f32[64,1536]{1,0:T(8,128)}, f32[64,1536]{1,0:T(8,128)}, u32[]{:S(2)}, u32[]{:S(2)}) collective-permute-start(f32[64,1536]{1,0:T(8,128)} %constant_dynamic-slice_fusion), channel_id=1, source_target_pairs={{0,1},{1,0},{2,3},{3,2},{4,5},{5,4},{6,7},{7,6},{8,9},{9,8},{10,11... | collective-permute-start | bytes 1179656 | tf_op jit(solution)/shard_map/ppermute | solution.py:199
  180.0 1.7 collective-permute-done
  181.7 1.8 %fusion.15 = bf16[1,64,1536]{2,1,0:T(8,128)(2,1)} fusion(f32[64,1536]{1,0:T(8,128)S(1)} %get-tuple-element.10, f32[64,1536]{1,0:T(8,128)} %collective-permute-done, f32[128,1536]{1,0:T(8,128)} %copy-done.1, s32[]{:T(128)S(6)} %select_n.36), kind=kLoop, calls=%fused_computation.29 | loop fusion | flops 294912 | bytes 1376260 | tf_op jit(solution)/shard_map/broadcast_in_dim | solution.py:200
  (43 shorter events, 7.6 us)
Async XLA Ops:
  0.0 120.5 %copy-start = (bf16[1,1536,1024]{2,1,0:T(8,128)(2,1)S(1)}, bf16[1,1536,1024]{2,1,0:T(8,128)(2,1)}, u32[]{:S(2)}) copy-start(bf16[1,1536,1024]{2,1,0:T(8,128)(2,1)} %param.20) | copy-start | bytes 9437188
  15.6 19.3 %copy-start.4 = (s32[1,64,6]{1,0,2:T(1,128)S(1)}, s32[1,64,6]{1,0,2:T(1,128)}, u32[]{:S(2)}) copy-start(s32[1,64,6]{1,0,2:T(1,128)} %param.18) | copy-start | bytes 4612
  30.5 4.5 %copy-start.5 = (bf16[1,64,6]{1,2,0:T(8,128)(2,1)S(1)}, bf16[1,64,6]{1,2,0:T(8,128)(2,1)}, u32[]{:S(2)}) copy-start(bf16[1,64,6]{1,2,0:T(8,128)(2,1)} %param.19) | copy-start | bytes 2308
  30.5 13.3 %all-to-all-start = ((bf16[4,64,1664]{2,1,0:T(8,128)(2,1)}), bf16[4,64,1664]{2,1,0:T(8,128)(2,1)}, u32[]{:S(2)}, u32[]{:S(2)}) async-start(bf16[4,64,1664]{2,1,0:T(8,128)(2,1)} %bitcast.53), calls=%async_computation | async-start | bytes 1703936 | tf_op jit(solution)/shard_map/all_to_all | solution.py:148
  53.8 3.5 %copy-start.3 = (f32[1536]{0:T(1024)S(1)}, f32[1536]{0:T(1024)}, u32[]{:S(2)}) copy-start(f32[1536]{0:T(1024)} %param.17) | copy-start | bytes 18436
  53.8 10.3 %copy-start.2 = (pred[32,9,2,128]{3,2,1,0:T(4,128)(4,1)S(1)}, pred[32,9,2,128]{3,2,1,0:T(4,128)(4,1)}, u32[]{:S(2)}) copy-start(pred[32,9,2,128]{3,2,1,0:T(4,128)(4,1)} %reshape.109) | copy-start | bytes 221188
  120.5 2.0 %copy-start.6 = (bf16[1,512,1536]{2,1,0:T(8,128)(2,1)S(1)}, bf16[1,512,1536]{2,1,0:T(8,128)(2,1)}, u32[]{:S(2)}) copy-start(bf16[1,512,1536]{2,1,0:T(8,128)(2,1)} %param.21) | copy-start | bytes 4718596
  126.6 45.4 %all-to-all-start.2 = ((bf16[32,9,2,1536]{3,2,1,0:T(2,128)(2,1)}), bf16[32,9,2,1536]{3,2,1,0:T(2,128)(2,1)}, u32[]{:S(2)}, u32[]{:S(2)}) async-start(bf16[32,9,2,1536]{3,2,1,0:T(2,128)(2,1)} %copy.92), calls=%async_computation.2 | async-start | bytes 3538944 | tf_op jit(solution)/shard_map/all_to_all | solution.py:189
  174.1 0.9 copy-start.1
  175.8 5.9 %collective-permute-start = (f32[64,1536]{1,0:T(8,128)}, f32[64,1536]{1,0:T(8,128)}, u32[]{:S(2)}, u32[]{:S(2)}) collective-permute-start(f32[64,1536]{1,0:T(8,128)} %constant_dynamic-slice_fusion), channel_id=1, source_target_pairs={{0,1},{1,0},{2,3},{3,2},{4,5},{5,4},{6,7},{7,6},{8,9},{9,8},{10,11... | collective-permute-start | bytes 1179656 | tf_op jit(solution)/shard_map/ppermute | solution.py:199

commit v7 on v6

--- a/solution.py
+++ b/solution.py
@@ -86,6 +86,55 @@
         ),
         cost_estimate=cost,
     )(scal, all_queries, cache_rows, cache_rows, new_rows, new_rows)
+
+
+def combine_kernel(got_ref, res_ref, w_ref, gain_ref, mixed_ref, normed_ref):
+    heads = KVH * GROUP
+    n_src = got_ref.shape[0]
+    base = heads * HD
+    stats = [got_ref[j, :, base : base + HD].astype(jnp.float32) for j in range(n_src)]
+    tops = [st + pltpu.roll(st, HD - heads, 1) for st in stats]
+    sums = [pltpu.roll(st, HD - 2 * heads, 1) + pltpu.roll(st, HD - 3 * heads, 1) for st in stats]
+    top = tops[0]
+    for t in tops[1:]:
+        top = jnp.maximum(top, t)
+    weights = [jnp.exp(t - top) for t in tops]
+    total = weights[0] * sums[0]
+    for w, s in zip(weights[1:], sums[1:]):
+        total = total + w * s
+    scales = [w / total for w in weights]
+    cols = []
+    for h in range(heads):
+        col = scales[0][:, h : h + 1] * got_ref[0, :, h * HD : (h + 1) * HD].astype(jnp.float32)
+        for j in range(1, n_src):
+            col = col + scales[j][:, h : h + 1] * got_ref[j, :, h * HD : (h + 1) * HD].astype(
+                jnp.float32
+            )
+        cols.append(col.astype(jnp.bfloat16))
+    attended = jnp.concatenate(cols, 1)
+    mixed = (
+        res_ref[...].astype(jnp.float32)
+        + jnp.dot(attended, w_ref[...], preferred_element_type=jnp.float32)
+    ).astype(jnp.bfloat16)
+    mixed_ref[...] = mixed
+    wide = mixed.astype(jnp.float32)
+    normed = wide * lax.rsqrt(jnp.mean(wide * wide, -1, keepdims=True) + 1e-06) * gain_ref[...]
+    normed_ref[...] = normed.astype(jnp.bfloat16)
+
+
+def combine_and_norm(got, residual, out_proj, norm_gain):
+    rows, width = residual.shape
+    out = jax.ShapeDtypeStruct((rows, width), jnp.bfloat16)
+    cost = pl.CostEstimate(
+        flops=2 * rows * out_proj.shape[0] * width,
+        transcendentals=0,
+        bytes_accessed=2 * (got.size + out_proj.size + 3 * residual.size),
+    )
+    return pl.pallas_call(
+        combine_kernel,
+        out_shape=(out, out),
+        cost_estimate=cost,
+    )(got, residual, out_proj, norm_gain.reshape(1, -1))
 
 
 EXP_AXES = ("z", "x", "core")
@@ -148,25 +197,8 @@
     got = lax.all_to_all(
         part.reshape(n_ctx, tok_count, part.shape[1]), "ctx", split_axis=0, concat_axis=0, tiled=True
     )
-    got_acc = got[..., : heads * HD].astype(jnp.float32).reshape(n_ctx, tok_count, heads, HD)
-    got_stats = got[..., heads * HD : heads * HD + 4 * heads].astype(jnp.float32)
-    got_stats = got_stats.reshape(n_ctx, tok_count, 4, heads)
-    got_max = got_stats[:, :, 0] + got_stats[:, :, 1]
-    got_sum = got_stats[:, :, 2] + got_stats[:, :, 3]
-    top_max = jnp.max(got_max, 0)
-    rescale = jnp.exp(got_max - top_max[None])
-    total_sum = jnp.sum(rescale * got_sum, 0)
-    total_acc = jnp.sum(rescale[..., None] * got_acc, 0)
-    attended = (total_acc / total_sum[..., None]).reshape(tok_count, heads * HD)
-    attended = attended.astype(jnp.bfloat16)
-    mixed = (
-        residual_in[0].astype(jnp.float32)
-        + jnp.dot(attended, out_proj, preferred_element_type=jnp.float32)
-    ).astype(jnp.bfloat16)
+    mixed, normed = combine_and_norm(got, residual_in[0], out_proj, norm_gain)
     widened = mixed.astype(jnp.float32)
-    normed = (
-        widened * lax.rsqrt(jnp.mean(widened * widened, -1, keepdims=True) + 1e-06) * norm_gain
-    ).astype(jnp.bfloat16)
 
     normed_both = lax.all_gather(normed, "core", axis=0, tiled=True)
     chip_count = expert_total // core_size

time: 184 us -> 175 us (0.951)
  local copies, waits for them, and re-layouts: 15.6 us -> 7.99 us
  Pallas kernels: 14.9 us -> 19.9 us
  other arithmetic: 8.09 us -> 3.64 us
  matrix products: 9.23 us -> 5.67 us
  waiting for transfers between devices: 40.5 us -> 42.4 us
    pallas_call x0 -> x1, Pallas kernels: none -> 4.93 us  [combine_and_norm(): pl.pallas_call(combine_kernel, out_shape=(out, out), cost_estimate=cost)]
    mul x2 -> x0, local copies, waits for them, and re-layouts: 4.55 us -> none  [local(): total_acc = jnp.sum(rescale[..., None] * got_acc, 0)]
    dot_general x1 -> x0, matrix products: 3.46 us -> none  [local(): jnp.dot(attended, out_proj, preferred_element_type=jnp.float32)]
    reduce_sum x2 -> x0, other arithmetic: 1.88 us -> none  [the longest x1 1.84 us: local(): total_acc = jnp.sum(rescale[..., None] * got_acc, 0)]
  transfers between devices with their start and end apart: 3 -> 3, of which waited for: 3 -> 3; matrix products, arithmetic and copies ran while one was open for 3% -> 2% of each run, Pallas kernels for 0% -> 0%
where the time goes in v7:
time: 175 us
  blocking collectives  80.4 us (46%)
  waiting for transfers between devices  42.4 us (24%)
  Pallas kernels  19.9 us (11%)
  starting transfers between devices  14 us (8%)
  local copies, waits for them, and re-layouts  7.99 us (5%)
  matrix products  5.67 us (3%)
  other arithmetic  3.64 us (2%)
    all_to_all x1, blocking collectives, local(): lax.all_to_all(outgoing, CHIP_AXES, split_axis=0, concat_axis=0, tiled=True)  53.9 us
    all_to_all x1, waiting for transfers between devices, local(): lax.all_to_all(result, CHIP_AXES, split_axis=0, concat_axis=0, tiled=True)  39.7 us
    pallas_call x1, Pallas kernels, partial_attention(): pl.pallas_call(attend_kernel, out_shape=jax.ShapeDtypeStruct((n_q, width)...  14.9 us
    all_gather x1, blocking collectives, local(): all_queries = lax.all_gather(queries[0], 'ctx', axis=0, tiled=True)  14.2 us
    all_gather x1, blocking collectives, local(): normed_both = lax.all_gather(normed, 'core', axis=0, tiled=True)  6.93 us
    all_to_all x1, starting transfers between devices, local(): lax.all_to_all(result, CHIP_AXES, split_axis=0, concat_axis=0, tiled=True)  5.43 us
    all_gather x1, blocking collectives, local(): both = lax.all_gather(packed, 'core', axis=0, tiled=True)  5.34 us
    pallas_call x1, Pallas kernels, combine_and_norm(): pl.pallas_call(combine_kernel, out_shape=(out, out), cost_estimate=cost)  4.93 us
  transfers between devices with their start and end apart: 3, of which 3 were waited for; matrix products, arithmetic and copies ran while one was open for 2% of the time, Pallas kernels for 0%

profile of v7, /device:TPU:1, one launch (start us, length us, event | category | flops | bytes accessed | tf_op | source)
XLA Modules:
  0.0 175.0 jit_solution(805979609242484489)
XLA Ops:
  0.8 14.2 %all-gather = bf16[1,256,1536]{2,1,0:T(8,128)(2,1)} all-gather(bf16[1,64,1536]{2,1,0:T(8,128)(2,1)} %param.12), channel_id=2, replica_groups=mesh['ctx'=4,'z'=8,'x'=4,'core'=2] {'ctx'}, dimensions={1}, use_global_device_ids=true | all-gather | bytes 983040 | tf_op jit(solution)/shard_map/all_gather | solution.py:194
  15.0 0.7 pad_add_fusion.scal_ref
  15.7 14.9 %shard_map.109 = bf16[256,1664]{1,0:T(8,128)(2,1)} custom-call(s32[2]{0:T(128)} %pad_add_fusion.scal_ref, bf16[256,1536]{1,0:T(8,128)(2,1)} %bitcast.34, bf16[1024,1024]{1,0:T(8,128)(2,1)} %bitcast.38, bf16[1024,1024]{1,0:T(8,128)(2,1)} %bitcast.39, bf16[64,1024]{1,0:T(8,128)(2,1)} %bitcast.40, bf16[64,1024]{1,0:T(8,128)(2,1)} %bitcast.41), custom_call_target="tpu_custom_call" | custom-call | flops 1711276032 | bytes 3866624 | tf_op jit(solution)/shard_map/pallas_call | solution.py:72
  30.6 4.3 %all-to-all-start = ((bf16[4,64,1664]{2,1,0:T(8,128)(2,1)}), bf16[4,64,1664]{2,1,0:T(8,128)(2,1)}, u32[]{:S(2)}, u32[]{:S(2)}) async-start(bf16[4,64,1664]{2,1,0:T(8,128)(2,1)} %bitcast.33), calls=%async_computation | async-start | bytes 1703936 | tf_op jit(solution)/shard_map/all_to_all | solution.py:197
  35.4 5.3 %all_gather.10 = bf16[128,128]{1,0:T(8,128)(2,1)S(1)} all-gather(bf16[64,128]{1,0:T(8,128)(2,1)S(1)} %maximum_maximum_fusion), channel_id=1, replica_groups=mesh['ctx'=4,'z'=8,'x'=4,'core'=2] {'core'}, dimensions={0}, use_global_device_ids=true | all-gather | bytes 49152 | tf_op jit(solution)/shard_map/all_gather | solution.py:178
  41.0 0.4 convert_reduce_fusion
  42.2 0.6 reshape.70.gain_ref
  42.8 1.2 all-to-all-done.got_ref
  44.0 4.9 %shard_map.110 = (bf16[64,1536]{1,0:T(8,128)(2,1)}, bf16[64,1536]{1,0:T(8,128)(2,1)}) custom-call(bf16[4,64,1664]{2,1,0:T(8,128)(2,1)} %all-to-all-done.got_ref, bf16[64,1536]{1,0:T(8,128)(2,1)} %bitcast.36, bf16[1536,1536]{1,0:T(8,128)(2,1)} %w_ref.1, f32[1,1536]{1,0:T(1,128)} %reshape.70.gain_ref), custom_call_target="tpu_custom_call" | custom-call | flops 301989888 | bytes 6160384 | tf_op jit(solution)/shard_map/pallas_call | solution.py:133
  48.9 6.9 %all_gather.11 = bf16[128,1536]{1,0:T(8,128)(2,1)S(1)} all-gather(bf16[64,1536]{1,0:T(8,128)(2,1)} %get-tuple-element.8), channel_id=1, replica_groups=mesh['ctx'=4,'z'=8,'x'=4,'core'=2] {'core'}, dimensions={0}, use_global_device_ids=true | all-gather | bytes 589824 | tf_op jit(solution)/shard_map/all_gather | solution.py:203
  55.8 0.6 convolution_convert_fusion
  56.4 1.8 %copy.41 = bf16[32,9,2,1536]{3,2,1,0:T(2,128)(2,1)S(1)} copy(bf16[32,9,2,1536]{3,0,2,1:T(8,128)(2,1)S(1)} %convolution_convert_fusion) | data formatting | bytes 3538944 | tf_op jit(solution)/shard_map/convert_element_type | solution.py:211
  58.3 53.9 %all_to_all.15 = bf16[32,9,2,1536]{3,2,1,0:T(2,128)(2,1)S(1)} all-to-all(bf16[32,9,2,1536]{3,2,1,0:T(2,128)(2,1)S(1)} %copy.41), channel_id=1, replica_groups=mesh['ctx'=4,'z'=8,'x'=4,'core'=2] {'z','x'}, dimensions={0} | all-to-all | bytes 3538944 | tf_op jit(solution)/shard_map/all_to_all | solution.py:212
  112.2 2.0 %fusion = f32[32,9,2,1024]{3,0,2,1:T(8,128)S(1)} fusion(bf16[1,1536,1024]{2,1,0:T(8,128)(2,1)S(1)} %copy-done, bf16[32,9,2,1536]{3,2,1,0:T(2,128)(2,1)S(1)} %all_to_all.15), kind=kOutput, calls=%fused_computation | convolution fusion | flops 1811939328 | bytes 7274496 | tf_op jit(solution)/shard_map/jscd,df->jscf/dot_general | solution.py:214
  114.2 1.1 convolution_convert_fusion.1
  115.3 3.0 %copy.44 = bf16[32,9,2,1536]{3,2,1,0:T(2,128)(2,1)} copy(bf16[32,9,2,1536]{3,0,1,2:T(8,128)(2,1)S(1)} %convolution_convert_fusion.1) | data formatting | bytes 3538944 | tf_op jit(solution)/shard_map/convert_element_type | solution.py:220
  118.3 5.4 %all-to-all-start.2 = ((bf16[32,9,2,1536]{3,2,1,0:T(2,128)(2,1)}), bf16[32,9,2,1536]{3,2,1,0:T(2,128)(2,1)}, u32[]{:S(2)}, u32[]{:S(2)}) async-start(bf16[32,9,2,1536]{3,2,1,0:T(2,128)(2,1)} %copy.44), calls=%async_computation.2 | async-start | bytes 3538944 | tf_op jit(solution)/shard_map/all_to_all | solution.py:221
  124.0 39.7 %all-to-all-done.2 = bf16[32,9,2,1536]{3,2,1,0:T(2,128)(2,1)} async-done(((bf16[32,9,2,1536]{3,2,1,0:T(2,128)(2,1)}), bf16[32,9,2,1536]{3,2,1,0:T(2,128)(2,1)}, u32[]{:S(2)}, u32[]{:S(2)}) %all-to-all-start.2) | async-done | bytes 1769504 | tf_op jit(solution)/shard_map/all_to_all | solution.py:221
  163.7 2.0 %convolution_bitcast_fusion = f32[128,1536]{1,0:T(8,128)S(1)} fusion(bf16[32,9,2,1536]{3,2,1,0:T(2,128)(2,1)} %all-to-all-done.2, bf16[128,32,9,2]{0,3,2,1:T(2,128)(2,1)S(1)} %bitcast.35), kind=kOutput, calls=%fused_computation.4 | convolution fusion | flops 226492416 | bytes 2703360 | tf_op jit(solution)/shard_map/tjsc,jscd->td/dot_general | solution.py:228
  165.7 0.9 copy-done.1
  166.6 0.8 constant_dynamic-slice_fusion
  167.4 4.2 %collective-permute-start = (f32[64,1536]{1,0:T(8,128)}, f32[64,1536]{1,0:T(8,128)S(1)}, u32[]{:S(2)}, u32[]{:S(2)}) collective-permute-start(f32[64,1536]{1,0:T(8,128)} %constant_dynamic-slice_fusion), channel_id=1, source_target_pairs={{0,1},{1,0},{2,3},{3,2},{4,5},{5,4},{6,7},{7,6},{8,9},{9,8},{10,11... | collective-permute-start | bytes 1179656 | tf_op jit(solution)/shard_map/ppermute | solution.py:231
  171.6 1.6 collective-permute-done
  173.2 1.8 %fusion.12 = bf16[1,64,1536]{2,1,0:T(8,128)(2,1)} fusion(f32[64,1536]{1,0:T(8,128)S(1)} %collective-permute-done, f32[128,1536]{1,0:T(8,128)} %copy-done.1, s32[]{:T(128)S(6)} %select_n.36, bf16[64,1536]{1,0:T(8,128)(2,1)} %get-tuple-element.7), kind=kLoop, calls=%fused_computation.21 | loop fusion | flops 393216 | bytes 1179652 | tf_op jit(solution)/shard_map/broadcast_in_dim | solution.py:232
  (29 shorter events, 1.7 us)
Async XLA Ops:
  0.0 112.2 %copy-start = (bf16[1,1536,1024]{2,1,0:T(8,128)(2,1)S(1)}, bf16[1,1536,1024]{2,1,0:T(8,128)(2,1)}, u32[]{:S(2)}) copy-start(bf16[1,1536,1024]{2,1,0:T(8,128)(2,1)} %param.20) | copy-start | bytes 9437188
  15.7 19.3 %copy-start.3 = (s32[1,64,6]{1,0,2:T(1,128)S(1)}, s32[1,64,6]{1,0,2:T(1,128)}, u32[]{:S(2)}) copy-start(s32[1,64,6]{1,0,2:T(1,128)} %param.18) | copy-start | bytes 4612
  30.6 4.5 %copy-start.4 = (bf16[1,64,6]{1,2,0:T(8,128)(2,1)S(1)}, bf16[1,64,6]{1,2,0:T(8,128)(2,1)}, u32[]{:S(2)}) copy-start(bf16[1,64,6]{1,2,0:T(8,128)(2,1)} %param.19) | copy-start | bytes 2308
  30.6 11.6 %copy-start.2 = (f32[1536]{0:T(1024)S(1)}, f32[1536]{0:T(1024)}, u32[]{:S(2)}) copy-start(f32[1536]{0:T(1024)} %param.17) | copy-start | bytes 18436
  30.6 13.3 %all-to-all-start = ((bf16[4,64,1664]{2,1,0:T(8,128)(2,1)}), bf16[4,64,1664]{2,1,0:T(8,128)(2,1)}, u32[]{:S(2)}, u32[]{:S(2)}) async-start(bf16[4,64,1664]{2,1,0:T(8,128)(2,1)} %bitcast.33), calls=%async_computation | async-start | bytes 1703936 | tf_op jit(solution)/shard_map/all_to_all | solution.py:197
  112.2 2.0 %copy-start.5 = (bf16[1,512,1536]{2,1,0:T(8,128)(2,1)S(1)}, bf16[1,512,1536]{2,1,0:T(8,128)(2,1)}, u32[]{:S(2)}) copy-start(bf16[1,512,1536]{2,1,0:T(8,128)(2,1)} %param.21) | copy-start | bytes 4718596
  118.3 45.4 %all-to-all-start.2 = ((bf16[32,9,2,1536]{3,2,1,0:T(2,128)(2,1)}), bf16[32,9,2,1536]{3,2,1,0:T(2,128)(2,1)}, u32[]{:S(2)}, u32[]{:S(2)}) async-start(bf16[32,9,2,1536]{3,2,1,0:T(2,128)(2,1)} %copy.44), calls=%async_computation.2 | async-start | bytes 3538944 | tf_op jit(solution)/shard_map/all_to_all | solution.py:221
  165.7 0.9 copy-start.1
  167.4 5.8 %collective-permute-start = (f32[64,1536]{1,0:T(8,128)}, f32[64,1536]{1,0:T(8,128)S(1)}, u32[]{:S(2)}, u32[]{:S(2)}) collective-permute-start(f32[64,1536]{1,0:T(8,128)} %constant_dynamic-slice_fusion), channel_id=1, source_target_pairs={{0,1},{1,0},{2,3},{3,2},{4,5},{5,4},{6,7},{7,6},{8,9},{9,8},{10,11... | collective-permute-start | bytes 1179656 | tf_op jit(solution)/shard_map/ppermute | solution.py:231

commit v8 on v7

--- a/solution.py
+++ b/solution.py
@@ -102,7 +102,9 @@
     total = weights[0] * sums[0]
     for w, s in zip(weights[1:], sums[1:]):
         total = total + w * s
-    scales = [w / total for w in weights]
+    inverse = 1.0 / total
+    inverse = inverse * (2.0 - total * inverse)
+    scales = [w * inverse for w in weights]
     cols = []
     for h in range(heads):
         col = scales[0][:, h : h + 1] * got_ref[0, :, h * HD : (h + 1) * HD].astype(jnp.float32)
@@ -118,7 +120,10 @@
     ).astype(jnp.bfloat16)
     mixed_ref[...] = mixed
     wide = mixed.astype(jnp.float32)
-    normed = wide * lax.rsqrt(jnp.mean(wide * wide, -1, keepdims=True) + 1e-06) * gain_ref[...]
+    square_mean = jnp.mean(wide * wide, -1, keepdims=True) + 1e-06
+    root = lax.rsqrt(square_mean)
+    root = root * (1.5 - 0.5 * square_mean * root * root)
+    normed = wide * root * gain_ref[...]
     normed_ref[...] = normed.astype(jnp.bfloat16)
 
 
@@ -224,11 +229,15 @@
             hits.transpose(1, 0, 2), weights_both[:, None, :], jnp.zeros((), weights_both.dtype)
         ),
         -1,
-    ).reshape(-1, *slot_shape)
-    partial = jnp.einsum("tjsc,jscd->td", combine, returned, preferred_element_type=jnp.float32)
-    mine = lax.dynamic_slice_in_dim(partial, core_pos * tok_count, tok_count, 0)
-    theirs = lax.dynamic_slice_in_dim(partial, (1 - core_pos) * tok_count, tok_count, 0)
-    blended = mine + lax.ppermute(theirs, "core", [(0, 1), (1, 0)])
+    ).reshape(core_size, tok_count, *slot_shape)
+    theirs = jnp.einsum(
+        "tjsc,jscd->td", combine[1 - core_pos], returned, preferred_element_type=jnp.float32
+    )
+    sent = lax.ppermute(theirs, "core", [(0, 1), (1, 0)])
+    mine = jnp.einsum(
+        "tjsc,jscd->td", combine[core_pos], returned, preferred_element_type=jnp.float32
+    )
+    blended = lax.optimization_barrier(mine) + sent
     return (widened + blended).astype(jnp.bfloat16)[None]
 
 

time: 175 us -> 173 us (0.989)
  waiting for transfers between devices: 42.4 us -> 37.7 us
  matrix products: 5.67 us -> 7.76 us
    all_to_all x1, waiting for transfers between devices: 39.7 us -> 36.5 us  [local(): lax.all_to_all(result, CHIP_AXES, split_axis=0, concat_axis=0, tiled=True)]
    dot_general x1 -> x2, matrix products: 1.97 us -> 4.05 us  [the longest x1 2.09 us: local(): jnp.einsum('tjsc,jscd->td', combine[1 - core_pos], returned, preferred_el...]
  transfers between devices with their start and end apart: 3 -> 3, of which waited for: 3 -> 2; matrix products, arithmetic and copies ran while one was open for 2% -> 4% of each run, Pallas kernels for 0% -> 0%
where the time goes in v8:
time: 173 us
  blocking collectives  80.4 us (46%)
  waiting for transfers between devices  37.7 us (22%)
  Pallas kernels  19.9 us (12%)
  starting transfers between devices  14.1 us (8%)
  local copies, waits for them, and re-layouts  8.81 us (5%)
  matrix products  7.76 us (4%)
  other arithmetic  3.15 us (2%)
    all_to_all x1, blocking collectives, local(): lax.all_to_all(outgoing, CHIP_AXES, split_axis=0, concat_axis=0, tiled=True)  53.9 us
    all_to_all x1, waiting for transfers between devices, local(): lax.all_to_all(result, CHIP_AXES, split_axis=0, concat_axis=0, tiled=True)  36.5 us
    pallas_call x1, Pallas kernels, partial_attention(): pl.pallas_call(attend_kernel, out_shape=jax.ShapeDtypeStruct((n_q, width)...  14.9 us
    all_gather x1, blocking collectives, local(): all_queries = lax.all_gather(queries[0], 'ctx', axis=0, tiled=True)  14.2 us
    all_gather x1, blocking collectives, local(): normed_both = lax.all_gather(normed, 'core', axis=0, tiled=True)  6.94 us
    all_to_all x1, starting transfers between devices, local(): lax.all_to_all(result, CHIP_AXES, split_axis=0, concat_axis=0, tiled=True)  5.42 us
    all_gather x1, blocking collectives, local(): both = lax.all_gather(packed, 'core', axis=0, tiled=True)  5.34 us
    pallas_call x1, Pallas kernels, combine_and_norm(): pl.pallas_call(combine_kernel, out_shape=(out, out), cost_estimate=cost)  4.93 us
  transfers between devices with their start and end apart: 3, of which 2 were waited for; matrix products, arithmetic and copies ran while one was open for 4% of the time, Pallas kernels for 0%

profile of v8, /device:TPU:1, one launch (start us, length us, event | category | flops | bytes accessed | tf_op | source)
XLA Modules:
  0.0 172.7 jit_solution(16556954554567995218)
XLA Ops:
  0.8 14.2 %all-gather = bf16[1,256,1536]{2,1,0:T(8,128)(2,1)} all-gather(bf16[1,64,1536]{2,1,0:T(8,128)(2,1)} %param.12), channel_id=2, replica_groups=mesh['ctx'=4,'z'=8,'x'=4,'core'=2] {'ctx'}, dimensions={1}, use_global_device_ids=true | all-gather | bytes 983040 | tf_op jit(solution)/shard_map/all_gather | solution.py:199
  15.0 0.6 pad_add_fusion.scal_ref
  15.6 14.9 %shard_map.109 = bf16[256,1664]{1,0:T(8,128)(2,1)} custom-call(s32[2]{0:T(128)} %pad_add_fusion.scal_ref, bf16[256,1536]{1,0:T(8,128)(2,1)} %bitcast.47, bf16[1024,1024]{1,0:T(8,128)(2,1)} %bitcast.50, bf16[1024,1024]{1,0:T(8,128)(2,1)} %bitcast.51, bf16[64,1024]{1,0:T(8,128)(2,1)} %bitcast.52, bf16[64,1024]{1,0:T(8,128)(2,1)} %bitcast.53), custom_call_target="tpu_custom_call" | custom-call | flops 1711276032 | bytes 3866624 | tf_op jit(solution)/shard_map/pallas_call | solution.py:72
  30.5 4.3 %all-to-all-start = ((bf16[4,64,1664]{2,1,0:T(8,128)(2,1)}), bf16[4,64,1664]{2,1,0:T(8,128)(2,1)}, u32[]{:S(2)}, u32[]{:S(2)}) async-start(bf16[4,64,1664]{2,1,0:T(8,128)(2,1)} %bitcast.46), calls=%async_computation | async-start | bytes 1703936 | tf_op jit(solution)/shard_map/all_to_all | solution.py:202
  35.3 5.3 %all_gather.10 = bf16[128,128]{1,0:T(8,128)(2,1)S(1)} all-gather(bf16[64,128]{1,0:T(8,128)(2,1)S(1)} %maximum_maximum_fusion), channel_id=1, replica_groups=mesh['ctx'=4,'z'=8,'x'=4,'core'=2] {'core'}, dimensions={0}, use_global_device_ids=true | all-gather | bytes 49152 | tf_op jit(solution)/shard_map/all_gather | solution.py:183
  40.7 0.6 reshape.70.gain_ref
  42.7 1.2 all-to-all-done.got_ref
  43.8 4.9 %shard_map.110 = (bf16[64,1536]{1,0:T(8,128)(2,1)}, bf16[64,1536]{1,0:T(8,128)(2,1)}) custom-call(bf16[4,64,1664]{2,1,0:T(8,128)(2,1)} %all-to-all-done.got_ref, bf16[64,1536]{1,0:T(8,128)(2,1)} %bitcast.48, bf16[1536,1536]{1,0:T(8,128)(2,1)} %w_ref.1, f32[1,1536]{1,0:T(1,128)} %reshape.70.gain_ref), custom_call_target="tpu_custom_call" | custom-call | flops 301989888 | bytes 6160384 | tf_op jit(solution)/shard_map/pallas_call | solution.py:138
  48.8 6.9 %all_gather.11 = bf16[128,1536]{1,0:T(8,128)(2,1)S(1)} all-gather(bf16[64,1536]{1,0:T(8,128)(2,1)} %get-tuple-element.8), channel_id=1, replica_groups=mesh['ctx'=4,'z'=8,'x'=4,'core'=2] {'core'}, dimensions={0}, use_global_device_ids=true | all-gather | bytes 589824 | tf_op jit(solution)/shard_map/all_gather | solution.py:208
  55.7 0.6 convolution_convert_fusion
  56.3 1.8 %copy.39 = bf16[32,9,2,1536]{3,2,1,0:T(2,128)(2,1)S(1)} copy(bf16[32,9,2,1536]{3,0,2,1:T(8,128)(2,1)S(1)} %convolution_convert_fusion) | data formatting | bytes 3538944 | tf_op jit(solution)/shard_map/convert_element_type | solution.py:216
  58.2 53.9 %all_to_all.15 = bf16[32,9,2,1536]{3,2,1,0:T(2,128)(2,1)S(1)} all-to-all(bf16[32,9,2,1536]{3,2,1,0:T(2,128)(2,1)S(1)} %copy.39), channel_id=1, replica_groups=mesh['ctx'=4,'z'=8,'x'=4,'core'=2] {'z','x'}, dimensions={0} | all-to-all | bytes 3538944 | tf_op jit(solution)/shard_map/all_to_all | solution.py:217
  112.1 2.0 %fusion = f32[32,9,2,1024]{3,0,2,1:T(8,128)S(1)} fusion(bf16[1,1536,1024]{2,1,0:T(8,128)(2,1)S(1)} %copy-done, bf16[32,9,2,1536]{3,2,1,0:T(2,128)(2,1)S(1)} %all_to_all.15), kind=kOutput, calls=%fused_computation | convolution fusion | flops 1811939328 | bytes 7274496 | tf_op jit(solution)/shard_map/jscd,df->jscf/dot_general | solution.py:219
  114.1 1.1 convolution_convert_fusion.1
  115.2 3.0 %copy.41 = bf16[32,9,2,1536]{3,2,1,0:T(2,128)(2,1)} copy(bf16[32,9,2,1536]{3,0,2,1:T(8,128)(2,1)S(1)} %convolution_convert_fusion.1) | data formatting | bytes 3538944 | tf_op jit(solution)/shard_map/convert_element_type | solution.py:225
  118.2 5.4 %all-to-all-start.2 = ((bf16[32,9,2,1536]{3,2,1,0:T(2,128)(2,1)}), bf16[32,9,2,1536]{3,2,1,0:T(2,128)(2,1)}, u32[]{:S(2)}, u32[]{:S(2)}) async-start(bf16[32,9,2,1536]{3,2,1,0:T(2,128)(2,1)} %copy.41), calls=%async_computation.2 | async-start | bytes 3538944 | tf_op jit(solution)/shard_map/all_to_all | solution.py:226
  123.7 0.9 fusion.9
  124.6 1.1 reshape.71
  125.6 1.4 constant_dynamic-slice_fusion
  127.1 36.5 %all-to-all-done.2 = bf16[32,9,2,1536]{3,2,1,0:T(2,128)(2,1)} async-done(((bf16[32,9,2,1536]{3,2,1,0:T(2,128)(2,1)}), bf16[32,9,2,1536]{3,2,1,0:T(2,128)(2,1)}, u32[]{:S(2)}, u32[]{:S(2)}) %all-to-all-start.2) | async-done | bytes 1769504 | tf_op jit(solution)/shard_map/all_to_all | solution.py:226
  163.6 2.1 %convolution_bitcast_fusion = f32[64,1536]{1,0:T(8,128)S(1)} fusion(bf16[32,9,2,1536]{3,2,1,0:T(2,128)(2,1)} %all-to-all-done.2, bf16[1,64,32,9,2]{1,0,4,3,2:T(2,128)(2,1)} %get-tuple-element.9), kind=kOutput, calls=%fused_computation.4 | convolution fusion | flops 113246208 | bytes 2236416 | tf_op jit(solution)/shard_map/tjsc,jscd->td/dot_general | solution.py:233
  165.7 4.3 %collective-permute-start = (f32[64,1536]{1,0:T(8,128)S(1)}, f32[64,1536]{1,0:T(8,128)S(1)}, u32[]{:S(2)}, u32[]{:S(2)}) collective-permute-start(f32[64,1536]{1,0:T(8,128)S(1)} %convolution_bitcast_fusion), channel_id=1, source_target_pairs={{0,1},{1,0},{2,3},{3,2},{4,5},{5,4},{6,7},{7,6},{8,9},{9,8},{10,11... | collective-permute-start | bytes 1179656 | tf_op jit(solution)/shard_map/ppermute | solution.py:236
  170.0 2.0 %convolution_bitcast_fusion.1 = f32[64,1536]{1,0:T(8,128)S(1)} fusion(bf16[32,9,2,1536]{3,2,1,0:T(2,128)(2,1)} %all-to-all-done.2, bf16[1,64,32,9,2]{1,0,4,3,2:T(2,128)(2,1)S(1)} %copy-done.1), kind=kOutput, calls=%fused_computation.5 | convolution fusion | flops 113246208 | bytes 2236416 | tf_op jit(solution)/shard_map/tjsc,jscd->td/dot_general | solution.py:237
  172.0 0.7 fusion.14
  (33 shorter events, 1.9 us)
Async XLA Ops:
  0.0 112.1 %copy-start = (bf16[1,1536,1024]{2,1,0:T(8,128)(2,1)S(1)}, bf16[1,1536,1024]{2,1,0:T(8,128)(2,1)}, u32[]{:S(2)}) copy-start(bf16[1,1536,1024]{2,1,0:T(8,128)(2,1)} %param.20) | copy-start | bytes 9437188
  15.6 19.3 %copy-start.5 = (bf16[1,64,6]{1,2,0:T(8,128)(2,1)S(1)}, bf16[1,64,6]{1,2,0:T(8,128)(2,1)}, u32[]{:S(2)}) copy-start(bf16[1,64,6]{1,2,0:T(8,128)(2,1)} %param.19) | copy-start | bytes 2308
  15.6 19.4 %copy-start.4 = (s32[1,64,6]{1,0,2:T(1,128)S(1)}, s32[1,64,6]{1,0,2:T(1,128)}, u32[]{:S(2)}) copy-start(s32[1,64,6]{1,0,2:T(1,128)} %param.18) | copy-start | bytes 4612
  30.5 10.2 %copy-start.3 = (f32[1536]{0:T(1024)S(1)}, f32[1536]{0:T(1024)}, u32[]{:S(2)}) copy-start(f32[1536]{0:T(1024)} %param.17) | copy-start | bytes 18436
  30.5 13.3 %all-to-all-start = ((bf16[4,64,1664]{2,1,0:T(8,128)(2,1)}), bf16[4,64,1664]{2,1,0:T(8,128)(2,1)}, u32[]{:S(2)}, u32[]{:S(2)}) async-start(bf16[4,64,1664]{2,1,0:T(8,128)(2,1)} %bitcast.46), calls=%async_computation | async-start | bytes 1703936 | tf_op jit(solution)/shard_map/all_to_all | solution.py:202
  112.1 2.0 %copy-start.6 = (bf16[1,512,1536]{2,1,0:T(8,128)(2,1)S(1)}, bf16[1,512,1536]{2,1,0:T(8,128)(2,1)}, u32[]{:S(2)}) copy-start(bf16[1,512,1536]{2,1,0:T(8,128)(2,1)} %param.21) | copy-start | bytes 4718596
  118.2 45.4 %all-to-all-start.2 = ((bf16[32,9,2,1536]{3,2,1,0:T(2,128)(2,1)}), bf16[32,9,2,1536]{3,2,1,0:T(2,128)(2,1)}, u32[]{:S(2)}, u32[]{:S(2)}) async-start(bf16[32,9,2,1536]{3,2,1,0:T(2,128)(2,1)} %copy.41), calls=%async_computation.2 | async-start | bytes 3538944 | tf_op jit(solution)/shard_map/all_to_all | solution.py:226
  127.1 43.0 %copy-start.1 = (bf16[1,64,32,9,2]{1,0,4,3,2:T(2,128)(2,1)S(1)}, bf16[1,64,32,9,2]{1,0,4,3,2:T(2,128)(2,1)}, u32[]{:S(2)}) copy-start(bf16[1,64,32,9,2]{1,0,4,3,2:T(2,128)(2,1)} %get-tuple-element.10) | copy-start | bytes 221188
  163.6 8.4 %copy-start.2 = (bf16[64,1536]{1,0:T(8,128)(2,1)S(1)}, bf16[64,1536]{1,0:T(8,128)(2,1)}, u32[]{:S(2)}) copy-start(bf16[64,1536]{1,0:T(8,128)(2,1)} %get-tuple-element.7) | copy-start | bytes 589828
  165.7 6.3 %collective-permute-start = (f32[64,1536]{1,0:T(8,128)S(1)}, f32[64,1536]{1,0:T(8,128)S(1)}, u32[]{:S(2)}, u32[]{:S(2)}) collective-permute-start(f32[64,1536]{1,0:T(8,128)S(1)} %convolution_bitcast_fusion), channel_id=1, source_target_pairs={{0,1},{1,0},{2,3},{3,2},{4,5},{5,4},{6,7},{7,6},{8,9},{9,8},{10,11... | collective-permute-start | bytes 1179656 | tf_op jit(solution)/shard_map/ppermute | solution.py:236

commit v9 on v8

--- a/solution.py
+++ b/solution.py
@@ -26,16 +26,18 @@
     s_n = lax.dot_general(q, kn_ref[...], dims, preferred_element_type=jnp.float32) * scale
     n_q, n_cache = s_c.shape
     n_new = s_n.shape[1]
-    use_c = ctx_pos * n_cache + lax.broadcasted_iota(jnp.int32, (n_q, n_cache), 1) < length
+    use_c = lax.broadcasted_iota(jnp.int32, (n_q, n_cache), 1) < length - ctx_pos * n_cache
     use_n = ctx_pos * n_new + lax.broadcasted_iota(jnp.int32, (n_q, n_new), 1) <= (
         lax.broadcasted_iota(jnp.int32, (n_q, n_new), 0)
     )
+    s_c = jnp.where(use_c, s_c, NEG_BIG)
+    s_n = jnp.where(use_n, s_n, NEG_BIG)
     top = jnp.maximum(
-        jnp.max(jnp.where(use_c, s_c, NEG_BIG), 1, keepdims=True),
-        jnp.max(jnp.where(use_n, s_n, NEG_BIG), 1, keepdims=True),
-    )
-    p_c = jnp.where(use_c, jnp.exp(s_c - top), 0.0)
-    p_n = jnp.where(use_n, jnp.exp(s_n - top), 0.0)
+        jnp.maximum(jnp.max(s_c, 1, keepdims=True), jnp.max(s_n, 1, keepdims=True)),
+        NEG_BIG / 10,
+    )
+    p_c = jnp.exp(s_c - top)
+    p_n = jnp.exp(s_n - top)
     total = jnp.sum(p_c, 1, keepdims=True) + jnp.sum(p_n, 1, keepdims=True)
     acc = jnp.dot(
         p_c.astype(jnp.bfloat16), vc_ref[...], preferred_element_type=jnp.float32

time: 173 us -> 172 us (level)
  transfers between devices with their start and end apart: 3 -> 3, of which waited for: 2 -> 2; matrix products, arithmetic and copies ran while one was open for 4% -> 5% of each run, Pallas kernels for 0% -> 0%
where the time goes in v9:
time: 172 us
  blocking collectives  80.4 us (47%)
  waiting for transfers between devices  37.7 us (22%)
  Pallas kernels  19 us (11%)
  starting transfers between devices  14.1 us (8%)
  local copies, waits for them, and re-layouts  8.81 us (5%)
  matrix products  7.75 us (5%)
  other arithmetic  3.15 us (2%)
    all_to_all x1, blocking collectives, local(): lax.all_to_all(outgoing, CHIP_AXES, split_axis=0, concat_axis=0, tiled=True)  53.9 us
    all_to_all x1, waiting for transfers between devices, local(): lax.all_to_all(result, CHIP_AXES, split_axis=0, concat_axis=0, tiled=True)  36.5 us
    all_gather x1, blocking collectives, local(): all_queries = lax.all_gather(queries[0], 'ctx', axis=0, tiled=True)  14.2 us
    pallas_call x1, Pallas kernels, partial_attention(): pl.pallas_call(attend_kernel, out_shape=jax.ShapeDtypeStruct((n_q, width)...  14.1 us
    all_gather x1, blocking collectives, local(): normed_both = lax.all_gather(normed, 'core', axis=0, tiled=True)  6.93 us
    all_to_all x1, starting transfers between devices, local(): lax.all_to_all(result, CHIP_AXES, split_axis=0, concat_axis=0, tiled=True)  5.43 us
    all_gather x1, blocking collectives, local(): both = lax.all_gather(packed, 'core', axis=0, tiled=True)  5.33 us
    pallas_call x1, Pallas kernels, combine_and_norm(): pl.pallas_call(combine_kernel, out_shape=(out, out), cost_estimate=cost)  4.93 us
  transfers between devices with their start and end apart: 3, of which 2 were waited for; matrix products, arithmetic and copies ran while one was open for 5% of the time, Pallas kernels for 0%

profile of v9, /device:TPU:1, one launch (start us, length us, event | category | flops | bytes accessed | tf_op | source)
XLA Modules:
  0.0 171.9 jit_solution(12862212171530149360)
XLA Ops:
  0.8 14.2 %all-gather = bf16[1,256,1536]{2,1,0:T(8,128)(2,1)} all-gather(bf16[1,64,1536]{2,1,0:T(8,128)(2,1)} %param.12), channel_id=2, replica_groups=mesh['ctx'=4,'z'=8,'x'=4,'core'=2] {'ctx'}, dimensions={1}, use_global_device_ids=true | all-gather | bytes 983040 | tf_op jit(solution)/shard_map/all_gather | solution.py:201
  15.0 0.6 pad_add_fusion.scal_ref
  15.6 14.1 %shard_map.109 = bf16[256,1664]{1,0:T(8,128)(2,1)} custom-call(s32[2]{0:T(128)} %pad_add_fusion.scal_ref, bf16[256,1536]{1,0:T(8,128)(2,1)} %bitcast.47, bf16[1024,1024]{1,0:T(8,128)(2,1)} %bitcast.50, bf16[1024,1024]{1,0:T(8,128)(2,1)} %bitcast.51, bf16[64,1024]{1,0:T(8,128)(2,1)} %bitcast.52, bf16[64,1024]{1,0:T(8,128)(2,1)} %bitcast.53), custom_call_target="tpu_custom_call" | custom-call | flops 1711276032 | bytes 3866624 | tf_op jit(solution)/shard_map/pallas_call | solution.py:74
  29.7 4.3 %all-to-all-start = ((bf16[4,64,1664]{2,1,0:T(8,128)(2,1)}), bf16[4,64,1664]{2,1,0:T(8,128)(2,1)}, u32[]{:S(2)}, u32[]{:S(2)}) async-start(bf16[4,64,1664]{2,1,0:T(8,128)(2,1)} %bitcast.46), calls=%async_computation | async-start | bytes 1703936 | tf_op jit(solution)/shard_map/all_to_all | solution.py:204
  34.4 5.3 %all_gather.10 = bf16[128,128]{1,0:T(8,128)(2,1)S(1)} all-gather(bf16[64,128]{1,0:T(8,128)(2,1)S(1)} %maximum_maximum_fusion), channel_id=1, replica_groups=mesh['ctx'=4,'z'=8,'x'=4,'core'=2] {'core'}, dimensions={0}, use_global_device_ids=true | all-gather | bytes 49152 | tf_op jit(solution)/shard_map/all_gather | solution.py:185
  39.9 0.6 reshape.70.gain_ref
  41.8 1.2 all-to-all-done.got_ref
  43.0 4.9 %shard_map.110 = (bf16[64,1536]{1,0:T(8,128)(2,1)}, bf16[64,1536]{1,0:T(8,128)(2,1)}) custom-call(bf16[4,64,1664]{2,1,0:T(8,128)(2,1)} %all-to-all-done.got_ref, bf16[64,1536]{1,0:T(8,128)(2,1)} %bitcast.48, bf16[1536,1536]{1,0:T(8,128)(2,1)} %w_ref.1, f32[1,1536]{1,0:T(1,128)} %reshape.70.gain_ref), custom_call_target="tpu_custom_call" | custom-call | flops 301989888 | bytes 6160384 | tf_op jit(solution)/shard_map/pallas_call | solution.py:140
  48.0 6.9 %all_gather.11 = bf16[128,1536]{1,0:T(8,128)(2,1)S(1)} all-gather(bf16[64,1536]{1,0:T(8,128)(2,1)} %get-tuple-element.8), channel_id=1, replica_groups=mesh['ctx'=4,'z'=8,'x'=4,'core'=2] {'core'}, dimensions={0}, use_global_device_ids=true | all-gather | bytes 589824 | tf_op jit(solution)/shard_map/all_gather | solution.py:210
  54.9 0.6 convolution_convert_fusion
  55.5 1.8 %copy.39 = bf16[32,9,2,1536]{3,2,1,0:T(2,128)(2,1)S(1)} copy(bf16[32,9,2,1536]{3,0,2,1:T(8,128)(2,1)S(1)} %convolution_convert_fusion) | data formatting | bytes 3538944 | tf_op jit(solution)/shard_map/convert_element_type | solution.py:218
  57.3 53.9 %all_to_all.15 = bf16[32,9,2,1536]{3,2,1,0:T(2,128)(2,1)S(1)} all-to-all(bf16[32,9,2,1536]{3,2,1,0:T(2,128)(2,1)S(1)} %copy.39), channel_id=1, replica_groups=mesh['ctx'=4,'z'=8,'x'=4,'core'=2] {'z','x'}, dimensions={0} | all-to-all | bytes 3538944 | tf_op jit(solution)/shard_map/all_to_all | solution.py:219
  111.3 2.0 %fusion = f32[32,9,2,1024]{3,0,2,1:T(8,128)S(1)} fusion(bf16[1,1536,1024]{2,1,0:T(8,128)(2,1)S(1)} %copy-done, bf16[32,9,2,1536]{3,2,1,0:T(2,128)(2,1)S(1)} %all_to_all.15), kind=kOutput, calls=%fused_computation | convolution fusion | flops 1811939328 | bytes 7274496 | tf_op jit(solution)/shard_map/jscd,df->jscf/dot_general | solution.py:221
  113.3 1.1 convolution_convert_fusion.1
  114.4 3.0 %copy.41 = bf16[32,9,2,1536]{3,2,1,0:T(2,128)(2,1)} copy(bf16[32,9,2,1536]{3,0,2,1:T(8,128)(2,1)S(1)} %convolution_convert_fusion.1) | data formatting | bytes 3538944 | tf_op jit(solution)/shard_map/convert_element_type | solution.py:227
  117.4 5.4 %all-to-all-start.2 = ((bf16[32,9,2,1536]{3,2,1,0:T(2,128)(2,1)}), bf16[32,9,2,1536]{3,2,1,0:T(2,128)(2,1)}, u32[]{:S(2)}, u32[]{:S(2)}) async-start(bf16[32,9,2,1536]{3,2,1,0:T(2,128)(2,1)} %copy.41), calls=%async_computation.2 | async-start | bytes 3538944 | tf_op jit(solution)/shard_map/all_to_all | solution.py:228
  122.9 0.9 fusion.9
  123.8 1.1 reshape.71
  124.8 1.4 constant_dynamic-slice_fusion
  126.3 36.5 %all-to-all-done.2 = bf16[32,9,2,1536]{3,2,1,0:T(2,128)(2,1)} async-done(((bf16[32,9,2,1536]{3,2,1,0:T(2,128)(2,1)}), bf16[32,9,2,1536]{3,2,1,0:T(2,128)(2,1)}, u32[]{:S(2)}, u32[]{:S(2)}) %all-to-all-start.2) | async-done | bytes 1769504 | tf_op jit(solution)/shard_map/all_to_all | solution.py:228
  162.8 2.1 %convolution_bitcast_fusion = f32[64,1536]{1,0:T(8,128)S(1)} fusion(bf16[32,9,2,1536]{3,2,1,0:T(2,128)(2,1)} %all-to-all-done.2, bf16[1,64,32,9,2]{1,0,4,3,2:T(2,128)(2,1)} %get-tuple-element.9), kind=kOutput, calls=%fused_computation.4 | convolution fusion | flops 113246208 | bytes 2236416 | tf_op jit(solution)/shard_map/tjsc,jscd->td/dot_general | solution.py:235
  164.9 4.3 %collective-permute-start = (f32[64,1536]{1,0:T(8,128)S(1)}, f32[64,1536]{1,0:T(8,128)S(1)}, u32[]{:S(2)}, u32[]{:S(2)}) collective-permute-start(f32[64,1536]{1,0:T(8,128)S(1)} %convolution_bitcast_fusion), channel_id=1, source_target_pairs={{0,1},{1,0},{2,3},{3,2},{4,5},{5,4},{6,7},{7,6},{8,9},{9,8},{10,11... | collective-permute-start | bytes 1179656 | tf_op jit(solution)/shard_map/ppermute | solution.py:238
  169.2 2.0 %convolution_bitcast_fusion.1 = f32[64,1536]{1,0:T(8,128)S(1)} fusion(bf16[32,9,2,1536]{3,2,1,0:T(2,128)(2,1)} %all-to-all-done.2, bf16[1,64,32,9,2]{1,0,4,3,2:T(2,128)(2,1)S(1)} %copy-done.1), kind=kOutput, calls=%fused_computation.5 | convolution fusion | flops 113246208 | bytes 2236416 | tf_op jit(solution)/shard_map/tjsc,jscd->td/dot_general | solution.py:239
  171.2 0.7 fusion.14
  (33 shorter events, 1.9 us)
Async XLA Ops:
  0.0 111.2 %copy-start = (bf16[1,1536,1024]{2,1,0:T(8,128)(2,1)S(1)}, bf16[1,1536,1024]{2,1,0:T(8,128)(2,1)}, u32[]{:S(2)}) copy-start(bf16[1,1536,1024]{2,1,0:T(8,128)(2,1)} %param.20) | copy-start | bytes 9437188
  15.6 18.5 %copy-start.5 = (bf16[1,64,6]{1,2,0:T(8,128)(2,1)S(1)}, bf16[1,64,6]{1,2,0:T(8,128)(2,1)}, u32[]{:S(2)}) copy-start(bf16[1,64,6]{1,2,0:T(8,128)(2,1)} %param.19) | copy-start | bytes 2308
  15.6 18.6 %copy-start.4 = (s32[1,64,6]{1,0,2:T(1,128)S(1)}, s32[1,64,6]{1,0,2:T(1,128)}, u32[]{:S(2)}) copy-start(s32[1,64,6]{1,0,2:T(1,128)} %param.18) | copy-start | bytes 4612
  29.7 10.2 %copy-start.3 = (f32[1536]{0:T(1024)S(1)}, f32[1536]{0:T(1024)}, u32[]{:S(2)}) copy-start(f32[1536]{0:T(1024)} %param.17) | copy-start | bytes 18436
  29.7 13.3 %all-to-all-start = ((bf16[4,64,1664]{2,1,0:T(8,128)(2,1)}), bf16[4,64,1664]{2,1,0:T(8,128)(2,1)}, u32[]{:S(2)}, u32[]{:S(2)}) async-start(bf16[4,64,1664]{2,1,0:T(8,128)(2,1)} %bitcast.46), calls=%async_computation | async-start | bytes 1703936 | tf_op jit(solution)/shard_map/all_to_all | solution.py:204
  111.2 2.0 %copy-start.6 = (bf16[1,512,1536]{2,1,0:T(8,128)(2,1)S(1)}, bf16[1,512,1536]{2,1,0:T(8,128)(2,1)}, u32[]{:S(2)}) copy-start(bf16[1,512,1536]{2,1,0:T(8,128)(2,1)} %param.21) | copy-start | bytes 4718596
  117.4 45.4 %all-to-all-start.2 = ((bf16[32,9,2,1536]{3,2,1,0:T(2,128)(2,1)}), bf16[32,9,2,1536]{3,2,1,0:T(2,128)(2,1)}, u32[]{:S(2)}, u32[]{:S(2)}) async-start(bf16[32,9,2,1536]{3,2,1,0:T(2,128)(2,1)} %copy.41), calls=%async_computation.2 | async-start | bytes 3538944 | tf_op jit(solution)/shard_map/all_to_all | solution.py:228
  126.3 43.0 %copy-start.1 = (bf16[1,64,32,9,2]{1,0,4,3,2:T(2,128)(2,1)S(1)}, bf16[1,64,32,9,2]{1,0,4,3,2:T(2,128)(2,1)}, u32[]{:S(2)}) copy-start(bf16[1,64,32,9,2]{1,0,4,3,2:T(2,128)(2,1)} %get-tuple-element.10) | copy-start | bytes 221188
  162.8 8.4 %copy-start.2 = (bf16[64,1536]{1,0:T(8,128)(2,1)S(1)}, bf16[64,1536]{1,0:T(8,128)(2,1)}, u32[]{:S(2)}) copy-start(bf16[64,1536]{1,0:T(8,128)(2,1)} %get-tuple-element.7) | copy-start | bytes 589828
  164.9 6.3 %collective-permute-start = (f32[64,1536]{1,0:T(8,128)S(1)}, f32[64,1536]{1,0:T(8,128)S(1)}, u32[]{:S(2)}, u32[]{:S(2)}) collective-permute-start(f32[64,1536]{1,0:T(8,128)S(1)} %convolution_bitcast_fusion), channel_id=1, source_target_pairs={{0,1},{1,0},{2,3},{3,2},{4,5},{5,4},{6,7},{7,6},{8,9},{9,8},{10,11... | collective-permute-start | bytes 1179656 | tf_op jit(solution)/shard_map/ppermute | solution.py:238

commit v10 on v9

--- a/solution.py
+++ b/solution.py
@@ -15,21 +15,23 @@
 
 
 def attend_kernel(scal_ref, q_ref, kc_ref, vc_ref, kn_ref, vn_ref, out_ref):
-    head = pl.program_id(0) * GROUP + pl.program_id(1)
+    kv_head = pl.program_id(0)
     heads = KVH * GROUP
     ctx_pos = scal_ref[0]
     length = scal_ref[1]
     scale = HD ** (-0.5)
-    q = q_ref[...]
+    n_q = q_ref.shape[0]
+    q = jnp.concatenate([q_ref[:, g * HD : (g + 1) * HD] for g in range(GROUP)], 0)
     dims = (((1,), (1,)), ((), ()))
     s_c = lax.dot_general(q, kc_ref[...], dims, preferred_element_type=jnp.float32) * scale
     s_n = lax.dot_general(q, kn_ref[...], dims, preferred_element_type=jnp.float32) * scale
-    n_q, n_cache = s_c.shape
+    n_rows, n_cache = s_c.shape
     n_new = s_n.shape[1]
-    use_c = lax.broadcasted_iota(jnp.int32, (n_q, n_cache), 1) < length - ctx_pos * n_cache
-    use_n = ctx_pos * n_new + lax.broadcasted_iota(jnp.int32, (n_q, n_new), 1) <= (
+    use_c = lax.broadcasted_iota(jnp.int32, (n_rows, n_cache), 1) < length - ctx_pos * n_cache
+    causal = ctx_pos * n_new + lax.broadcasted_iota(jnp.int32, (n_q, n_new), 1) <= (
         lax.broadcasted_iota(jnp.int32, (n_q, n_new), 0)
     )
+    use_n = jnp.concatenate([causal] * GROUP, 0)
     s_c = jnp.where(use_c, s_c, NEG_BIG)
     s_n = jnp.where(use_n, s_n, NEG_BIG)
     top = jnp.maximum(
@@ -42,10 +44,9 @@
     acc = jnp.dot(
         p_c.astype(jnp.bfloat16), vc_ref[...], preferred_element_type=jnp.float32
     ) + jnp.dot(p_n.astype(jnp.bfloat16), vn_ref[...], preferred_element_type=jnp.float32)
-    out_ref[:, pl.ds(pl.multiple_of(head * HD, HD), HD)] = acc.astype(out_ref.dtype)
     stat_cols = slice(heads * HD, (heads + 1) * HD)
 
-    @pl.when(head == 0)
+    @pl.when(kv_head == 0)
     def _():
         out_ref[:, stat_cols] = jnp.zeros((n_q, HD), out_ref.dtype)
 
@@ -53,10 +54,14 @@
     total_hi = total.astype(jnp.bfloat16).astype(jnp.float32)
     lane = lax.broadcasted_iota(jnp.int32, (n_q, HD), 1)
     held = out_ref[:, stat_cols].astype(jnp.float32)
-    held = jnp.where(lane == head, top_hi, held)
-    held = jnp.where(lane == heads + head, top - top_hi, held)
-    held = jnp.where(lane == 2 * heads + head, total_hi, held)
-    held = jnp.where(lane == 3 * heads + head, total - total_hi, held)
+    for g in range(GROUP):
+        head = kv_head * GROUP + g
+        rows = slice(g * n_q, (g + 1) * n_q)
+        out_ref[:, pl.ds(pl.multiple_of(head * HD, HD), HD)] = acc[rows].astype(out_ref.dtype)
+        held = jnp.where(lane == head, top_hi[rows], held)
+        held = jnp.where(lane == heads + head, (top - top_hi)[rows], held)
+        held = jnp.where(lane == 2 * heads + head, total_hi[rows], held)
+        held = jnp.where(lane == 3 * heads + head, (total - total_hi)[rows], held)
     out_ref[:, stat_cols] = held.astype(out_ref.dtype)
 
 
@@ -76,15 +81,15 @@
         out_shape=jax.ShapeDtypeStruct((n_q, width), jnp.bfloat16),
         grid_spec=pltpu.PrefetchScalarGridSpec(
             num_scalar_prefetch=1,
-            grid=(KVH, GROUP),
+            grid=(KVH,),
             in_specs=[
-                pl.BlockSpec((n_q, HD), lambda k, g, s: (0, k * GROUP + g)),
-                pl.BlockSpec((n_cache, HD), lambda k, g, s: (0, k)),
-                pl.BlockSpec((n_cache, HD), lambda k, g, s: (0, KVH + k)),
-                pl.BlockSpec((n_new, HD), lambda k, g, s: (0, k)),
-                pl.BlockSpec((n_new, HD), lambda k, g, s: (0, KVH + k)),
+                pl.BlockSpec((n_q, GROUP * HD), lambda k, s: (0, k)),
+                pl.BlockSpec((n_cache, HD), lambda k, s: (0, k)),
+                pl.BlockSpec((n_cache, HD), lambda k, s: (0, KVH + k)),
+                pl.BlockSpec((n_new, HD), lambda k, s: (0, k)),
+                pl.BlockSpec((n_new, HD), lambda k, s: (0, KVH + k)),
             ],
-            out_specs=pl.BlockSpec((n_q, width), lambda k, g, s: (0, 0)),
+            out_specs=pl.BlockSpec((n_q, width), lambda k, s: (0, 0)),
         ),
         cost_estimate=cost,
     )(scal, all_queries, cache_rows, cache_rows, new_rows, new_rows)

time: 172 us -> 170 us (0.988)
  Pallas kernels: 19 us -> 17.1 us
    pallas_call x1, Pallas kernels: 14.1 us -> 12.2 us  [partial_attention(): pl.pallas_call(attend_kernel, out_shape=jax.ShapeDtypeStruct((n_q, width)...]
where the time goes in v10:
time: 170 us
  blocking collectives  80.4 us (47%)
  waiting for transfers between devices  37.7 us (22%)
  Pallas kernels  17.1 us (10%)
  starting transfers between devices  14.1 us (8%)
  local copies, waits for them, and re-layouts  8.81 us (5%)
  matrix products  7.76 us (5%)
  other arithmetic  3.15 us (2%)
    all_to_all x1, blocking collectives, local(): lax.all_to_all(outgoing, CHIP_AXES, split_axis=0, concat_axis=0, tiled=True)  53.9 us
    all_to_all x1, waiting for transfers between devices, local(): lax.all_to_all(result, CHIP_AXES, split_axis=0, concat_axis=0, tiled=True)  36.5 us
    all_gather x1, blocking collectives, local(): all_queries = lax.all_gather(queries[0], 'ctx', axis=0, tiled=True)  14.2 us
    pallas_call x1, Pallas kernels, partial_attention(): pl.pallas_call(attend_kernel, out_shape=jax.ShapeDtypeStruct((n_q, width)...  12.2 us
    all_gather x1, blocking collectives, local(): normed_both = lax.all_gather(normed, 'core', axis=0, tiled=True)  6.94 us
    all_to_all x1, starting transfers between devices, local(): lax.all_to_all(result, CHIP_AXES, split_axis=0, concat_axis=0, tiled=True)  5.42 us
    all_gather x1, blocking collectives, local(): both = lax.all_gather(packed, 'core', axis=0, tiled=True)  5.34 us
    pallas_call x1, Pallas kernels, combine_and_norm(): pl.pallas_call(combine_kernel, out_shape=(out, out), cost_estimate=cost)  4.93 us
  transfers between devices with their start and end apart: 3, of which 2 were waited for; matrix products, arithmetic and copies ran while one was open for 5% of the time, Pallas kernels for 0%

profile of v10, /device:TPU:1, one launch (start us, length us, event | category | flops | bytes accessed | tf_op | source)
XLA Modules:
  0.0 170.0 jit_solution(8453225128065281684)
XLA Ops:
  0.8 14.2 %all-gather = bf16[1,256,1536]{2,1,0:T(8,128)(2,1)} all-gather(bf16[1,64,1536]{2,1,0:T(8,128)(2,1)} %param.12), channel_id=2, replica_groups=mesh['ctx'=4,'z'=8,'x'=4,'core'=2] {'ctx'}, dimensions={1}, use_global_device_ids=true | all-gather | bytes 983040 | tf_op jit(solution)/shard_map/all_gather | solution.py:206
  15.0 0.6 pad_add_fusion.scal_ref
  15.6 12.2 %shard_map.109 = bf16[256,1664]{1,0:T(8,128)(2,1)} custom-call(s32[2]{0:T(128)} %pad_add_fusion.scal_ref, bf16[256,1536]{1,0:T(8,128)(2,1)} %bitcast.47, bf16[1024,1024]{1,0:T(8,128)(2,1)} %bitcast.50, bf16[1024,1024]{1,0:T(8,128)(2,1)} %bitcast.51, bf16[64,1024]{1,0:T(8,128)(2,1)} %bitcast.52, bf16[64,1024]{1,0:T(8,128)(2,1)} %bitcast.53), custom_call_target="tpu_custom_call" | custom-call | flops 1711276032 | bytes 3866624 | tf_op jit(solution)/shard_map/pallas_call | solution.py:79
  27.8 4.3 %all-to-all-start = ((bf16[4,64,1664]{2,1,0:T(8,128)(2,1)}), bf16[4,64,1664]{2,1,0:T(8,128)(2,1)}, u32[]{:S(2)}, u32[]{:S(2)}) async-start(bf16[4,64,1664]{2,1,0:T(8,128)(2,1)} %bitcast.46), calls=%async_computation | async-start | bytes 1703936 | tf_op jit(solution)/shard_map/all_to_all | solution.py:209
  32.5 5.3 %all_gather.10 = bf16[128,128]{1,0:T(8,128)(2,1)S(1)} all-gather(bf16[64,128]{1,0:T(8,128)(2,1)S(1)} %maximum_maximum_fusion), channel_id=1, replica_groups=mesh['ctx'=4,'z'=8,'x'=4,'core'=2] {'core'}, dimensions={0}, use_global_device_ids=true | all-gather | bytes 49152 | tf_op jit(solution)/shard_map/all_gather | solution.py:190
  37.9 0.6 reshape.70.gain_ref
  39.9 1.2 all-to-all-done.got_ref
  41.1 4.9 %shard_map.110 = (bf16[64,1536]{1,0:T(8,128)(2,1)}, bf16[64,1536]{1,0:T(8,128)(2,1)}) custom-call(bf16[4,64,1664]{2,1,0:T(8,128)(2,1)} %all-to-all-done.got_ref, bf16[64,1536]{1,0:T(8,128)(2,1)} %bitcast.48, bf16[1536,1536]{1,0:T(8,128)(2,1)} %w_ref.1, f32[1,1536]{1,0:T(1,128)} %reshape.70.gain_ref), custom_call_target="tpu_custom_call" | custom-call | flops 301989888 | bytes 6160384 | tf_op jit(solution)/shard_map/pallas_call | solution.py:145
  46.0 6.9 %all_gather.11 = bf16[128,1536]{1,0:T(8,128)(2,1)S(1)} all-gather(bf16[64,1536]{1,0:T(8,128)(2,1)} %get-tuple-element.8), channel_id=1, replica_groups=mesh['ctx'=4,'z'=8,'x'=4,'core'=2] {'core'}, dimensions={0}, use_global_device_ids=true | all-gather | bytes 589824 | tf_op jit(solution)/shard_map/all_gather | solution.py:215
  53.0 0.6 convolution_convert_fusion
  53.6 1.8 %copy.39 = bf16[32,9,2,1536]{3,2,1,0:T(2,128)(2,1)S(1)} copy(bf16[32,9,2,1536]{3,0,2,1:T(8,128)(2,1)S(1)} %convolution_convert_fusion) | data formatting | bytes 3538944 | tf_op jit(solution)/shard_map/convert_element_type | solution.py:223
  55.4 53.9 %all_to_all.15 = bf16[32,9,2,1536]{3,2,1,0:T(2,128)(2,1)S(1)} all-to-all(bf16[32,9,2,1536]{3,2,1,0:T(2,128)(2,1)S(1)} %copy.39), channel_id=1, replica_groups=mesh['ctx'=4,'z'=8,'x'=4,'core'=2] {'z','x'}, dimensions={0} | all-to-all | bytes 3538944 | tf_op jit(solution)/shard_map/all_to_all | solution.py:224
  109.3 2.0 %fusion = f32[32,9,2,1024]{3,0,2,1:T(8,128)S(1)} fusion(bf16[1,1536,1024]{2,1,0:T(8,128)(2,1)S(1)} %copy-done, bf16[32,9,2,1536]{3,2,1,0:T(2,128)(2,1)S(1)} %all_to_all.15), kind=kOutput, calls=%fused_computation | convolution fusion | flops 1811939328 | bytes 7274496 | tf_op jit(solution)/shard_map/jscd,df->jscf/dot_general | solution.py:226
  111.3 1.1 convolution_convert_fusion.1
  112.5 3.0 %copy.41 = bf16[32,9,2,1536]{3,2,1,0:T(2,128)(2,1)} copy(bf16[32,9,2,1536]{3,0,2,1:T(8,128)(2,1)S(1)} %convolution_convert_fusion.1) | data formatting | bytes 3538944 | tf_op jit(solution)/shard_map/convert_element_type | solution.py:232
  115.5 5.4 %all-to-all-start.2 = ((bf16[32,9,2,1536]{3,2,1,0:T(2,128)(2,1)}), bf16[32,9,2,1536]{3,2,1,0:T(2,128)(2,1)}, u32[]{:S(2)}, u32[]{:S(2)}) async-start(bf16[32,9,2,1536]{3,2,1,0:T(2,128)(2,1)} %copy.41), calls=%async_computation.2 | async-start | bytes 3538944 | tf_op jit(solution)/shard_map/all_to_all | solution.py:233
  121.0 0.9 fusion.9
  121.8 1.1 reshape.71
  122.9 1.4 constant_dynamic-slice_fusion
  124.3 36.5 %all-to-all-done.2 = bf16[32,9,2,1536]{3,2,1,0:T(2,128)(2,1)} async-done(((bf16[32,9,2,1536]{3,2,1,0:T(2,128)(2,1)}), bf16[32,9,2,1536]{3,2,1,0:T(2,128)(2,1)}, u32[]{:S(2)}, u32[]{:S(2)}) %all-to-all-start.2) | async-done | bytes 1769504 | tf_op jit(solution)/shard_map/all_to_all | solution.py:233
  160.9 2.1 %convolution_bitcast_fusion = f32[64,1536]{1,0:T(8,128)S(1)} fusion(bf16[32,9,2,1536]{3,2,1,0:T(2,128)(2,1)} %all-to-all-done.2, bf16[1,64,32,9,2]{1,0,4,3,2:T(2,128)(2,1)} %get-tuple-element.9), kind=kOutput, calls=%fused_computation.4 | convolution fusion | flops 113246208 | bytes 2236416 | tf_op jit(solution)/shard_map/tjsc,jscd->td/dot_general | solution.py:240
  163.0 4.3 %collective-permute-start = (f32[64,1536]{1,0:T(8,128)S(1)}, f32[64,1536]{1,0:T(8,128)S(1)}, u32[]{:S(2)}, u32[]{:S(2)}) collective-permute-start(f32[64,1536]{1,0:T(8,128)S(1)} %convolution_bitcast_fusion), channel_id=1, source_target_pairs={{0,1},{1,0},{2,3},{3,2},{4,5},{5,4},{6,7},{7,6},{8,9},{9,8},{10,11... | collective-permute-start | bytes 1179656 | tf_op jit(solution)/shard_map/ppermute | solution.py:243
  167.3 2.0 %convolution_bitcast_fusion.1 = f32[64,1536]{1,0:T(8,128)S(1)} fusion(bf16[32,9,2,1536]{3,2,1,0:T(2,128)(2,1)} %all-to-all-done.2, bf16[1,64,32,9,2]{1,0,4,3,2:T(2,128)(2,1)S(1)} %copy-done.1), kind=kOutput, calls=%fused_computation.5 | convolution fusion | flops 113246208 | bytes 2236416 | tf_op jit(solution)/shard_map/tjsc,jscd->td/dot_general | solution.py:244
  169.3 0.7 fusion.14
  (33 shorter events, 1.9 us)
Async XLA Ops:
  0.0 109.3 %copy-start = (bf16[1,1536,1024]{2,1,0:T(8,128)(2,1)S(1)}, bf16[1,1536,1024]{2,1,0:T(8,128)(2,1)}, u32[]{:S(2)}) copy-start(bf16[1,1536,1024]{2,1,0:T(8,128)(2,1)} %param.20) | copy-start | bytes 9437188
  15.6 16.5 %copy-start.5 = (bf16[1,64,6]{1,2,0:T(8,128)(2,1)S(1)}, bf16[1,64,6]{1,2,0:T(8,128)(2,1)}, u32[]{:S(2)}) copy-start(bf16[1,64,6]{1,2,0:T(8,128)(2,1)} %param.19) | copy-start | bytes 2308
  15.6 16.6 %copy-start.4 = (s32[1,64,6]{1,0,2:T(1,128)S(1)}, s32[1,64,6]{1,0,2:T(1,128)}, u32[]{:S(2)}) copy-start(s32[1,64,6]{1,0,2:T(1,128)} %param.18) | copy-start | bytes 4612
  27.8 10.2 %copy-start.3 = (f32[1536]{0:T(1024)S(1)}, f32[1536]{0:T(1024)}, u32[]{:S(2)}) copy-start(f32[1536]{0:T(1024)} %param.17) | copy-start | bytes 18436
  27.8 13.3 %all-to-all-start = ((bf16[4,64,1664]{2,1,0:T(8,128)(2,1)}), bf16[4,64,1664]{2,1,0:T(8,128)(2,1)}, u32[]{:S(2)}, u32[]{:S(2)}) async-start(bf16[4,64,1664]{2,1,0:T(8,128)(2,1)} %bitcast.46), calls=%async_computation | async-start | bytes 1703936 | tf_op jit(solution)/shard_map/all_to_all | solution.py:209
  109.3 2.0 %copy-start.6 = (bf16[1,512,1536]{2,1,0:T(8,128)(2,1)S(1)}, bf16[1,512,1536]{2,1,0:T(8,128)(2,1)}, u32[]{:S(2)}) copy-start(bf16[1,512,1536]{2,1,0:T(8,128)(2,1)} %param.21) | copy-start | bytes 4718596
  115.5 45.4 %all-to-all-start.2 = ((bf16[32,9,2,1536]{3,2,1,0:T(2,128)(2,1)}), bf16[32,9,2,1536]{3,2,1,0:T(2,128)(2,1)}, u32[]{:S(2)}, u32[]{:S(2)}) async-start(bf16[32,9,2,1536]{3,2,1,0:T(2,128)(2,1)} %copy.41), calls=%async_computation.2 | async-start | bytes 3538944 | tf_op jit(solution)/shard_map/all_to_all | solution.py:233
  124.3 43.0 %copy-start.1 = (bf16[1,64,32,9,2]{1,0,4,3,2:T(2,128)(2,1)S(1)}, bf16[1,64,32,9,2]{1,0,4,3,2:T(2,128)(2,1)}, u32[]{:S(2)}) copy-start(bf16[1,64,32,9,2]{1,0,4,3,2:T(2,128)(2,1)} %get-tuple-element.10) | copy-start | bytes 221188
  160.9 8.4 %copy-start.2 = (bf16[64,1536]{1,0:T(8,128)(2,1)S(1)}, bf16[64,1536]{1,0:T(8,128)(2,1)}, u32[]{:S(2)}) copy-start(bf16[64,1536]{1,0:T(8,128)(2,1)} %get-tuple-element.7) | copy-start | bytes 589828
  163.0 6.3 %collective-permute-start = (f32[64,1536]{1,0:T(8,128)S(1)}, f32[64,1536]{1,0:T(8,128)S(1)}, u32[]{:S(2)}, u32[]{:S(2)}) collective-permute-start(f32[64,1536]{1,0:T(8,128)S(1)} %convolution_bitcast_fusion), channel_id=1, source_target_pairs={{0,1},{1,0},{2,3},{3,2},{4,5},{5,4},{6,7},{7,6},{8,9},{9,8},{10,11... | collective-permute-start | bytes 1179656 | tf_op jit(solution)/shard_map/ppermute | solution.py:243

commit v11 on v10

--- a/solution.py
+++ b/solution.py
@@ -20,11 +20,12 @@
     ctx_pos = scal_ref[0]
     length = scal_ref[1]
     scale = HD ** (-0.5)
+    scale_log2 = scale * 1.4426950408889634
     n_q = q_ref.shape[0]
     q = jnp.concatenate([q_ref[:, g * HD : (g + 1) * HD] for g in range(GROUP)], 0)
     dims = (((1,), (1,)), ((), ()))
-    s_c = lax.dot_general(q, kc_ref[...], dims, preferred_element_type=jnp.float32) * scale
-    s_n = lax.dot_general(q, kn_ref[...], dims, preferred_element_type=jnp.float32) * scale
+    s_c = lax.dot_general(q, kc_ref[...], dims, preferred_element_type=jnp.float32)
+    s_n = lax.dot_general(q, kn_ref[...], dims, preferred_element_type=jnp.float32)
     n_rows, n_cache = s_c.shape
     n_new = s_n.shape[1]
     use_c = lax.broadcasted_iota(jnp.int32, (n_rows, n_cache), 1) < length - ctx_pos * n_cache
@@ -38,8 +39,9 @@
         jnp.maximum(jnp.max(s_c, 1, keepdims=True), jnp.max(s_n, 1, keepdims=True)),
         NEG_BIG / 10,
     )
-    p_c = jnp.exp(s_c - top)
-    p_n = jnp.exp(s_n - top)
+    p_c = jnp.exp2((s_c - top) * scale_log2)
+    p_n = jnp.exp2((s_n - top) * scale_log2)
+    top = top * scale
     total = jnp.sum(p_c, 1, keepdims=True) + jnp.sum(p_n, 1, keepdims=True)
     acc = jnp.dot(
         p_c.astype(jnp.bfloat16), vc_ref[...], preferred_element_type=jnp.float32

time: 170 us -> 170 us (level)
  no operation moved by 1% of the time
where the time goes in v11:
time: 170 us
  blocking collectives  80.4 us (47%)
  waiting for transfers between devices  37.7 us (22%)
  Pallas kernels  17 us (10%)
  starting transfers between devices  14.1 us (8%)
  local copies, waits for them, and re-layouts  8.81 us (5%)
  matrix products  7.75 us (5%)
  other arithmetic  3.15 us (2%)
    all_to_all x1, blocking collectives, local(): lax.all_to_all(outgoing, CHIP_AXES, split_axis=0, concat_axis=0, tiled=True)  53.9 us
    all_to_all x1, waiting for transfers between devices, local(): lax.all_to_all(result, CHIP_AXES, split_axis=0, concat_axis=0, tiled=True)  36.6 us
    all_gather x1, blocking collectives, local(): all_queries = lax.all_gather(queries[0], 'ctx', axis=0, tiled=True)  14.2 us
    pallas_call x1, Pallas kernels, partial_attention(): pl.pallas_call(attend_kernel, out_shape=jax.ShapeDtypeStruct((n_q, width)...  12 us
    all_gather x1, blocking collectives, local(): normed_both = lax.all_gather(normed, 'core', axis=0, tiled=True)  6.94 us
    all_to_all x1, starting transfers between devices, local(): lax.all_to_all(result, CHIP_AXES, split_axis=0, concat_axis=0, tiled=True)  5.43 us
    all_gather x1, blocking collectives, local(): both = lax.all_gather(packed, 'core', axis=0, tiled=True)  5.34 us
    pallas_call x1, Pallas kernels, combine_and_norm(): pl.pallas_call(combine_kernel, out_shape=(out, out), cost_estimate=cost)  4.93 us
  transfers between devices with their start and end apart: 3, of which 2 were waited for; matrix products, arithmetic and copies ran while one was open for 5% of the time, Pallas kernels for 0%

profile of v11, /device:TPU:1, one launch (start us, length us, event | category | flops | bytes accessed | tf_op | source)
XLA Modules:
  0.0 169.9 jit_solution(1203569933804322683)
XLA Ops:
  0.8 14.2 %all-gather = bf16[1,256,1536]{2,1,0:T(8,128)(2,1)} all-gather(bf16[1,64,1536]{2,1,0:T(8,128)(2,1)} %param.12), channel_id=2, replica_groups=mesh['ctx'=4,'z'=8,'x'=4,'core'=2] {'ctx'}, dimensions={1}, use_global_device_ids=true | all-gather | bytes 983040 | tf_op jit(solution)/shard_map/all_gather | solution.py:208
  15.0 0.6 pad_add_fusion.scal_ref
  15.6 12.0 %shard_map.109 = bf16[256,1664]{1,0:T(8,128)(2,1)} custom-call(s32[2]{0:T(128)} %pad_add_fusion.scal_ref, bf16[256,1536]{1,0:T(8,128)(2,1)} %bitcast.47, bf16[1024,1024]{1,0:T(8,128)(2,1)} %bitcast.50, bf16[1024,1024]{1,0:T(8,128)(2,1)} %bitcast.51, bf16[64,1024]{1,0:T(8,128)(2,1)} %bitcast.52, bf16[64,1024]{1,0:T(8,128)(2,1)} %bitcast.53), custom_call_target="tpu_custom_call" | custom-call | flops 1711276032 | bytes 3866624 | tf_op jit(solution)/shard_map/pallas_call | solution.py:81
  27.6 4.3 %all-to-all-start = ((bf16[4,64,1664]{2,1,0:T(8,128)(2,1)}), bf16[4,64,1664]{2,1,0:T(8,128)(2,1)}, u32[]{:S(2)}, u32[]{:S(2)}) async-start(bf16[4,64,1664]{2,1,0:T(8,128)(2,1)} %bitcast.46), calls=%async_computation | async-start | bytes 1703936 | tf_op jit(solution)/shard_map/all_to_all | solution.py:211
  32.4 5.3 %all_gather.10 = bf16[128,128]{1,0:T(8,128)(2,1)S(1)} all-gather(bf16[64,128]{1,0:T(8,128)(2,1)S(1)} %maximum_maximum_fusion), channel_id=1, replica_groups=mesh['ctx'=4,'z'=8,'x'=4,'core'=2] {'core'}, dimensions={0}, use_global_device_ids=true | all-gather | bytes 49152 | tf_op jit(solution)/shard_map/all_gather | solution.py:192
  37.8 0.6 reshape.70.gain_ref
  39.8 1.2 all-to-all-done.got_ref
  40.9 4.9 %shard_map.110 = (bf16[64,1536]{1,0:T(8,128)(2,1)}, bf16[64,1536]{1,0:T(8,128)(2,1)}) custom-call(bf16[4,64,1664]{2,1,0:T(8,128)(2,1)} %all-to-all-done.got_ref, bf16[64,1536]{1,0:T(8,128)(2,1)} %bitcast.48, bf16[1536,1536]{1,0:T(8,128)(2,1)} %w_ref.1, f32[1,1536]{1,0:T(1,128)} %reshape.70.gain_ref), custom_call_target="tpu_custom_call" | custom-call | flops 301989888 | bytes 6160384 | tf_op jit(solution)/shard_map/pallas_call | solution.py:147
  45.9 6.9 %all_gather.11 = bf16[128,1536]{1,0:T(8,128)(2,1)S(1)} all-gather(bf16[64,1536]{1,0:T(8,128)(2,1)} %get-tuple-element.8), channel_id=1, replica_groups=mesh['ctx'=4,'z'=8,'x'=4,'core'=2] {'core'}, dimensions={0}, use_global_device_ids=true | all-gather | bytes 589824 | tf_op jit(solution)/shard_map/all_gather | solution.py:217
  52.8 0.6 convolution_convert_fusion
  53.4 1.8 %copy.39 = bf16[32,9,2,1536]{3,2,1,0:T(2,128)(2,1)S(1)} copy(bf16[32,9,2,1536]{3,0,2,1:T(8,128)(2,1)S(1)} %convolution_convert_fusion) | data formatting | bytes 3538944 | tf_op jit(solution)/shard_map/convert_element_type | solution.py:225
  55.3 53.9 %all_to_all.15 = bf16[32,9,2,1536]{3,2,1,0:T(2,128)(2,1)S(1)} all-to-all(bf16[32,9,2,1536]{3,2,1,0:T(2,128)(2,1)S(1)} %copy.39), channel_id=1, replica_groups=mesh['ctx'=4,'z'=8,'x'=4,'core'=2] {'z','x'}, dimensions={0} | all-to-all | bytes 3538944 | tf_op jit(solution)/shard_map/all_to_all | solution.py:226
  109.2 2.0 %fusion = f32[32,9,2,1024]{3,0,2,1:T(8,128)S(1)} fusion(bf16[1,1536,1024]{2,1,0:T(8,128)(2,1)S(1)} %copy-done, bf16[32,9,2,1536]{3,2,1,0:T(2,128)(2,1)S(1)} %all_to_all.15), kind=kOutput, calls=%fused_computation | convolution fusion | flops 1811939328 | bytes 7274496 | tf_op jit(solution)/shard_map/jscd,df->jscf/dot_general | solution.py:228
  111.2 1.1 convolution_convert_fusion.1
  112.3 3.0 %copy.41 = bf16[32,9,2,1536]{3,2,1,0:T(2,128)(2,1)} copy(bf16[32,9,2,1536]{3,0,2,1:T(8,128)(2,1)S(1)} %convolution_convert_fusion.1) | data formatting | bytes 3538944 | tf_op jit(solution)/shard_map/convert_element_type | solution.py:234
  115.3 5.4 %all-to-all-start.2 = ((bf16[32,9,2,1536]{3,2,1,0:T(2,128)(2,1)}), bf16[32,9,2,1536]{3,2,1,0:T(2,128)(2,1)}, u32[]{:S(2)}, u32[]{:S(2)}) async-start(bf16[32,9,2,1536]{3,2,1,0:T(2,128)(2,1)} %copy.41), calls=%async_computation.2 | async-start | bytes 3538944 | tf_op jit(solution)/shard_map/all_to_all | solution.py:235
  120.8 0.9 fusion.9
  121.7 1.1 reshape.71
  122.7 1.4 constant_dynamic-slice_fusion
  124.2 36.6 %all-to-all-done.2 = bf16[32,9,2,1536]{3,2,1,0:T(2,128)(2,1)} async-done(((bf16[32,9,2,1536]{3,2,1,0:T(2,128)(2,1)}), bf16[32,9,2,1536]{3,2,1,0:T(2,128)(2,1)}, u32[]{:S(2)}, u32[]{:S(2)}) %all-to-all-start.2) | async-done | bytes 1769504 | tf_op jit(solution)/shard_map/all_to_all | solution.py:235
  160.7 2.1 %convolution_bitcast_fusion = f32[64,1536]{1,0:T(8,128)S(1)} fusion(bf16[32,9,2,1536]{3,2,1,0:T(2,128)(2,1)} %all-to-all-done.2, bf16[1,64,32,9,2]{1,0,4,3,2:T(2,128)(2,1)} %get-tuple-element.9), kind=kOutput, calls=%fused_computation.4 | convolution fusion | flops 113246208 | bytes 2236416 | tf_op jit(solution)/shard_map/tjsc,jscd->td/dot_general | solution.py:242
  162.8 4.3 %collective-permute-start = (f32[64,1536]{1,0:T(8,128)S(1)}, f32[64,1536]{1,0:T(8,128)S(1)}, u32[]{:S(2)}, u32[]{:S(2)}) collective-permute-start(f32[64,1536]{1,0:T(8,128)S(1)} %convolution_bitcast_fusion), channel_id=1, source_target_pairs={{0,1},{1,0},{2,3},{3,2},{4,5},{5,4},{6,7},{7,6},{8,9},{9,8},{10,11... | collective-permute-start | bytes 1179656 | tf_op jit(solution)/shard_map/ppermute | solution.py:245
  167.1 2.0 %convolution_bitcast_fusion.1 = f32[64,1536]{1,0:T(8,128)S(1)} fusion(bf16[32,9,2,1536]{3,2,1,0:T(2,128)(2,1)} %all-to-all-done.2, bf16[1,64,32,9,2]{1,0,4,3,2:T(2,128)(2,1)S(1)} %copy-done.1), kind=kOutput, calls=%fused_computation.5 | convolution fusion | flops 113246208 | bytes 2236416 | tf_op jit(solution)/shard_map/tjsc,jscd->td/dot_general | solution.py:246
  169.1 0.7 fusion.14
  (33 shorter events, 1.9 us)
Async XLA Ops:
  0.0 109.2 %copy-start = (bf16[1,1536,1024]{2,1,0:T(8,128)(2,1)S(1)}, bf16[1,1536,1024]{2,1,0:T(8,128)(2,1)}, u32[]{:S(2)}) copy-start(bf16[1,1536,1024]{2,1,0:T(8,128)(2,1)} %param.20) | copy-start | bytes 9437188
  15.6 16.4 %copy-start.5 = (bf16[1,64,6]{1,2,0:T(8,128)(2,1)S(1)}, bf16[1,64,6]{1,2,0:T(8,128)(2,1)}, u32[]{:S(2)}) copy-start(bf16[1,64,6]{1,2,0:T(8,128)(2,1)} %param.19) | copy-start | bytes 2308
  15.6 16.5 %copy-start.4 = (s32[1,64,6]{1,0,2:T(1,128)S(1)}, s32[1,64,6]{1,0,2:T(1,128)}, u32[]{:S(2)}) copy-start(s32[1,64,6]{1,0,2:T(1,128)} %param.18) | copy-start | bytes 4612
  27.6 10.2 %copy-start.3 = (f32[1536]{0:T(1024)S(1)}, f32[1536]{0:T(1024)}, u32[]{:S(2)}) copy-start(f32[1536]{0:T(1024)} %param.17) | copy-start | bytes 18436
  27.6 13.3 %all-to-all-start = ((bf16[4,64,1664]{2,1,0:T(8,128)(2,1)}), bf16[4,64,1664]{2,1,0:T(8,128)(2,1)}, u32[]{:S(2)}, u32[]{:S(2)}) async-start(bf16[4,64,1664]{2,1,0:T(8,128)(2,1)} %bitcast.46), calls=%async_computation | async-start | bytes 1703936 | tf_op jit(solution)/shard_map/all_to_all | solution.py:211
  109.2 2.0 %copy-start.6 = (bf16[1,512,1536]{2,1,0:T(8,128)(2,1)S(1)}, bf16[1,512,1536]{2,1,0:T(8,128)(2,1)}, u32[]{:S(2)}) copy-start(bf16[1,512,1536]{2,1,0:T(8,128)(2,1)} %param.21) | copy-start | bytes 4718596
  115.3 45.4 %all-to-all-start.2 = ((bf16[32,9,2,1536]{3,2,1,0:T(2,128)(2,1)}), bf16[32,9,2,1536]{3,2,1,0:T(2,128)(2,1)}, u32[]{:S(2)}, u32[]{:S(2)}) async-start(bf16[32,9,2,1536]{3,2,1,0:T(2,128)(2,1)} %copy.41), calls=%async_computation.2 | async-start | bytes 3538944 | tf_op jit(solution)/shard_map/all_to_all | solution.py:235
  124.2 43.0 %copy-start.1 = (bf16[1,64,32,9,2]{1,0,4,3,2:T(2,128)(2,1)S(1)}, bf16[1,64,32,9,2]{1,0,4,3,2:T(2,128)(2,1)}, u32[]{:S(2)}) copy-start(bf16[1,64,32,9,2]{1,0,4,3,2:T(2,128)(2,1)} %get-tuple-element.10) | copy-start | bytes 221188
  160.7 8.4 %copy-start.2 = (bf16[64,1536]{1,0:T(8,128)(2,1)S(1)}, bf16[64,1536]{1,0:T(8,128)(2,1)}, u32[]{:S(2)}) copy-start(bf16[64,1536]{1,0:T(8,128)(2,1)} %get-tuple-element.7) | copy-start | bytes 589828
  162.8 6.3 %collective-permute-start = (f32[64,1536]{1,0:T(8,128)S(1)}, f32[64,1536]{1,0:T(8,128)S(1)}, u32[]{:S(2)}, u32[]{:S(2)}) collective-permute-start(f32[64,1536]{1,0:T(8,128)S(1)} %convolution_bitcast_fusion), channel_id=1, source_target_pairs={{0,1},{1,0},{2,3},{3,2},{4,5},{5,4},{6,7},{7,6},{8,9},{9,8},{10,11... | collective-permute-start | bytes 1179656 | tf_op jit(solution)/shard_map/ppermute | solution.py:245

commit v12 on v11

--- a/solution.py
+++ b/solution.py
@@ -214,15 +214,22 @@
     mixed, normed = combine_and_norm(got, residual_in[0], out_proj, norm_gain)
     widened = mixed.astype(jnp.float32)
 
-    normed_both = lax.all_gather(normed, "core", axis=0, tiled=True)
+    partner_normed = lax.ppermute(normed, "core", [(0, 1), (1, 0)])
     chip_count = expert_total // core_size
     slot_ids = jnp.arange(chip_count * block_rows)
     hits = dest[None, :, :] == slot_ids[:, None, None]
     slot_shape = (chip_count, capacity, core_size)
-    select = jnp.any(hits, -1).astype(jnp.bfloat16).reshape(*slot_shape, -1)
-    outgoing = jnp.einsum(
-        "jscr,rd->jscd", select, normed_both, preferred_element_type=jnp.float32
-    ).astype(jnp.bfloat16)
+    select = jnp.any(hits, -1).astype(jnp.bfloat16).reshape(*slot_shape, core_size, tok_count)
+    own_rows = jnp.einsum(
+        "jscr,rd->jscd", select[:, :, :, core_pos], normed, preferred_element_type=jnp.float32
+    )
+    partner_rows = jnp.einsum(
+        "jscr,rd->jscd",
+        select[:, :, :, 1 - core_pos],
+        partner_normed,
+        preferred_element_type=jnp.float32,
+    )
+    outgoing = (lax.optimization_barrier(own_rows) + partner_rows).astype(jnp.bfloat16)
     incoming = lax.all_to_all(outgoing, CHIP_AXES, split_axis=0, concat_axis=0, tiled=True)
     hidden_half = w_gate_up.shape[2] // 2
     gate_up = jnp.einsum("jscd,df->jscf", incoming, w_gate_up[0], preferred_element_type=jnp.float32)

time: 170 us -> 171 us (level)
  blocking collectives: 80.4 us -> 74.2 us
  matrix products: 7.75 us -> 10.3 us
  local copies, waits for them, and re-layouts: 8.81 us -> 11.3 us
  starting transfers between devices: 14.1 us -> 16.5 us
    all_gather x1 -> x0, blocking collectives: 6.94 us -> none  [local(): normed_both = lax.all_gather(normed, 'core', axis=0, tiled=True)]
    ppermute x0 -> x1, starting transfers between devices: none -> 3.74 us  [local(): partner_normed = lax.ppermute(normed, 'core', [(0, 1), (1, 0)])]
    dot_general x1 -> x2, matrix products: 0.6 us -> 3.17 us  [the longest x1 1.61 us: local(): jnp.einsum('jscr,rd->jscd', select[:, :, :, core_pos], normed, preferred_...]
  transfers between devices with their start and end apart: 3 -> 4, of which waited for: 2 -> 1; matrix products, arithmetic and copies ran while one was open for 5% -> 7% of each run, Pallas kernels for 0% -> 0%
where the time goes in v12:
time: 171 us
  blocking collectives  74.2 us (43%)
  waiting for transfers between devices  37.4 us (22%)
  Pallas kernels  16.8 us (10%)
  starting transfers between devices  16.5 us (10%)
  local copies, waits for them, and re-layouts  11.3 us (7%)
  matrix products  10.3 us (6%)
  other arithmetic  3.21 us (2%)
    all_to_all x1, blocking collectives, local(): lax.all_to_all(outgoing, CHIP_AXES, split_axis=0, concat_axis=0, tiled=True)  54.6 us
    all_to_all x1, waiting for transfers between devices, local(): lax.all_to_all(result, CHIP_AXES, split_axis=0, concat_axis=0, tiled=True)  37.4 us
    all_gather x1, blocking collectives, local(): all_queries = lax.all_gather(queries[0], 'ctx', axis=0, tiled=True)  14.2 us
    pallas_call x1, Pallas kernels, partial_attention(): pl.pallas_call(attend_kernel, out_shape=jax.ShapeDtypeStruct((n_q, width)...  11.9 us
    all_gather x1, blocking collectives, local(): both = lax.all_gather(packed, 'core', axis=0, tiled=True)  5.35 us
    all_to_all x1, starting transfers between devices, local(): lax.all_to_all(result, CHIP_AXES, split_axis=0, concat_axis=0, tiled=True)  5.01 us
    pallas_call x1, Pallas kernels, combine_and_norm(): pl.pallas_call(combine_kernel, out_shape=(out, out), cost_estimate=cost)  4.94 us
    all_to_all x1, starting transfers between devices, local(): lax.all_to_all(part.reshape(n_ctx, tok_count, part.shape[1]), 'ctx', spli...  4.34 us
  transfers between devices with their start and end apart: 4, of which 1 were waited for; matrix products, arithmetic and copies ran while one was open for 7% of the time, Pallas kernels for 0%

profile of v12, /device:TPU:1, one launch (start us, length us, event | category | flops | bytes accessed | tf_op | source)
XLA Modules:
  0.0 170.8 jit_solution(13644208690911520483)
XLA Ops:
  0.8 14.2 %all-gather = bf16[1,256,1536]{2,1,0:T(8,128)(2,1)} all-gather(bf16[1,64,1536]{2,1,0:T(8,128)(2,1)} %param.12), channel_id=2, replica_groups=mesh['ctx'=4,'z'=8,'x'=4,'core'=2] {'ctx'}, dimensions={1}, use_global_device_ids=true | all-gather | bytes 983040 | tf_op jit(solution)/shard_map/all_gather | solution.py:208
  15.6 11.9 %shard_map.109 = bf16[256,1664]{1,0:T(8,128)(2,1)} custom-call(s32[2]{0:T(128)} %pad_add_fusion.scal_ref, bf16[256,1536]{1,0:T(8,128)(2,1)} %bitcast.58, bf16[1024,1024]{1,0:T(8,128)(2,1)} %bitcast.61, bf16[1024,1024]{1,0:T(8,128)(2,1)} %bitcast.62, bf16[64,1024]{1,0:T(8,128)(2,1)} %bitcast.63, bf16[64,1024]{1,0:T(8,128)(2,1)} %bitcast.64), custom_call_target="tpu_custom_call" | custom-call | flops 1711276032 | bytes 3866624 | tf_op jit(solution)/shard_map/pallas_call | solution.py:81
  27.5 4.3 %all-to-all-start = ((bf16[4,64,1664]{2,1,0:T(8,128)(2,1)}), bf16[4,64,1664]{2,1,0:T(8,128)(2,1)}, u32[]{:S(2)}, u32[]{:S(2)}) async-start(bf16[4,64,1664]{2,1,0:T(8,128)(2,1)} %bitcast.57), calls=%async_computation | async-start | bytes 1703936 | tf_op jit(solution)/shard_map/all_to_all | solution.py:211
  32.3 5.4 %all_gather.7 = bf16[128,128]{1,0:T(8,128)(2,1)S(1)} all-gather(bf16[64,128]{1,0:T(8,128)(2,1)S(1)} %maximum_maximum_fusion), channel_id=1, replica_groups=mesh['ctx'=4,'z'=8,'x'=4,'core'=2] {'core'}, dimensions={0}, use_global_device_ids=true | all-gather | bytes 49152 | tf_op jit(solution)/shard_map/all_gather | solution.py:192
  39.2 1.3 reshape.70.gain_ref
  40.5 1.6 constant_dynamic-slice_fusion.1
  42.2 4.9 %shard_map.110 = (bf16[64,1536]{1,0:T(8,128)(2,1)}, bf16[64,1536]{1,0:T(8,128)(2,1)}) custom-call(bf16[4,64,1664]{2,1,0:T(8,128)(2,1)} %all-to-all-done.got_ref, bf16[64,1536]{1,0:T(8,128)(2,1)} %bitcast.59, bf16[1536,1536]{1,0:T(8,128)(2,1)} %w_ref.1, f32[1,1536]{1,0:T(1,128)} %reshape.70.gain_ref), custom_call_target="tpu_custom_call" | custom-call | flops 301989888 | bytes 6160384 | tf_op jit(solution)/shard_map/pallas_call | solution.py:147
  47.1 3.7 %collective-permute-start = (bf16[64,1536]{1,0:T(8,128)(2,1)}, bf16[64,1536]{1,0:T(8,128)(2,1)S(1)}, u32[]{:S(2)}, u32[]{:S(2)}) collective-permute-start(bf16[64,1536]{1,0:T(8,128)(2,1)} %get-tuple-element.8), channel_id=1, source_target_pairs={{0,1},{1,0},{2,3},{3,2},{4,5},{5,4},{6,7},{7,6},{8,9},{9,8},{10,11... | collective-permute-start | bytes 589832 | tf_op jit(solution)/shard_map/ppermute | solution.py:217
  50.8 1.6 fusion.13
  52.5 1.6 add_convert_fusion
  54.0 1.8 %copy.43 = bf16[32,9,2,1536]{3,2,1,0:T(2,128)(2,1)S(1)} copy(bf16[32,9,2,1536]{3,0,2,1:T(8,128)(2,1)S(1)} %add_convert_fusion) | data formatting | bytes 3538944 | tf_op jit(solution)/shard_map/convert_element_type | solution.py:232
  55.8 54.6 %all_to_all.15 = bf16[32,9,2,1536]{3,2,1,0:T(2,128)(2,1)S(1)} all-to-all(bf16[32,9,2,1536]{3,2,1,0:T(2,128)(2,1)S(1)} %copy.43), channel_id=1, replica_groups=mesh['ctx'=4,'z'=8,'x'=4,'core'=2] {'z','x'}, dimensions={0} | all-to-all | bytes 3538944 | tf_op jit(solution)/shard_map/all_to_all | solution.py:233
  110.5 2.0 %fusion = f32[32,9,2,1024]{3,0,2,1:T(8,128)S(1)} fusion(bf16[1,1536,1024]{2,1,0:T(8,128)(2,1)S(1)} %copy-done, bf16[32,9,2,1536]{3,2,1,0:T(2,128)(2,1)S(1)} %all_to_all.15), kind=kOutput, calls=%fused_computation.1 | convolution fusion | flops 1811939328 | bytes 7274496 | tf_op jit(solution)/shard_map/jscd,df->jscf/dot_general | solution.py:235
  112.5 1.1 convolution_convert_fusion
  113.6 3.0 %copy.45 = bf16[32,9,2,1536]{3,2,1,0:T(2,128)(2,1)} copy(bf16[32,9,2,1536]{3,0,2,1:T(8,128)(2,1)S(1)} %convolution_convert_fusion) | data formatting | bytes 3538944 | tf_op jit(solution)/shard_map/convert_element_type | solution.py:241
  116.6 5.0 %all-to-all-start.2 = ((bf16[32,9,2,1536]{3,2,1,0:T(2,128)(2,1)}), bf16[32,9,2,1536]{3,2,1,0:T(2,128)(2,1)}, u32[]{:S(2)}, u32[]{:S(2)}) async-start(bf16[32,9,2,1536]{3,2,1,0:T(2,128)(2,1)} %copy.45), calls=%async_computation.2 | async-start | bytes 3538944 | tf_op jit(solution)/shard_map/all_to_all | solution.py:242
  121.7 0.9 fusion.9
  122.6 1.1 reshape.71
  123.7 1.4 constant_dynamic-slice_fusion
  125.1 37.4 %all-to-all-done.2 = bf16[32,9,2,1536]{3,2,1,0:T(2,128)(2,1)} async-done(((bf16[32,9,2,1536]{3,2,1,0:T(2,128)(2,1)}), bf16[32,9,2,1536]{3,2,1,0:T(2,128)(2,1)}, u32[]{:S(2)}, u32[]{:S(2)}) %all-to-all-start.2) | async-done | bytes 1769504 | tf_op jit(solution)/shard_map/all_to_all | solution.py:242
  162.5 2.1 %convolution_bitcast_fusion = f32[64,1536]{1,0:T(8,128)S(1)} fusion(bf16[32,9,2,1536]{3,2,1,0:T(2,128)(2,1)} %all-to-all-done.2, bf16[1,64,32,9,2]{1,0,4,3,2:T(2,128)(2,1)} %get-tuple-element.9), kind=kOutput, calls=%fused_computation.4 | convolution fusion | flops 113246208 | bytes 2236416 | tf_op jit(solution)/shard_map/tjsc,jscd->td/dot_general | solution.py:249
  164.6 3.4 %collective-permute-start.1 = (f32[64,1536]{1,0:T(8,128)S(1)}, f32[64,1536]{1,0:T(8,128)S(1)}, u32[]{:S(2)}, u32[]{:S(2)}) collective-permute-start(f32[64,1536]{1,0:T(8,128)S(1)} %convolution_bitcast_fusion), channel_id=1, source_target_pairs={{0,1},{1,0},{2,3},{3,2},{4,5},{5,4},{6,7},{7,6},{8,9},{9,8},{10,11... | collective-permute-start | bytes 1179656 | tf_op jit(solution)/shard_map/ppermute | solution.py:252
  168.1 2.0 %convolution_bitcast_fusion.1 = f32[64,1536]{1,0:T(8,128)S(1)} fusion(bf16[32,9,2,1536]{3,2,1,0:T(2,128)(2,1)} %all-to-all-done.2, bf16[1,64,32,9,2]{1,0,4,3,2:T(2,128)(2,1)S(1)} %copy-done.1), kind=kOutput, calls=%fused_computation.5 | convolution fusion | flops 113246208 | bytes 2236416 | tf_op jit(solution)/shard_map/tjsc,jscd->td/dot_general | solution.py:253
  170.0 0.7 fusion.17
  (34 shorter events, 2.6 us)
Async XLA Ops:
  0.0 110.5 %copy-start = (bf16[1,1536,1024]{2,1,0:T(8,128)(2,1)S(1)}, bf16[1,1536,1024]{2,1,0:T(8,128)(2,1)}, u32[]{:S(2)}) copy-start(bf16[1,1536,1024]{2,1,0:T(8,128)(2,1)} %param.20) | copy-start | bytes 9437188
  27.5 4.4 %copy-start.3 = (s32[1,64,6]{1,0,2:T(1,128)S(1)}, s32[1,64,6]{1,0,2:T(1,128)}, u32[]{:S(2)}) copy-start(s32[1,64,6]{1,0,2:T(1,128)} %param.18) | copy-start | bytes 4612
  27.5 4.5 %copy-start.4 = (bf16[1,64,6]{1,2,0:T(8,128)(2,1)S(1)}, bf16[1,64,6]{1,2,0:T(8,128)(2,1)}, u32[]{:S(2)}) copy-start(bf16[1,64,6]{1,2,0:T(8,128)(2,1)} %param.19) | copy-start | bytes 2308
  27.5 14.6 %all-to-all-start = ((bf16[4,64,1664]{2,1,0:T(8,128)(2,1)}), bf16[4,64,1664]{2,1,0:T(8,128)(2,1)}, u32[]{:S(2)}, u32[]{:S(2)}) async-start(bf16[4,64,1664]{2,1,0:T(8,128)(2,1)} %bitcast.57), calls=%async_computation | async-start | bytes 1703936 | tf_op jit(solution)/shard_map/all_to_all | solution.py:211
  47.1 5.4 %collective-permute-start = (bf16[64,1536]{1,0:T(8,128)(2,1)}, bf16[64,1536]{1,0:T(8,128)(2,1)S(1)}, u32[]{:S(2)}, u32[]{:S(2)}) collective-permute-start(bf16[64,1536]{1,0:T(8,128)(2,1)} %get-tuple-element.8), channel_id=1, source_target_pairs={{0,1},{1,0},{2,3},{3,2},{4,5},{5,4},{6,7},{7,6},{8,9},{9,8},{10,11... | collective-permute-start | bytes 589832 | tf_op jit(solution)/shard_map/ppermute | solution.py:217
  110.5 2.0 %copy-start.5 = (bf16[1,512,1536]{2,1,0:T(8,128)(2,1)S(1)}, bf16[1,512,1536]{2,1,0:T(8,128)(2,1)}, u32[]{:S(2)}) copy-start(bf16[1,512,1536]{2,1,0:T(8,128)(2,1)} %param.21) | copy-start | bytes 4718596
  116.6 45.9 %all-to-all-start.2 = ((bf16[32,9,2,1536]{3,2,1,0:T(2,128)(2,1)}), bf16[32,9,2,1536]{3,2,1,0:T(2,128)(2,1)}, u32[]{:S(2)}, u32[]{:S(2)}) async-start(bf16[32,9,2,1536]{3,2,1,0:T(2,128)(2,1)} %copy.45), calls=%async_computation.2 | async-start | bytes 3538944 | tf_op jit(solution)/shard_map/all_to_all | solution.py:242
  125.1 43.0 %copy-start.1 = (bf16[1,64,32,9,2]{1,0,4,3,2:T(2,128)(2,1)S(1)}, bf16[1,64,32,9,2]{1,0,4,3,2:T(2,128)(2,1)}, u32[]{:S(2)}) copy-start(bf16[1,64,32,9,2]{1,0,4,3,2:T(2,128)(2,1)} %get-tuple-element.10) | copy-start | bytes 221188
  162.5 7.5 %copy-start.2 = (bf16[64,1536]{1,0:T(8,128)(2,1)S(1)}, bf16[64,1536]{1,0:T(8,128)(2,1)}, u32[]{:S(2)}) copy-start(bf16[64,1536]{1,0:T(8,128)(2,1)} %get-tuple-element.7) | copy-start | bytes 589828
  164.6 5.4 %collective-permute-start.1 = (f32[64,1536]{1,0:T(8,128)S(1)}, f32[64,1536]{1,0:T(8,128)S(1)}, u32[]{:S(2)}, u32[]{:S(2)}) collective-permute-start(f32[64,1536]{1,0:T(8,128)S(1)} %convolution_bitcast_fusion), channel_id=1, source_target_pairs={{0,1},{1,0},{2,3},{3,2},{4,5},{5,4},{6,7},{7,6},{8,9},{9,8},{10,11... | collective-permute-start | bytes 1179656 | tf_op jit(solution)/shard_map/ppermute | solution.py:252

commit v13 on v11

--- a/solution.py
+++ b/solution.py
@@ -97,7 +97,9 @@
     )(scal, all_queries, cache_rows, cache_rows, new_rows, new_rows)
 
 
-def combine_kernel(got_ref, res_ref, w_ref, gain_ref, mixed_ref, normed_ref):
+def combine_kernel(got_ref, res_ref, w_hbm, gain_ref, mixed_ref, normed_ref, w_ref, w_sem):
+    w_copy = pltpu.make_async_copy(w_hbm, w_ref, w_sem)
+    w_copy.start()
     heads = KVH * GROUP
     n_src = got_ref.shape[0]
     base = heads * HD
@@ -123,6 +125,7 @@
             )
         cols.append(col.astype(jnp.bfloat16))
     attended = jnp.concatenate(cols, 1)
+    w_copy.wait()
     mixed = (
         res_ref[...].astype(jnp.float32)
         + jnp.dot(attended, w_ref[...], preferred_element_type=jnp.float32)
@@ -144,9 +147,16 @@
         transcendentals=0,
         bytes_accessed=2 * (got.size + out_proj.size + 3 * residual.size),
     )
+    vmem = pl.BlockSpec(memory_space=pltpu.VMEM)
     return pl.pallas_call(
         combine_kernel,
         out_shape=(out, out),
+        in_specs=[vmem, vmem, pl.BlockSpec(memory_space=pl.ANY), vmem],
+        out_specs=(vmem, vmem),
+        scratch_shapes=[
+            pltpu.VMEM(out_proj.shape, out_proj.dtype),
+            pltpu.SemaphoreType.DMA(()),
+        ],
         cost_estimate=cost,
     )(got, residual, out_proj, norm_gain.reshape(1, -1))
 

time: 170 us -> 171 us (level)
  no operation moved by 1% of the time
where the time goes in v13:
time: 171 us; the launch traced here: 170 us
  blocking collectives  80.4 us (47%)
  waiting for transfers between devices  37.7 us (22%)
  Pallas kernels  17.4 us (10%)
  starting transfers between devices  14.1 us (8%)
  local copies, waits for them, and re-layouts  8.81 us (5%)
  matrix products  7.75 us (5%)
  other arithmetic  3.15 us (2%)
    all_to_all x1, blocking collectives, local(): lax.all_to_all(outgoing, CHIP_AXES, split_axis=0, concat_axis=0, tiled=True)  53.9 us
    all_to_all x1, waiting for transfers between devices, local(): lax.all_to_all(result, CHIP_AXES, split_axis=0, concat_axis=0, tiled=True)  36.5 us
    all_gather x1, blocking collectives, local(): all_queries = lax.all_gather(queries[0], 'ctx', axis=0, tiled=True)  14.2 us
    pallas_call x1, Pallas kernels, partial_attention(): pl.pallas_call(attend_kernel, out_shape=jax.ShapeDtypeStruct((n_q, width)...  12 us
    all_gather x1, blocking collectives, local(): normed_both = lax.all_gather(normed, 'core', axis=0, tiled=True)  6.96 us
    all_to_all x1, starting transfers between devices, local(): lax.all_to_all(result, CHIP_AXES, split_axis=0, concat_axis=0, tiled=True)  5.43 us
    pallas_call x1, Pallas kernels, combine_and_norm(): pl.pallas_call(combine_kernel, out_shape=(out, out), in_specs=[vmem, vmem...  5.34 us
    all_gather x1, blocking collectives, local(): both = lax.all_gather(packed, 'core', axis=0, tiled=True)  5.34 us
  transfers between devices with their start and end apart: 3, of which 2 were waited for; matrix products, arithmetic and copies ran while one was open for 5% of the time, Pallas kernels for 0%

profile of v13, /device:TPU:1, one launch (start us, length us, event | category | flops | bytes accessed | tf_op | source)
XLA Modules:
  0.0 170.3 jit_solution(15441168169903922247)
XLA Ops:
  0.8 14.2 %all-gather = bf16[1,256,1536]{2,1,0:T(8,128)(2,1)} all-gather(bf16[1,64,1536]{2,1,0:T(8,128)(2,1)} %param.12), channel_id=2, replica_groups=mesh['ctx'=4,'z'=8,'x'=4,'core'=2] {'ctx'}, dimensions={1}, use_global_device_ids=true | all-gather | bytes 983040 | tf_op jit(solution)/shard_map/all_gather | solution.py:218
  15.0 0.6 pad_add_fusion.scal_ref
  15.6 12.0 %shard_map.109 = bf16[256,1664]{1,0:T(8,128)(2,1)} custom-call(s32[2]{0:T(128)} %pad_add_fusion.scal_ref, bf16[256,1536]{1,0:T(8,128)(2,1)} %bitcast.47, bf16[1024,1024]{1,0:T(8,128)(2,1)} %bitcast.50, bf16[1024,1024]{1,0:T(8,128)(2,1)} %bitcast.51, bf16[64,1024]{1,0:T(8,128)(2,1)} %bitcast.52, bf16[64,1024]{1,0:T(8,128)(2,1)} %bitcast.53), custom_call_target="tpu_custom_call" | custom-call | flops 1711276032 | bytes 3866624 | tf_op jit(solution)/shard_map/pallas_call | solution.py:81
  27.6 4.3 %all-to-all-start = ((bf16[4,64,1664]{2,1,0:T(8,128)(2,1)}), bf16[4,64,1664]{2,1,0:T(8,128)(2,1)}, u32[]{:S(2)}, u32[]{:S(2)}) async-start(bf16[4,64,1664]{2,1,0:T(8,128)(2,1)} %bitcast.46), calls=%async_computation | async-start | bytes 1703936 | tf_op jit(solution)/shard_map/all_to_all | solution.py:221
  32.4 5.3 %all_gather.10 = bf16[128,128]{1,0:T(8,128)(2,1)S(1)} all-gather(bf16[64,128]{1,0:T(8,128)(2,1)S(1)} %maximum_maximum_fusion), channel_id=1, replica_groups=mesh['ctx'=4,'z'=8,'x'=4,'core'=2] {'core'}, dimensions={0}, use_global_device_ids=true | all-gather | bytes 49152 | tf_op jit(solution)/shard_map/all_gather | solution.py:202
  37.8 0.6 reshape.70.gain_ref
  39.8 1.2 all-to-all-done.got_ref
  40.9 5.3 %shard_map.110 = (bf16[64,1536]{1,0:T(8,128)(2,1)}, bf16[64,1536]{1,0:T(8,128)(2,1)}) custom-call(bf16[4,64,1664]{2,1,0:T(8,128)(2,1)} %all-to-all-done.got_ref, bf16[64,1536]{1,0:T(8,128)(2,1)} %bitcast.48, bf16[1536,1536]{1,0:T(8,128)(2,1)} %w_hbm.1, f32[1,1536]{1,0:T(1,128)} %reshape.70.gain_ref), custom_call_target="tpu_custom_call" | custom-call | flops 301989888 | bytes 6160384 | tf_op jit(solution)/shard_map/pallas_call | solution.py:151
  46.3 7.0 %all_gather.11 = bf16[128,1536]{1,0:T(8,128)(2,1)S(1)} all-gather(bf16[64,1536]{1,0:T(8,128)(2,1)} %get-tuple-element.8), channel_id=1, replica_groups=mesh['ctx'=4,'z'=8,'x'=4,'core'=2] {'core'}, dimensions={0}, use_global_device_ids=true | all-gather | bytes 589824 | tf_op jit(solution)/shard_map/all_gather | solution.py:227
  53.3 0.6 convolution_convert_fusion
  53.9 1.8 %copy.39 = bf16[32,9,2,1536]{3,2,1,0:T(2,128)(2,1)S(1)} copy(bf16[32,9,2,1536]{3,0,2,1:T(8,128)(2,1)S(1)} %convolution_convert_fusion) | data formatting | bytes 3538944 | tf_op jit(solution)/shard_map/convert_element_type | solution.py:235
  55.7 53.9 %all_to_all.15 = bf16[32,9,2,1536]{3,2,1,0:T(2,128)(2,1)S(1)} all-to-all(bf16[32,9,2,1536]{3,2,1,0:T(2,128)(2,1)S(1)} %copy.39), channel_id=1, replica_groups=mesh['ctx'=4,'z'=8,'x'=4,'core'=2] {'z','x'}, dimensions={0} | all-to-all | bytes 3538944 | tf_op jit(solution)/shard_map/all_to_all | solution.py:236
  109.6 2.0 %fusion = f32[32,9,2,1024]{3,0,2,1:T(8,128)S(1)} fusion(bf16[1,1536,1024]{2,1,0:T(8,128)(2,1)S(1)} %copy-done, bf16[32,9,2,1536]{3,2,1,0:T(2,128)(2,1)S(1)} %all_to_all.15), kind=kOutput, calls=%fused_computation | convolution fusion | flops 1811939328 | bytes 7274496 | tf_op jit(solution)/shard_map/jscd,df->jscf/dot_general | solution.py:238
  111.6 1.1 convolution_convert_fusion.1
  112.7 3.0 %copy.41 = bf16[32,9,2,1536]{3,2,1,0:T(2,128)(2,1)} copy(bf16[32,9,2,1536]{3,0,2,1:T(8,128)(2,1)S(1)} %convolution_convert_fusion.1) | data formatting | bytes 3538944 | tf_op jit(solution)/shard_map/convert_element_type | solution.py:244
  115.7 5.4 %all-to-all-start.2 = ((bf16[32,9,2,1536]{3,2,1,0:T(2,128)(2,1)}), bf16[32,9,2,1536]{3,2,1,0:T(2,128)(2,1)}, u32[]{:S(2)}, u32[]{:S(2)}) async-start(bf16[32,9,2,1536]{3,2,1,0:T(2,128)(2,1)} %copy.41), calls=%async_computation.2 | async-start | bytes 3538944 | tf_op jit(solution)/shard_map/all_to_all | solution.py:245
  121.2 0.9 fusion.9
  122.1 1.1 reshape.71
  123.2 1.4 constant_dynamic-slice_fusion
  124.6 36.5 %all-to-all-done.2 = bf16[32,9,2,1536]{3,2,1,0:T(2,128)(2,1)} async-done(((bf16[32,9,2,1536]{3,2,1,0:T(2,128)(2,1)}), bf16[32,9,2,1536]{3,2,1,0:T(2,128)(2,1)}, u32[]{:S(2)}, u32[]{:S(2)}) %all-to-all-start.2) | async-done | bytes 1769504 | tf_op jit(solution)/shard_map/all_to_all | solution.py:245
  161.1 2.1 %convolution_bitcast_fusion = f32[64,1536]{1,0:T(8,128)S(1)} fusion(bf16[32,9,2,1536]{3,2,1,0:T(2,128)(2,1)} %all-to-all-done.2, bf16[1,64,32,9,2]{1,0,4,3,2:T(2,128)(2,1)} %get-tuple-element.9), kind=kOutput, calls=%fused_computation.4 | convolution fusion | flops 113246208 | bytes 2236416 | tf_op jit(solution)/shard_map/tjsc,jscd->td/dot_general | solution.py:252
  163.2 4.3 %collective-permute-start = (f32[64,1536]{1,0:T(8,128)S(1)}, f32[64,1536]{1,0:T(8,128)S(1)}, u32[]{:S(2)}, u32[]{:S(2)}) collective-permute-start(f32[64,1536]{1,0:T(8,128)S(1)} %convolution_bitcast_fusion), channel_id=1, source_target_pairs={{0,1},{1,0},{2,3},{3,2},{4,5},{5,4},{6,7},{7,6},{8,9},{9,8},{10,11... | collective-permute-start | bytes 1179656 | tf_op jit(solution)/shard_map/ppermute | solution.py:255
  167.6 2.0 %convolution_bitcast_fusion.1 = f32[64,1536]{1,0:T(8,128)S(1)} fusion(bf16[32,9,2,1536]{3,2,1,0:T(2,128)(2,1)} %all-to-all-done.2, bf16[1,64,32,9,2]{1,0,4,3,2:T(2,128)(2,1)S(1)} %copy-done.1), kind=kOutput, calls=%fused_computation.5 | convolution fusion | flops 113246208 | bytes 2236416 | tf_op jit(solution)/shard_map/tjsc,jscd->td/dot_general | solution.py:256
  169.5 0.7 fusion.14
  (33 shorter events, 1.9 us)
Async XLA Ops:
  0.0 109.6 %copy-start = (bf16[1,1536,1024]{2,1,0:T(8,128)(2,1)S(1)}, bf16[1,1536,1024]{2,1,0:T(8,128)(2,1)}, u32[]{:S(2)}) copy-start(bf16[1,1536,1024]{2,1,0:T(8,128)(2,1)} %param.20) | copy-start | bytes 9437188
  15.6 16.4 %copy-start.5 = (bf16[1,64,6]{1,2,0:T(8,128)(2,1)S(1)}, bf16[1,64,6]{1,2,0:T(8,128)(2,1)}, u32[]{:S(2)}) copy-start(bf16[1,64,6]{1,2,0:T(8,128)(2,1)} %param.19) | copy-start | bytes 2308
  15.6 16.5 %copy-start.4 = (s32[1,64,6]{1,0,2:T(1,128)S(1)}, s32[1,64,6]{1,0,2:T(1,128)}, u32[]{:S(2)}) copy-start(s32[1,64,6]{1,0,2:T(1,128)} %param.18) | copy-start | bytes 4612
  27.6 10.2 %copy-start.3 = (f32[1536]{0:T(1024)S(1)}, f32[1536]{0:T(1024)}, u32[]{:S(2)}) copy-start(f32[1536]{0:T(1024)} %param.17) | copy-start | bytes 18436
  27.6 13.3 %all-to-all-start = ((bf16[4,64,1664]{2,1,0:T(8,128)(2,1)}), bf16[4,64,1664]{2,1,0:T(8,128)(2,1)}, u32[]{:S(2)}, u32[]{:S(2)}) async-start(bf16[4,64,1664]{2,1,0:T(8,128)(2,1)} %bitcast.46), calls=%async_computation | async-start | bytes 1703936 | tf_op jit(solution)/shard_map/all_to_all | solution.py:221
  109.6 2.0 %copy-start.6 = (bf16[1,512,1536]{2,1,0:T(8,128)(2,1)S(1)}, bf16[1,512,1536]{2,1,0:T(8,128)(2,1)}, u32[]{:S(2)}) copy-start(bf16[1,512,1536]{2,1,0:T(8,128)(2,1)} %param.21) | copy-start | bytes 4718596
  115.7 45.4 %all-to-all-start.2 = ((bf16[32,9,2,1536]{3,2,1,0:T(2,128)(2,1)}), bf16[32,9,2,1536]{3,2,1,0:T(2,128)(2,1)}, u32[]{:S(2)}, u32[]{:S(2)}) async-start(bf16[32,9,2,1536]{3,2,1,0:T(2,128)(2,1)} %copy.41), calls=%async_computation.2 | async-start | bytes 3538944 | tf_op jit(solution)/shard_map/all_to_all | solution.py:245
  124.6 43.0 %copy-start.1 = (bf16[1,64,32,9,2]{1,0,4,3,2:T(2,128)(2,1)S(1)}, bf16[1,64,32,9,2]{1,0,4,3,2:T(2,128)(2,1)}, u32[]{:S(2)}) copy-start(bf16[1,64,32,9,2]{1,0,4,3,2:T(2,128)(2,1)} %get-tuple-element.10) | copy-start | bytes 221188
  161.1 8.4 %copy-start.2 = (bf16[64,1536]{1,0:T(8,128)(2,1)S(1)}, bf16[64,1536]{1,0:T(8,128)(2,1)}, u32[]{:S(2)}) copy-start(bf16[64,1536]{1,0:T(8,128)(2,1)} %get-tuple-element.7) | copy-start | bytes 589828
  163.2 6.3 %collective-permute-start = (f32[64,1536]{1,0:T(8,128)S(1)}, f32[64,1536]{1,0:T(8,128)S(1)}, u32[]{:S(2)}, u32[]{:S(2)}) collective-permute-start(f32[64,1536]{1,0:T(8,128)S(1)} %convolution_bitcast_fusion), channel_id=1, source_target_pairs={{0,1},{1,0},{2,3},{3,2},{4,5},{5,4},{6,7},{7,6},{8,9},{9,8},{10,11... | collective-permute-start | bytes 1179656 | tf_op jit(solution)/shard_map/ppermute | solution.py:255
